TPU v7x, 1024 devices: a whole 4x8x16 slice. The times are simulated.
1024 devices in a mesh: task: 8 (over y), fsdp: 128 (over z, x, core).
Axes of the slice: x: 4, y: 8, z: 16, core: 2. Of those that a mesh axis runs over, the one named last changes fastest.
Arguments:
- contexts: bfloat16 [8, 24576, 4096], P('task', 'fsdp'), may hold values from -3400 to 3400
- cotangents: bfloat16 [8, 24576, 4096], P('task', 'fsdp'), may hold values from -3400 to 3400
- adapter: bfloat16 [4096, 256], P('fsdp'), may hold values from -0.09375 to 0.09375
- moment_one: float32 [4096, 256], P('fsdp', 'task'), may hold values from -6 to 6
- moment_two: float32 [4096, 256], P('fsdp', 'task'), may hold values from 0.01 to 10
Outputs:
- first_moment: float32 [4096, 256], P('fsdp', 'task')
- second_moment: float32 [4096, 256], P('fsdp', 'task')
- adam_step: float32 [4096, 256], P('fsdp', 'task')
All inputs are finite; a program needn't handle non-finite values.
Results may differ from a plain program's by a relative error of at most 0.0004.
The roundings to bfloat16 on the way count: a program that leaves them out, or rounds other values in their place, can miss the bound.
Values may be sent and summed in bfloat16 or wider, within the bound.
No kernel may reach another device: no remote copies, remote signals or barrier semaphores. Data moves between devices by JAX's collectives and lax.ppermute only.
A program may use at most 32 MiB of HBM per device.

v0:
```python
import math

import jax
import jax.numpy as jnp
from jax import lax
from jax.sharding import PartitionSpec as P

D = 4096
RANK = 128


def eliminate(matrix, vector):
    extent = vector.shape[0]
    matrix_rows = [matrix[position] for position in range(extent)]
    values = [vector[position] for position in range(extent)]
    for column in range(extent):
        for target in range(column + 1, extent):
            factor = matrix_rows[target][column] / matrix_rows[column][column]
            matrix_rows[target] = matrix_rows[target] - factor * matrix_rows[column]
            values[target] = values[target] - factor * values[column]
    answer = [values[0] for position in range(extent)]
    for column in reversed(range(extent)):
        running = values[column]
        for follow in range(column + 1, extent):
            running = running - matrix_rows[column][follow] * answer[follow]
        answer[column] = running / matrix_rows[column][column]
    return jnp.stack(answer)


def task_weights(gram_matrix):
    task_norms = jnp.sqrt(jnp.diagonal(gram_matrix))
    right_side = gram_matrix[0, 0] / task_norms[0] - gram_matrix[0, 1:] / task_norms[1:]
    system = (gram_matrix[0, 0] - gram_matrix[1:, 0])[:, None] / task_norms[0] - (
        gram_matrix[0, 1:][None, :] - gram_matrix[1:, 1:]
    ) / task_norms[1:][None, :]
    solution = eliminate(system.T, right_side)
    return jnp.concatenate([jnp.reshape(1.0 - jnp.sum(solution), (1,)), solution])


def body(contexts, cotangents, adapter, moment_one, moment_two):
    own_context = contexts[0]
    own_cotangent = cotangents[0]
    rank_width = adapter.shape[1] // 2
    piece = lax.all_gather(adapter, "fsdp", axis=0, tiled=True)
    context_cols = own_context
    cotangent_cols = own_cotangent
    low_part = jnp.dot(context_cols, piece[:, :rank_width], preferred_element_type=jnp.float32)
    back_part = jnp.dot(cotangent_cols, piece[:, rank_width:], preferred_element_type=jnp.float32)
    low = low_part.astype(jnp.bfloat16)
    back = back_part.astype(jnp.bfloat16)
    context_cols = own_context
    cotangent_cols = own_cotangent
    down_part = lax.dot_general(
        context_cols, back, (((0,), (0,)), ((), ())), preferred_element_type=jnp.float32
    )
    up_part = lax.dot_general(
        cotangent_cols, low, (((0,), (0,)), ((), ())), preferred_element_type=jnp.float32
    )
    grad_rows = lax.psum_scatter(
        jnp.concatenate([down_part, up_part], axis=1), "fsdp", scatter_dimension=0, tiled=True
    )
    gathered = lax.all_gather(grad_rows[None], "task", axis=0, tiled=True)
    partial_gram = jnp.einsum("sij,tij->st", gathered, gathered, precision=lax.Precision.HIGHEST)
    gram_matrix = lax.psum(partial_gram, "fsdp")
    block_width = gathered.shape[2] // lax.axis_size("task")
    pieces = lax.dynamic_slice_in_dim(
        gathered, lax.axis_index("task") * block_width, block_width, 2
    )
    task_alpha = task_weights(gram_matrix)
    combined = jnp.einsum("t,tij->ij", task_alpha, pieces, precision=lax.Precision.HIGHEST)
    squared = lax.psum(jnp.sum(combined * combined), ("task", "fsdp"))
    grad_norm = jnp.sqrt(1e-06 + squared)
    clipped = combined * (math.sqrt(2 * RANK * D) / grad_norm)
    first_moment = 0.9 * moment_one + 0.1 * clipped
    second_moment = 0.95 * moment_two + 0.05 * clipped * clipped
    adam_step = (
        first_moment / (1.0 - 0.9**20) / (jnp.sqrt(second_moment / (1.0 - 0.95**20)) + 1e-08)
    )
    return (first_moment, second_moment, adam_step)


def solution(mesh):
    in_specs = (
        P("task", "fsdp", None),
        P("task", "fsdp", None),
        P("fsdp", None),
        P("fsdp", "task"),
        P("fsdp", "task"),
    )
    out_specs = (P("fsdp", "task"), P("fsdp", "task"), P("fsdp", "task"))
    return jax.shard_map(body, mesh=mesh, in_specs=in_specs, out_specs=out_specs, check_vma=False)
```

profile of v0, /device:TPU:6, one launch (start us, length us, event | category | flops | bytes accessed | tf_op | source)
XLA Modules:
  0.0 927.9 jit_solution(4628626883556321073)
XLA Ops:
  7.2 0.7 all-gather.3.cloned.1.call-update
  8.0 158.8 %all-gather.3.cloned.1.call-done = bf16[4096,256]{1,0:T(8,128)(2,1)} async-done(((bf16[32,256]{1,0:T(8,128)(2,1)}), bf16[4096,256]{1,0:T(8,128)(2,1)}) %all-gather.3.cloned.1.call-update) | async-done | bytes 2097168 | tf_op jit(solution)/shard_map/all_gather | solution.py:44
  166.7 4.0 convolution_bitcast_fusion
  170.8 3.6 convolution_bitcast_fusion.1
  174.4 4.6 pad_maximum_fusion
  179.0 5.6 copy.18
  184.7 272.6 %reduce-scatter.4.cloned.1.call-done = f32[32,256]{1,0:T(8,128)} async-done(((f32[4096,256]{1,0:T(8,128)}), f32[32,256]{1,0:T(8,128)}) %reduce-scatter.4.cloned.1.call-update) | async-done | bytes 32784 | tf_op jit(solution)/shard_map/reduce_scatter | solution.py:59
  457.3 26.0 %all-gather = f32[256,256]{1,0:T(8,128)S(1)} all-gather(f32[32,256]{1,0:T(8,128)} %reduce-scatter.4.cloned.1.call-done), channel_id=2, replica_groups=mesh['task'=8,'fsdp'=128] {'task'}, dimensions={0}, use_global_device_ids=true | all-gather | bytes 294912 | tf_op jit(solution)/shard_map/all_gather | solution.py:62
  483.3 0.7 convolution_bitcast_fusion.2
  484.1 232.7 %psum.14 = f32[8,8]{1,0:T(8,128)S(1)} all-reduce(f32[8,8]{1,0:T(8,128)S(1)} %convolution_bitcast_fusion.2), channel_id=1, replica_groups=mesh['task'=8,'fsdp'=128] {'fsdp'}, use_global_device_ids=true, to_apply=%region_1.0 | all-reduce | flops 64 | bytes 512 | tf_op jit(solution)/shard_map/psum | solution.py:64
  717.3 0.6 gather_fusion
  718.6 0.8 divide_reduce_fusion
  719.7 0.7 fusion.26
  728.2 0.7 fusion.32
  732.1 0.6 fusion.27
  732.7 0.6 slice.309
  742.6 0.6 fusion.28
  743.2 0.6 slice.317
  743.8 0.5 slice.325
  747.0 0.5 slice.334
  748.8 0.5 slice.310
  751.3 0.6 fusion.29
  751.9 0.5 slice.358
  752.4 0.6 slice.359
  755.6 0.6 slice.356
  758.2 0.6 fusion.30
  758.8 0.6 slice.365
  764.4 0.6 slice.370
  766.4 0.6 slice.372
  787.3 0.6 multiply_reduce_fusion
  787.9 131.9 %psum.15 = f32[]{:T(128)} all-reduce(f32[]{:T(128)} %multiply_reduce_fusion), channel_id=1, replica_groups=mesh['task'=8,'fsdp'=128] {'task','fsdp'}, use_global_device_ids=true, to_apply=%region_3.4 | all-reduce | flops 1 | bytes 8 | tf_op jit(solution)/shard_map/psum | solution.py:71
  920.5 0.6 add_divide_fusion
  (32 shorter events, 4.6 us)
Async XLA Ops:
  7.2 159.6 %copy-start = (bf16[1,192,4096]{2,1,0:T(8,128)(2,1)S(1)}, bf16[1,192,4096]{2,1,0:T(8,128)(2,1)}, u32[]{:S(2)}) copy-start(bf16[1,192,4096]{2,1,0:T(8,128)(2,1)} %param.6) | copy-start | bytes 4718596
  7.2 159.6 %all-gather.3.cloned.1.call-start = ((), (), s32[]{:S(2)}) async-start(), calls=%async_computation.1 | async-start | bytes 2113536 | tf_op jit(solution)/shard_map/all_gather | solution.py:44
  7.9 162.9 %copy-start.1 = (bf16[1,192,4096]{2,1,0:T(8,128)(2,1)S(1)}, bf16[1,192,4096]{2,1,0:T(8,128)(2,1)}, u32[]{:S(2)}) copy-start(bf16[1,192,4096]{2,1,0:T(8,128)(2,1)} %param.5) | copy-start | bytes 4718596
  7.9 449.4 %reduce-scatter.4.cloned.1.call-start = ((), (), s32[]{:S(2)}) async-start(), calls=%async_computation.2 | async-start | bytes 4227072 | tf_op jit(solution)/shard_map/reduce_scatter | solution.py:59
  184.7 735.8 %copy-start.2 = (f32[32,32]{1,0:T(8,128)S(1)}, f32[32,32]{1,0:T(8,128)}, u32[]{:S(2)}) copy-start(f32[32,32]{1,0:T(8,128)} %param.9) | copy-start | bytes 12292
  184.7 735.8 %copy-start.3 = (f32[32,32]{1,0:T(8,128)S(1)}, f32[32,32]{1,0:T(8,128)}, u32[]{:S(2)}) copy-start(f32[32,32]{1,0:T(8,128)} %param.8) | copy-start | bytes 12292
Sparse Core Ops, SparseCore 0:
  12.3 154.3 all-gather.2
  184.8 272.4 reduce-scatter.3
where the time goes:
time: 931 us; the launch traced here: 928 us
  waiting for transfers between devices  432 us (46%)
  blocking collectives  391 us (42%)
  between operations  69.4 us (7%)
  local copies, waits for them, and re-layouts  20.2 us (2%)
    reduce_scatter x1, waiting for transfers between devices, body(): lax.psum_scatter(jnp.concatenate([down_part, up_part], axis=1), 'fsdp', s...  273 us
    psum x1, blocking collectives, body(): gram_matrix = lax.psum(partial_gram, 'fsdp')  233 us
    all_gather x1, waiting for transfers between devices, body(): piece = lax.all_gather(adapter, 'fsdp', axis=0, tiled=True)  159 us
    psum x1, blocking collectives, body(): squared = lax.psum(jnp.sum(combined * combined), ('task', 'fsdp'))  132 us
    all_gather x1, blocking collectives, body(): gathered = lax.all_gather(grad_rows[None], 'task', axis=0, tiled=True)  26 us
  transfers between devices with their start and end apart: 2, of which 2 were waited for; matrix products, arithmetic and copies ran while one was open for 0% of the time, Pallas kernels for 0%

commit v1 on v0

v1 whole, which is shorter than its diff:
```python
import math

import jax
import jax.numpy as jnp
from jax import lax
from jax.sharding import Mesh
from jax.sharding import PartitionSpec as P

D = 4096
RANK = 128
FSDP = ("z", "x", "core")
ALL_AXES = ("core", "x", "z", "task")


def eliminate(matrix, vector):
    extent = vector.shape[0]
    matrix_rows = [matrix[position] for position in range(extent)]
    values = [vector[position] for position in range(extent)]
    for column in range(extent):
        for target in range(column + 1, extent):
            factor = matrix_rows[target][column] / matrix_rows[column][column]
            matrix_rows[target] = matrix_rows[target] - factor * matrix_rows[column]
            values[target] = values[target] - factor * values[column]
    answer = [values[0] for position in range(extent)]
    for column in reversed(range(extent)):
        running = values[column]
        for follow in range(column + 1, extent):
            running = running - matrix_rows[column][follow] * answer[follow]
        answer[column] = running / matrix_rows[column][column]
    return jnp.stack(answer)


def task_weights(gram_matrix):
    task_norms = jnp.sqrt(jnp.diagonal(gram_matrix))
    right_side = gram_matrix[0, 0] / task_norms[0] - gram_matrix[0, 1:] / task_norms[1:]
    system = (gram_matrix[0, 0] - gram_matrix[1:, 0])[:, None] / task_norms[0] - (
        gram_matrix[0, 1:][None, :] - gram_matrix[1:, 1:]
    ) / task_norms[1:][None, :]
    solution = eliminate(system.T, right_side)
    return jnp.concatenate([jnp.reshape(1.0 - jnp.sum(solution), (1,)), solution])


def butterfly_sum(value, axis):
    size = lax.axis_size(axis)
    step = 1
    while step < size:
        pairs = [(i, i ^ step) for i in range(size)]
        value = value + lax.ppermute(value, axis, pairs)
        step *= 2
    return value


def body(contexts, cotangents, adapter, moment_one, moment_two):
    own_context = contexts[0]
    own_cotangent = cotangents[0]
    rank_width = adapter.shape[1] // 2
    piece = adapter
    for axis in ("core", "x", "z"):
        piece = lax.all_gather(piece, axis, axis=0, tiled=True)
    low = jnp.dot(own_context, piece[:, :rank_width], preferred_element_type=jnp.float32).astype(jnp.bfloat16)
    back = jnp.dot(own_cotangent, piece[:, rank_width:], preferred_element_type=jnp.float32).astype(jnp.bfloat16)
    down_part = lax.dot_general(
        own_context, back, (((0,), (0,)), ((), ())), preferred_element_type=jnp.float32
    )
    up_part = lax.dot_general(
        own_cotangent, low, (((0,), (0,)), ((), ())), preferred_element_type=jnp.float32
    )
    grad_rows = jnp.concatenate([down_part, up_part], axis=1)
    for axis in ("z", "x", "core"):
        grad_rows = lax.psum_scatter(grad_rows, axis, scatter_dimension=0, tiled=True)
    tasks = lax.axis_size("task")
    rows, width = grad_rows.shape
    blocks = grad_rows.reshape(rows, tasks, width // tasks).transpose(1, 0, 2)
    pieces = lax.all_to_all(blocks, "task", 0, 0, tiled=True)
    partial_gram = jnp.einsum("sij,tij->st", pieces, pieces, precision=lax.Precision.HIGHEST)
    gram_matrix = partial_gram
    for axis in ALL_AXES:
        gram_matrix = butterfly_sum(gram_matrix, axis)
    task_alpha = task_weights(gram_matrix)
    combined = jnp.einsum("t,tij->ij", task_alpha, pieces, precision=lax.Precision.HIGHEST)
    squared = jnp.dot(
        task_alpha, jnp.dot(gram_matrix, task_alpha, precision=lax.Precision.HIGHEST),
        precision=lax.Precision.HIGHEST,
    )
    grad_norm = jnp.sqrt(1e-06 + squared)
    clipped = combined * (math.sqrt(2 * RANK * D) / grad_norm)
    first_moment = 0.9 * moment_one + 0.1 * clipped
    second_moment = 0.95 * moment_two + 0.05 * clipped * clipped
    adam_step = (
        first_moment / (1.0 - 0.9**20) / (jnp.sqrt(second_moment / (1.0 - 0.95**20)) + 1e-08)
    )
    return (first_moment, second_moment, adam_step)


def solution(mesh):
    tasks, fsdp = mesh.devices.shape
    split = Mesh(mesh.devices.reshape(tasks, fsdp // 8, 4, 2), ("task",) + FSDP)
    in_specs = (
        P("task", FSDP, None),
        P("task", FSDP, None),
        P(FSDP, None),
        P(FSDP, "task"),
        P(FSDP, "task"),
    )
    out_specs = (P(FSDP, "task"), P(FSDP, "task"), P(FSDP, "task"))
    return jax.shard_map(body, mesh=split, in_specs=in_specs, out_specs=out_specs, check_vma=False)
```

time: 931 us -> 428 us (0.46)
  blocking collectives: 391 us -> 39.3 us
  waiting for transfers between devices: 432 us -> 238 us
  starting transfers between devices: 0.08 us -> 44.9 us
    psum x2 -> x0, blocking collectives: 365 us -> none  [the longest x1 233 us: body(): gram_matrix = lax.psum(partial_gram, 'fsdp')]
    reduce_scatter x1, waiting for transfers between devices: 273 us -> 81.3 us  [body(): lax.psum_scatter(grad_rows, axis, scatter_dimension=0, tiled=True)]
    all_gather x1, waiting for transfers between devices: 159 us -> 74.4 us  [body(): piece = lax.all_gather(piece, axis, axis=0, tiled=True)]
    unnamed x2 -> x6, waiting for transfers between devices: 0.7 us -> 53.7 us
    ppermute x0 -> x10, starting transfers between devices: none -> 44.8 us  [butterfly_sum(): value = value + lax.ppermute(value, axis, pairs)]
    ppermute x0 -> x10, waiting for transfers between devices: none -> 28.5 us  [butterfly_sum(): value = value + lax.ppermute(value, axis, pairs)]
    all_to_all x0 -> x1, blocking collectives: none -> 14.6 us  [body(): pieces = lax.all_to_all(blocks, 'task', 0, 0, tiled=True)]
    all_gather x1 -> x2, blocking collectives: 26 us -> 24.8 us  [body(): piece = lax.all_gather(piece, axis, axis=0, tiled=True)]
  transfers between devices with their start and end apart: 2 -> 14, of which waited for: 2 -> 14; matrix products, arithmetic and copies ran while one was open for 0% -> 0% of each run, Pallas kernels for 0% -> 0%
where the time goes in v1:
time: 428 us; the launch traced here: 427 us
  waiting for transfers between devices  238 us (56%)
  between operations  69.4 us (16%)
  starting transfers between devices  44.9 us (10%)
  blocking collectives  39.3 us (9%)
  local copies, waits for them, and re-layouts  19.1 us (4%)
  matrix products  9.12 us (2%)
  other arithmetic  6.97 us (2%)
    reduce_scatter x1, waiting for transfers between devices, body(): lax.psum_scatter(grad_rows, axis, scatter_dimension=0, tiled=True)  81.3 us
    all_gather x1, waiting for transfers between devices, body(): piece = lax.all_gather(piece, axis, axis=0, tiled=True)  74.4 us
    unnamed x6, waiting for transfers between devices  53.7 us
    ppermute x10, starting transfers between devices, butterfly_sum(): value = value + lax.ppermute(value, axis, pairs)  44.8 us
    ppermute x10, waiting for transfers between devices, butterfly_sum(): value = value + lax.ppermute(value, axis, pairs)  28.5 us
    all_gather x2, blocking collectives, body(): piece = lax.all_gather(piece, axis, axis=0, tiled=True)  24.8 us
    all_to_all x1, blocking collectives, body(): pieces = lax.all_to_all(blocks, 'task', 0, 0, tiled=True)  14.6 us
    slice x16, local copies, waits for them, and re-layouts, eliminate(): factor = matrix_rows[target][column] / matrix_rows[column][column]  9.69 us
  transfers between devices with their start and end apart: 14, of which 14 were waited for; matrix products, arithmetic and copies ran while one was open for 0% of the time, Pallas kernels for 0%

profile of v1, /device:TPU:6, one launch (start us, length us, event | category | flops | bytes accessed | tf_op | source)
XLA Modules:
  0.0 426.7 jit_solution(18055182590916171361)
XLA Ops:
  7.2 2.2 all_gather.9
  9.4 22.6 %all_gather.10 = bf16[256,256]{1,0:T(8,128)(2,1)} all-gather(bf16[64,256]{1,0:T(8,128)(2,1)S(1)} %all_gather.9), channel_id=1, replica_groups=mesh['task'=8,'z'=16,'x'=4,'core'=2] {'x'}, dimensions={0}, use_global_device_ids=true | all-gather | bytes 163840 | tf_op jit(solution)/shard_map/all_gather | solution.py:59
  32.1 74.4 %all-gather.2.cloned.1.call-done = bf16[4096,256]{1,0:T(8,128)(2,1)} async-done(((bf16[256,256]{1,0:T(8,128)(2,1)}), bf16[4096,256]{1,0:T(8,128)(2,1)}) %all-gather.2.cloned.1.call-update) | async-done | bytes 2097168 | tf_op jit(solution)/shard_map/all_gather | solution.py:59
  106.5 4.1 convolution_bitcast_fusion
  110.6 3.6 convolution_bitcast_fusion.1
  114.2 4.6 %pad_maximum_fusion = f32[4096,256]{0,1:T(8,128)} fusion(f32[4096,128]{0,1:T(8,128)} %convolution_bitcast_fusion, f32[4096,128]{0,1:T(8,128)} %convolution_bitcast_fusion.1), kind=kLoop, calls=%fused_computation.3 | loop fusion | flops 1048576 | bytes 8388608 | tf_op jit(solution)/shard_map/concatenate | solution.py:68
  118.9 81.3 %reduce-scatter.8.cloned.1.call-done = f32[256,256]{0,1:T(8,128)} async-done(((f32[4096,256]{0,1:T(8,128)}), f32[256,256]{0,1:T(8,128)}) %reduce-scatter.8.cloned.1.call-update) | async-done | bytes 262160 | tf_op jit(solution)/shard_map/reduce_scatter | solution.py:70
  200.2 1.8 copy.16
  202.0 29.9 %reduce-scatter.10.cloned.1.call-done = f32[64,256]{1,0:T(8,128)} async-done(((f32[256,256]{1,0:T(8,128)}), f32[64,256]{1,0:T(8,128)}) %reduce-scatter.10.cloned.1.call-update) | async-done | bytes 65552
  231.9 23.7 %reduce-scatter.12.cloned.1.call-done = f32[32,256]{1,0:T(8,128)} async-done(((f32[64,256]{1,0:T(8,128)}), f32[32,256]{1,0:T(8,128)}) %reduce-scatter.12.cloned.1.call-update) | async-done | bytes 32784
  255.6 0.9 copy.19
  256.7 14.6 %all_to_all.5 = f32[8,1,1024]{2,1,0:T(1,128)S(1)} all-to-all(f32[8,1,1024]{2,1,0:T(1,128)S(1)} %reshape.210), channel_id=1, replica_groups=mesh['task'=8,'z'=16,'x'=4,'core'=2] {'task'}, dimensions={0} | all-to-all | bytes 65536 | tf_op jit(solution)/shard_map/all_to_all | solution.py:74
  273.0 2.0 collective-permute-start
  274.9 1.1 collective-permute-done
  276.1 2.8 collective-permute-start.1
  278.9 2.7 collective-permute-done.1
  281.6 3.3 collective-permute-start.2
  284.9 3.6 collective-permute-done.2
  288.6 3.6 collective-permute-start.3
  292.1 1.9 collective-permute-done.3
  294.1 4.6 %collective-permute-start.4 = (f32[8,8]{0,1:T(8,128)S(1)}, f32[8,8]{0,1:T(8,128)S(1)}, u32[]{:S(2)}, u32[]{:S(2)}) collective-permute-start(f32[8,8]{0,1:T(8,128)S(1)} %add.55), channel_id=1, source_target_pairs={{0,16},{8,24},{16,0},{24,8},{32,48},{40,56},{48,32},{56,40},{64,80... | collective-permute-start | bytes 776 | tf_op jit(solution)/shard_map/ppermute | solution.py:48
  298.7 1.8 collective-permute-done.4
  300.5 8.0 %collective-permute-start.5 = (f32[8,8]{0,1:T(8,128)S(1)}, f32[8,8]{0,1:T(8,128)S(1)}, u32[]{:S(2)}, u32[]{:S(2)}) collective-permute-start(f32[8,8]{0,1:T(8,128)S(1)} %add.56), channel_id=1, source_target_pairs={{0,32},{8,40},{16,48},{24,56},{32,0},{40,8},{48,16},{56,24},{64,96... | collective-permute-start | bytes 776 | tf_op jit(solution)/shard_map/ppermute | solution.py:48
  308.5 1.6 collective-permute-done.5
  310.1 13.4 %collective-permute-start.6 = (f32[8,8]{0,1:T(8,128)S(1)}, f32[8,8]{0,1:T(8,128)S(1)}, u32[]{:S(2)}, u32[]{:S(2)}) collective-permute-start(f32[8,8]{0,1:T(8,128)S(1)} %add.57), channel_id=1, source_target_pairs={{0,64},{8,72},{16,80},{24,88},{32,96},{40,104},{48,112},{56,120},{... | collective-permute-start | bytes 776 | tf_op jit(solution)/shard_map/ppermute | solution.py:48
  323.4 1.6 collective-permute-done.6
  325.0 2.5 collective-permute-start.7
  327.5 3.0 collective-permute-done.7
  330.5 2.4 collective-permute-start.8
  332.9 4.1 collective-permute-done.8
  337.0 2.3 collective-permute-start.9
  339.3 7.0 %collective-permute-done.9 = f32[8,8]{0,1:T(8,128)S(1)} collective-permute-done((f32[8,8]{0,1:T(8,128)S(1)}, f32[8,8]{0,1:T(8,128)S(1)}, u32[]{:S(2)}, u32[]{:S(2)}) %collective-permute-start.9) | collective-permute-done | bytes 288 | tf_op jit(solution)/shard_map/ppermute | solution.py:48
  (73 shorter events, 20.5 us)
Async XLA Ops:
  7.2 99.3 %copy-start = (bf16[1,192,4096]{2,1,0:T(8,128)(2,1)S(1)}, bf16[1,192,4096]{2,1,0:T(8,128)(2,1)}, u32[]{:S(2)}) copy-start(bf16[1,192,4096]{2,1,0:T(8,128)(2,1)} %param.6) | copy-start | bytes 4718596
  7.2 99.3 %all-gather.2.cloned.1.call-start = ((), (), s32[]{:S(2)}) async-start(), calls=%async_computation.4 | async-start | bytes 2228224 | tf_op jit(solution)/shard_map/all_gather | solution.py:59
  32.0 78.5 %copy-start.1 = (bf16[1,192,4096]{2,1,0:T(8,128)(2,1)S(1)}, bf16[1,192,4096]{2,1,0:T(8,128)(2,1)}, u32[]{:S(2)}) copy-start(bf16[1,192,4096]{2,1,0:T(8,128)(2,1)} %param.5) | copy-start | bytes 4718596
  32.0 168.1 %reduce-scatter.8.cloned.1.call-start = ((), (), s32[]{:S(2)}) async-start(), calls=%async_computation.5 | async-start | bytes 4456448 | tf_op jit(solution)/shard_map/reduce_scatter | solution.py:70
  118.8 300.7 %copy-start.2 = (f32[32,32]{1,0:T(8,128)S(1)}, f32[32,32]{1,0:T(8,128)}, u32[]{:S(2)}) copy-start(f32[32,32]{1,0:T(8,128)} %param.9) | copy-start | bytes 12292
  118.8 300.7 %copy-start.3 = (f32[32,32]{1,0:T(8,128)S(1)}, f32[32,32]{1,0:T(8,128)}, u32[]{:S(2)}) copy-start(f32[32,32]{1,0:T(8,128)} %param.8) | copy-start | bytes 12292
  118.8 113.0 %reduce-scatter.10.cloned.1.call-start = ((), (), s32[]{:S(2)}) async-start(), calls=%async_computation.6 | async-start | bytes 327680
  202.0 53.7 %reduce-scatter.12.cloned.1.call-start = ((), (), s32[]{:S(2)}) async-start(), calls=%async_computation.7 | async-start | bytes 98304
  273.0 3.1 collective-permute-start
  276.1 5.5 %collective-permute-start.1 = (f32[8,8]{0,1:T(8,128)S(1)}, f32[8,8]{0,1:T(8,128)S(1)}, u32[]{:S(2)}, u32[]{:S(2)}) collective-permute-start(f32[8,8]{0,1:T(8,128)S(1)} %add.52), channel_id=1, source_target_pairs={{0,2},{2,0},{4,6},{6,4},{1,3},{3,1},{5,7},{7,5},{8,10},{10,8},{12,... | collective-permute-start | bytes 776 | tf_op jit(solution)/shard_map/ppermute | solution.py:48
  281.6 7.0 %collective-permute-start.2 = (f32[8,8]{0,1:T(8,128)S(1)}, f32[8,8]{0,1:T(8,128)S(1)}, u32[]{:S(2)}, u32[]{:S(2)}) collective-permute-start(f32[8,8]{0,1:T(8,128)S(1)} %add.53), channel_id=1, source_target_pairs={{0,4},{2,6},{4,0},{6,2},{1,5},{3,7},{5,1},{7,3},{8,12},{10,14},{12... | collective-permute-start | bytes 776 | tf_op jit(solution)/shard_map/ppermute | solution.py:48
  288.6 5.5 %collective-permute-start.3 = (f32[8,8]{0,1:T(8,128)S(1)}, f32[8,8]{0,1:T(8,128)S(1)}, u32[]{:S(2)}, u32[]{:S(2)}) collective-permute-start(f32[8,8]{0,1:T(8,128)S(1)} %add.54), channel_id=1, source_target_pairs={{0,8},{8,0},{16,24},{24,16},{32,40},{40,32},{48,56},{56,48},{64,72... | collective-permute-start | bytes 776 | tf_op jit(solution)/shard_map/ppermute | solution.py:48
  294.1 6.4 %collective-permute-start.4 = (f32[8,8]{0,1:T(8,128)S(1)}, f32[8,8]{0,1:T(8,128)S(1)}, u32[]{:S(2)}, u32[]{:S(2)}) collective-permute-start(f32[8,8]{0,1:T(8,128)S(1)} %add.55), channel_id=1, source_target_pairs={{0,16},{8,24},{16,0},{24,8},{32,48},{40,56},{48,32},{56,40},{64,80... | collective-permute-start | bytes 776 | tf_op jit(solution)/shard_map/ppermute | solution.py:48
  300.5 9.6 %collective-permute-start.5 = (f32[8,8]{0,1:T(8,128)S(1)}, f32[8,8]{0,1:T(8,128)S(1)}, u32[]{:S(2)}, u32[]{:S(2)}) collective-permute-start(f32[8,8]{0,1:T(8,128)S(1)} %add.56), channel_id=1, source_target_pairs={{0,32},{8,40},{16,48},{24,56},{32,0},{40,8},{48,16},{56,24},{64,96... | collective-permute-start | bytes 776 | tf_op jit(solution)/shard_map/ppermute | solution.py:48
  310.1 14.9 %collective-permute-start.6 = (f32[8,8]{0,1:T(8,128)S(1)}, f32[8,8]{0,1:T(8,128)S(1)}, u32[]{:S(2)}, u32[]{:S(2)}) collective-permute-start(f32[8,8]{0,1:T(8,128)S(1)} %add.57), channel_id=1, source_target_pairs={{0,64},{8,72},{16,80},{24,88},{32,96},{40,104},{48,112},{56,120},{... | collective-permute-start | bytes 776 | tf_op jit(solution)/shard_map/ppermute | solution.py:48
  325.0 5.5 %collective-permute-start.7 = (f32[8,8]{0,1:T(8,128)S(1)}, f32[8,8]{0,1:T(8,128)S(1)}, u32[]{:S(2)}, u32[]{:S(2)}) collective-permute-start(f32[8,8]{0,1:T(8,128)S(1)} %add.58), channel_id=1, source_target_pairs={{0,128},{128,0},{256,384},{384,256},{512,640},{640,512},{768,896},... | collective-permute-start | bytes 776 | tf_op jit(solution)/shard_map/ppermute | solution.py:48
  330.5 6.5 %collective-permute-start.8 = (f32[8,8]{0,1:T(8,128)S(1)}, f32[8,8]{0,1:T(8,128)S(1)}, u32[]{:S(2)}, u32[]{:S(2)}) collective-permute-start(f32[8,8]{0,1:T(8,128)S(1)} %add.59), channel_id=1, source_target_pairs={{0,256},{128,384},{256,0},{384,128},{512,768},{640,896},{768,512},... | collective-permute-start | bytes 776 | tf_op jit(solution)/shard_map/ppermute | solution.py:48
  337.0 9.4 %collective-permute-start.9 = (f32[8,8]{0,1:T(8,128)S(1)}, f32[8,8]{0,1:T(8,128)S(1)}, u32[]{:S(2)}, u32[]{:S(2)}) collective-permute-start(f32[8,8]{0,1:T(8,128)S(1)} %add.60), channel_id=1, source_target_pairs={{0,512},{128,640},{256,768},{384,896},{512,0},{640,128},{768,256},... | collective-permute-start | bytes 776 | tf_op jit(solution)/shard_map/ppermute | solution.py:48
Sparse Core Ops, SparseCore 0:
  32.1 74.2 all-gather.1
  118.9 81.1 reduce-scatter.7
  203.5 28.2 reduce-scatter.9
  235.0 20.5 reduce-scatter.11

commit v2 on v1

v2 whole, which is shorter than its diff:
```python
import math

import jax
import jax.numpy as jnp
from jax import lax
from jax.experimental import pallas as pl
from jax.sharding import Mesh
from jax.sharding import PartitionSpec as P

D = 4096
RANK = 128
FSDP = ("z", "x", "core")
ALL_AXES = ("core", "x", "z", "task")


def tail_kernel(gram_ref, gramt_ref, pieces_ref, m1_ref, m2_ref, first_ref, second_ref, step_ref):
    gram = gram_ref[...]
    kt = gramt_ref[...]
    shape = gram.shape
    row = lax.broadcasted_iota(jnp.int32, shape, 0)
    lane = lax.broadcasted_iota(jnp.int32, shape, 1)

    def lanes(x):
        return jnp.sum(x, axis=1, keepdims=True)

    def sublanes(x):
        return jnp.sum(x, axis=0, keepdims=True)

    def pick(x, r, l):
        return lanes(sublanes(jnp.where((row == r) & (lane == l), x, 0.0)))

    norm_col = jnp.sqrt(lanes(jnp.where(row == lane, gram, 0.0)))
    k00 = pick(gram, 0, 0)
    n0 = jnp.sqrt(k00)
    k_i0 = sublanes(jnp.where(row == 0, kt, 0.0))
    k_0j = lanes(jnp.where(lane == 0, kt, 0.0))
    system = (k00 - k_i0) / n0 - (k_0j - kt) / norm_col
    right = k00 / n0 - k_0j / norm_col
    aug = jnp.where(lane == 0, right, system)
    tasks = pieces_ref.shape[0]
    for column in range(1, tasks):
        pivot_row = sublanes(jnp.where(row == column, aug, 0.0))
        column_vals = lanes(jnp.where(lane == column, aug, 0.0))
        pivot = lanes(jnp.where(lane[:1] == column, pivot_row, 0.0))
        factor = column_vals / pivot
        aug = jnp.where(row > column, aug - factor * pivot_row, aug)
    answer = [None] * tasks
    lane_row = lax.broadcasted_iota(jnp.int32, (1, shape[1]), 1)
    row_col = lax.broadcasted_iota(jnp.int32, (shape[0], 1), 0)
    for column in reversed(range(1, tasks)):
        pivot_row = sublanes(jnp.where(row == column, aug, 0.0))
        running = lanes(jnp.where(lane_row == 0, pivot_row, 0.0))
        for follow in range(column + 1, tasks):
            running = running - lanes(jnp.where(lane_row == follow, pivot_row, 0.0)) * answer[follow]
        answer[column] = running / lanes(jnp.where(lane_row == column, pivot_row, 0.0))
    total = answer[1]
    for column in range(2, tasks):
        total = total + answer[column]
    answer[0] = 1.0 - total
    alpha_row = jnp.zeros((1, shape[1]), jnp.float32)
    alpha_col = jnp.zeros((shape[0], 1), jnp.float32)
    for t in range(tasks):
        alpha_row = jnp.where(lane_row == t, answer[t], alpha_row)
        alpha_col = jnp.where(row_col == t, answer[t], alpha_col)
    combined = answer[0] * pieces_ref[0]
    for t in range(1, tasks):
        combined = combined + answer[t] * pieces_ref[t]
    squared = sublanes(alpha_col * lanes(gram * alpha_row))
    grad_norm = jnp.sqrt(1e-06 + squared)
    clipped = combined * (math.sqrt(2 * RANK * D) / grad_norm)
    first = 0.9 * m1_ref[...] + 0.1 * clipped
    second = 0.95 * m2_ref[...] + 0.05 * clipped * clipped
    first_ref[...] = first
    second_ref[...] = second
    step_ref[...] = first / (1.0 - 0.9**20) / (jnp.sqrt(second / (1.0 - 0.95**20)) + 1e-08)


def tail(gram, pieces, moment_one, moment_two):
    tasks = gram.shape[0]
    padded = jnp.zeros((8, 128), jnp.float32).at[:tasks, :tasks].set(gram)
    padded_t = jnp.zeros((8, 128), jnp.float32).at[:tasks, :tasks].set(gram.T)
    out = jax.ShapeDtypeStruct(moment_one.shape, jnp.float32)
    return pl.pallas_call(tail_kernel, out_shape=(out, out, out))(
        padded, padded_t, pieces, moment_one, moment_two
    )


def halve(value, axis, bit):
    me = (lax.axis_index(axis) >> bit) & 1
    size = lax.axis_size(axis)
    halves = value.reshape((2, value.shape[0] // 2) + value.shape[1:])
    mine = lax.dynamic_index_in_dim(halves, me, 0, keepdims=False)
    other = lax.dynamic_index_in_dim(halves, 1 - me, 0, keepdims=False)
    pairs = [(i, i ^ (1 << bit)) for i in range(size)]
    return mine + lax.ppermute(other, axis, pairs)


def butterfly_sum(value, axis):
    size = lax.axis_size(axis)
    step = 1
    while step < size:
        pairs = [(i, i ^ step) for i in range(size)]
        value = value + lax.ppermute(value, axis, pairs)
        step *= 2
    return value


def body(contexts, cotangents, adapter, moment_one, moment_two):
    own_context = contexts[0]
    own_cotangent = cotangents[0]
    rank_width = adapter.shape[1] // 2
    piece = adapter
    for axis in ("z", "x", "core"):
        piece = lax.all_gather(piece, axis, axis=0, tiled=True)
    zs, xs, cs = (lax.axis_size(a) for a in FSDP)
    blocks_in = piece.reshape(cs, xs, zs, -1, piece.shape[1])
    piece = blocks_in.transpose(2, 1, 0, 3, 4).reshape(piece.shape)
    low = jnp.dot(own_context, piece[:, :rank_width], preferred_element_type=jnp.float32).astype(jnp.bfloat16)
    back = jnp.dot(own_cotangent, piece[:, rank_width:], preferred_element_type=jnp.float32).astype(jnp.bfloat16)
    down_part = lax.dot_general(
        own_context, back, (((0,), (0,)), ((), ())), preferred_element_type=jnp.float32
    )
    up_part = lax.dot_general(
        own_cotangent, low, (((0,), (0,)), ((), ())), preferred_element_type=jnp.float32
    )
    grad_rows = jnp.concatenate([down_part, up_part], axis=1)
    full = grad_rows.shape
    grad_rows = grad_rows.reshape(zs, xs, cs, -1, full[1]).transpose(2, 0, 1, 3, 4).reshape(full)
    grad_rows = halve(grad_rows, "core", 0)
    grad_rows = lax.psum_scatter(grad_rows, "z", scatter_dimension=0, tiled=True)
    grad_rows = halve(grad_rows, "x", 1)
    grad_rows = halve(grad_rows, "x", 0)
    tasks = lax.axis_size("task")
    rows, width = grad_rows.shape
    blocks = grad_rows.reshape(rows, tasks, width // tasks).transpose(1, 0, 2)
    pieces = lax.all_to_all(blocks, "task", 0, 0, tiled=True)
    partial_gram = jnp.einsum("sij,tij->st", pieces, pieces, precision=lax.Precision.HIGHEST)
    gram_matrix = partial_gram
    for axis in ALL_AXES:
        gram_matrix = butterfly_sum(gram_matrix, axis)
    return tail(gram_matrix, pieces, moment_one, moment_two)


def solution(mesh):
    tasks, fsdp = mesh.devices.shape
    split = Mesh(mesh.devices.reshape(tasks, fsdp // 8, 4, 2), ("task",) + FSDP)
    in_specs = (
        P("task", FSDP, None),
        P("task", FSDP, None),
        P(FSDP, None),
        P(FSDP, "task"),
        P(FSDP, "task"),
    )
    out_specs = (P(FSDP, "task"), P(FSDP, "task"), P(FSDP, "task"))
    return jax.shard_map(body, mesh=split, in_specs=in_specs, out_specs=out_specs, check_vma=False)
```

time: 428 us -> 341 us (0.80)
  waiting for transfers between devices: 238 us -> 182 us
  between operations: 69.4 us -> 14 us
  blocking collectives: 39.3 us -> 60.9 us
  other arithmetic: 6.97 us -> 11.4 us
    unnamed x6 -> x3, waiting for transfers between devices: 53.7 us -> 0.05 us
    all_gather x2 -> x1, blocking collectives: 24.8 us -> 46.3 us  [body(): piece = lax.all_gather(piece, axis, axis=0, tiled=True)]
    all_gather x1 -> x2, waiting for transfers between devices: 74.4 us -> 55.2 us  [body(): piece = lax.all_gather(piece, axis, axis=0, tiled=True)]
    slice x25 -> x0, local copies, waits for them, and re-layouts: 14.9 us -> none  [the longest x16 9.69 us: eliminate(): factor = matrix_rows[target][column] / matrix_rows[column][column]]
    ppermute x0 -> x3, waiting for transfers between devices: none -> 11.1 us  [halve(): return mine + lax.ppermute(other, axis, pairs)]
    ppermute x10, starting transfers between devices: 44.8 us -> 35.7 us  [butterfly_sum(): value = value + lax.ppermute(value, axis, pairs)]
    ppermute x0 -> x3, starting transfers between devices: none -> 8.7 us  [halve(): return mine + lax.ppermute(other, axis, pairs)]
    ppermute x10, waiting for transfers between devices: 28.5 us -> 35.9 us  [butterfly_sum(): value = value + lax.ppermute(value, axis, pairs)]
  transfers between devices with their start and end apart: 14 -> 16, of which waited for: 14 -> 16; matrix products, arithmetic and copies ran while one was open for 0% -> 0% of each run, Pallas kernels for 0% -> 0%
where the time goes in v2:
time: 341 us; the launch traced here: 340 us
  waiting for transfers between devices  182 us (53%)
  blocking collectives  60.9 us (18%)
  starting transfers between devices  44.5 us (13%)
  local copies, waits for them, and re-layouts  17.1 us (5%)
  between operations  14 us (4%)
  other arithmetic  11.4 us (3%)
  matrix products  7.54 us (2%)
    reduce_scatter x1, waiting for transfers between devices, body(): lax.psum_scatter(grad_rows, 'z', scatter_dimension=0, tiled=True)  79.6 us
    all_gather x2, waiting for transfers between devices, body(): piece = lax.all_gather(piece, axis, axis=0, tiled=True)  55.2 us
    all_gather x1, blocking collectives, body(): piece = lax.all_gather(piece, axis, axis=0, tiled=True)  46.3 us
    ppermute x10, waiting for transfers between devices, butterfly_sum(): value = value + lax.ppermute(value, axis, pairs)  35.9 us
    ppermute x10, starting transfers between devices, butterfly_sum(): value = value + lax.ppermute(value, axis, pairs)  35.7 us
    all_to_all x1, blocking collectives, body(): pieces = lax.all_to_all(blocks, 'task', 0, 0, tiled=True)  14.6 us
    ppermute x3, waiting for transfers between devices, halve(): return mine + lax.ppermute(other, axis, pairs)  11.1 us
    ppermute x3, starting transfers between devices, halve(): return mine + lax.ppermute(other, axis, pairs)  8.7 us
  transfers between devices with their start and end apart: 16, of which 16 were waited for; matrix products, arithmetic and copies ran while one was open for 0% of the time, Pallas kernels for 0%

profile of v2, /device:TPU:6, one launch (start us, length us, event | category | flops | bytes accessed | tf_op | source)
XLA Modules:
  0.0 339.7 jit_solution(12786017621271852857)
XLA Ops:
  7.2 46.3 %all_gather.9 = bf16[512,256]{1,0:T(8,128)(2,1)} all-gather(bf16[32,256]{1,0:T(8,128)(2,1)} %param.11), channel_id=1, replica_groups=mesh['task'=8,'z'=16,'x'=4,'core'=2] {'z'}, dimensions={0}, use_global_device_ids=true | all-gather | bytes 278528 | tf_op jit(solution)/shard_map/all_gather | solution.py:114
  53.6 27.5 %all-gather.3.cloned.1.call-done = bf16[2048,256]{1,0:T(8,128)(2,1)} async-done(((bf16[512,256]{1,0:T(8,128)(2,1)}), bf16[2048,256]{1,0:T(8,128)(2,1)}) %all-gather.3.cloned.1.call-update) | async-done | bytes 1048592 | tf_op jit(solution)/shard_map/all_gather | solution.py:114
  81.2 27.7 %all-gather.5.cloned.1.call-done = bf16[4096,256]{1,0:T(8,128)(2,1)} async-done(((bf16[2048,256]{1,0:T(8,128)(2,1)}), bf16[4096,256]{1,0:T(8,128)(2,1)}) %all-gather.5.cloned.1.call-update) | async-done | bytes 2097168 | tf_op jit(solution)/shard_map/all_gather | solution.py:114
  108.9 3.3 copy.21
  112.2 3.6 %convolution_bitcast_fusion = f32[4096,128]{0,1:T(8,128)} fusion(bf16[1,192,4096]{2,1,0:T(8,128)(2,1)S(1)} %copy-done, bf16[1,192,4096]{2,1,0:T(8,128)(2,1)S(1)} %copy-done.2, bf16[4096,256]{1,0:T(8,128)(2,1)} %bitcast.55), kind=kOutput, calls=%fused_computation | convolution fusion | flops 402677760 | bytes 6291456 | tf_op jit(solution)/shard_map/dot_general | solution.py:123
  115.8 3.6 %convolution_bitcast_fusion.1 = f32[4096,128]{0,1:T(8,128)} fusion(bf16[1,192,4096]{2,1,0:T(8,128)(2,1)S(1)} %copy-done.2, bf16[1,192,4096]{2,1,0:T(8,128)(2,1)S(1)} %copy-done, bf16[4096,256]{1,0:T(8,128)(2,1)} %bitcast.56), kind=kOutput, calls=%fused_computation.1 | convolution fusion | flops 402677760 | bytes 6291456 | tf_op jit(solution)/shard_map/dot_general | solution.py:120
  119.4 4.6 %pad_maximum_fusion = f32[4096,256]{0,1:T(8,128)} fusion(f32[4096,128]{0,1:T(8,128)} %convolution_bitcast_fusion, f32[4096,128]{0,1:T(8,128)} %convolution_bitcast_fusion.1), kind=kLoop, calls=%fused_computation.2 | loop fusion | flops 1048576 | bytes 8388608 | tf_op jit(solution)/shard_map/concatenate | solution.py:126
  124.0 5.7 %copy.22 = f32[4096,256]{1,0:T(8,128)} copy(f32[4096,256]{0,1:T(8,128)} %pad_maximum_fusion) | data formatting | bytes 8388608 | tf_op jit(solution)/shard_map/concatenate | solution.py:126
  129.7 2.5 copy.23
  137.0 4.2 %collective-permute-done = f32[2048,256]{1,0:T(8,128)} collective-permute-done((f32[2048,256]{1,0:T(8,128)}, f32[2048,256]{1,0:T(8,128)}, u32[]{:S(2)}, u32[]{:S(2)}) %collective-permute-start) | collective-permute-done | bytes 2097184 | tf_op jit(solution)/shard_map/ppermute | solution.py:95
  141.2 3.8 %bitcast_add_fusion = f32[2048,256]{1,0:T(8,128)} fusion(f32[2048,256]{1,0:T(8,128)} %collective-permute-done, f32[2,2048,256]{2,1,0:T(8,128)} %bitcast.53, s32[]{:T(128)S(6)} %select_n.21), kind=kLoop, calls=%fused_computation.3 | loop fusion | flops 524288 | bytes 6291460 | tf_op jit(solution)/shard_map/add | solution.py:95
  145.1 79.6 %reduce-scatter.2.cloned.1.call-done = f32[128,256]{1,0:T(8,128)} async-done(((f32[2048,256]{1,0:T(8,128)}), f32[128,256]{1,0:T(8,128)}) %reduce-scatter.2.cloned.1.call-update) | async-done | bytes 131088 | tf_op jit(solution)/shard_map/reduce_scatter | solution.py:130
  225.5 3.5 %collective-permute-start.1 = (f32[64,256]{1,0:T(8,128)S(1)}, f32[64,256]{1,0:T(8,128)S(1)}, u32[]{:S(2)}, u32[]{:S(2)}) collective-permute-start(f32[64,256]{1,0:T(8,128)S(1)} %dynamic-slice_bitcast_fusion.1), channel_id=1, source_target_pairs={{0,4},{2,6},{4,0},{6,2},{1,5},{3,7},{5,1},{7,3},{8,12},{10,14},{12... | collective-permute-start | bytes 196616 | tf_op jit(solution)/shard_map/ppermute | solution.py:95
  229.1 4.1 %collective-permute-done.1 = f32[64,256]{1,0:T(8,128)S(1)} collective-permute-done((f32[64,256]{1,0:T(8,128)S(1)}, f32[64,256]{1,0:T(8,128)S(1)}, u32[]{:S(2)}, u32[]{:S(2)}) %collective-permute-start.1) | collective-permute-done | bytes 65568 | tf_op jit(solution)/shard_map/ppermute | solution.py:95
  234.0 3.0 collective-permute-start.2
  237.0 2.8 collective-permute-done.2
  240.1 14.6 %all_to_all.5 = f32[8,1,1024]{2,1,0:T(1,128)S(1)} all-to-all(f32[8,1,1024]{2,1,0:T(1,128)S(1)} %reshape.80), channel_id=1, replica_groups=mesh['task'=8,'z'=16,'x'=4,'core'=2] {'task'}, dimensions={0} | all-to-all | bytes 65536 | tf_op jit(solution)/shard_map/all_to_all | solution.py:136
  259.5 2.8 collective-permute-start.4
  262.3 2.6 collective-permute-done.4
  265.0 3.3 collective-permute-start.5
  268.3 3.7 %collective-permute-done.5 = f32[8,8]{0,1:T(8,128)S(1)} collective-permute-done((f32[8,8]{0,1:T(8,128)S(1)}, f32[8,8]{0,1:T(8,128)S(1)}, u32[]{:S(2)}, u32[]{:S(2)}) %collective-permute-start.5) | collective-permute-done | bytes 288 | tf_op jit(solution)/shard_map/ppermute | solution.py:103
  272.0 2.6 collective-permute-start.6
  274.6 2.9 collective-permute-done.6
  277.5 3.3 collective-permute-start.7
  280.7 3.1 collective-permute-done.7
  283.9 5.4 %collective-permute-start.8 = (f32[8,8]{0,1:T(8,128)S(1)}, f32[8,8]{0,1:T(8,128)S(1)}, u32[]{:S(2)}, u32[]{:S(2)}) collective-permute-start(f32[8,8]{0,1:T(8,128)S(1)} %add.86), channel_id=1, source_target_pairs={{0,32},{8,40},{16,48},{24,56},{32,0},{40,8},{48,16},{56,24},{64,96... | collective-permute-start | bytes 776 | tf_op jit(solution)/shard_map/ppermute | solution.py:103
  289.3 4.0 %collective-permute-done.8 = f32[8,8]{0,1:T(8,128)S(1)} collective-permute-done((f32[8,8]{0,1:T(8,128)S(1)}, f32[8,8]{0,1:T(8,128)S(1)}, u32[]{:S(2)}, u32[]{:S(2)}) %collective-permute-start.8) | collective-permute-done | bytes 288 | tf_op jit(solution)/shard_map/ppermute | solution.py:103
  293.3 9.2 %collective-permute-start.9 = (f32[8,8]{0,1:T(8,128)S(1)}, f32[8,8]{0,1:T(8,128)S(1)}, u32[]{:S(2)}, u32[]{:S(2)}) collective-permute-start(f32[8,8]{0,1:T(8,128)S(1)} %add.87), channel_id=1, source_target_pairs={{0,64},{8,72},{16,80},{24,88},{32,96},{40,104},{48,112},{56,120},{... | collective-permute-start | bytes 776 | tf_op jit(solution)/shard_map/ppermute | solution.py:103
  302.4 5.0 %collective-permute-done.9 = f32[8,8]{0,1:T(8,128)S(1)} collective-permute-done((f32[8,8]{0,1:T(8,128)S(1)}, f32[8,8]{0,1:T(8,128)S(1)}, u32[]{:S(2)}, u32[]{:S(2)}) %collective-permute-start.9) | collective-permute-done | bytes 288 | tf_op jit(solution)/shard_map/ppermute | solution.py:103
  309.9 3.0 collective-permute-done.10
  315.3 4.1 %collective-permute-done.11 = f32[8,8]{0,1:T(8,128)S(1)} collective-permute-done((f32[8,8]{0,1:T(8,128)S(1)}, f32[8,8]{0,1:T(8,128)S(1)}, u32[]{:S(2)}, u32[]{:S(2)}) %collective-permute-start.11) | collective-permute-done | bytes 288 | tf_op jit(solution)/shard_map/ppermute | solution.py:103
  322.4 6.4 %collective-permute-done.12 = f32[8,8]{0,1:T(8,128)S(1)} collective-permute-done((f32[8,8]{0,1:T(8,128)S(1)}, f32[8,8]{0,1:T(8,128)S(1)}, u32[]{:S(2)}, u32[]{:S(2)}) %collective-permute-start.12) | collective-permute-done | bytes 288 | tf_op jit(solution)/shard_map/ppermute | solution.py:103
  (47 shorter events, 23.9 us)
Async XLA Ops:
  7.2 105.0 %copy-start = (bf16[1,192,4096]{2,1,0:T(8,128)(2,1)S(1)}, bf16[1,192,4096]{2,1,0:T(8,128)(2,1)}, u32[]{:S(2)}) copy-start(bf16[1,192,4096]{2,1,0:T(8,128)(2,1)} %param.10) | copy-start | bytes 4718596
  7.2 73.9 %all-gather.3.cloned.1.call-start = ((), (), s32[]{:S(2)}) async-start(), calls=%async_computation.2 | async-start | bytes 1310720 | tf_op jit(solution)/shard_map/all_gather | solution.py:114
  53.6 55.4 %all-gather.5.cloned.1.call-start = ((), (), s32[]{:S(2)}) async-start(), calls=%async_computation.3 | async-start | bytes 3145728 | tf_op jit(solution)/shard_map/all_gather | solution.py:114
  81.1 143.5 %reduce-scatter.2.cloned.1.call-start = ((), (), s32[]{:S(2)}) async-start(), calls=%async_computation.4 | async-start | bytes 2228224 | tf_op jit(solution)/shard_map/reduce_scatter | solution.py:130
  108.9 3.3 copy-start.2
  132.2 2.6 copy-start.1
  134.8 6.4 %collective-permute-start = (f32[2048,256]{1,0:T(8,128)}, f32[2048,256]{1,0:T(8,128)}, u32[]{:S(2)}, u32[]{:S(2)}) collective-permute-start(f32[2048,256]{1,0:T(8,128)} %dynamic-slice_bitcast_fusion), channel_id=1, source_target_pairs={{0,1},{1,0},{2,3},{3,2},{4,5},{5,4},{6,7},{7,6},{8,9},{9,8},{10,11... | collective-permute-start | bytes 6291464 | tf_op jit(solution)/shard_map/ppermute | solution.py:95
  225.5 7.7 %collective-permute-start.1 = (f32[64,256]{1,0:T(8,128)S(1)}, f32[64,256]{1,0:T(8,128)S(1)}, u32[]{:S(2)}, u32[]{:S(2)}) collective-permute-start(f32[64,256]{1,0:T(8,128)S(1)} %dynamic-slice_bitcast_fusion.1), channel_id=1, source_target_pairs={{0,4},{2,6},{4,0},{6,2},{1,5},{3,7},{5,1},{7,3},{8,12},{10,14},{12... | collective-permute-start | bytes 196616 | tf_op jit(solution)/shard_map/ppermute | solution.py:95
  234.0 5.8 %collective-permute-start.2 = (f32[32,256]{1,0:T(8,128)S(1)}, f32[32,256]{1,0:T(8,128)S(1)}, u32[]{:S(2)}, u32[]{:S(2)}) collective-permute-start(f32[32,256]{1,0:T(8,128)S(1)} %dynamic-slice_bitcast_fusion.2), channel_id=1, source_target_pairs={{0,2},{2,0},{4,6},{6,4},{1,3},{3,1},{5,7},{7,5},{8,10},{10,8},{12,... | collective-permute-start | bytes 98312 | tf_op jit(solution)/shard_map/ppermute | solution.py:95
  256.0 74.7 %copy-start.3 = (f32[8,32,32]{2,1,0:T(8,128)}, f32[8,32,32]{2,1,0:T(8,128)S(1)}, u32[]{:S(2)}) copy-start(f32[8,32,32]{2,1,0:T(8,128)S(1)} %reshape.81.pieces_ref) | copy-start | bytes 98308
  256.4 3.1 collective-permute-start.3
  259.5 5.5 %collective-permute-start.4 = (f32[8,8]{0,1:T(8,128)S(1)}, f32[8,8]{0,1:T(8,128)S(1)}, u32[]{:S(2)}, u32[]{:S(2)}) collective-permute-start(f32[8,8]{0,1:T(8,128)S(1)} %add.82), channel_id=1, source_target_pairs={{0,2},{2,0},{4,6},{6,4},{1,3},{3,1},{5,7},{7,5},{8,10},{10,8},{12,... | collective-permute-start | bytes 776 | tf_op jit(solution)/shard_map/ppermute | solution.py:103
  265.0 7.0 %collective-permute-start.5 = (f32[8,8]{0,1:T(8,128)S(1)}, f32[8,8]{0,1:T(8,128)S(1)}, u32[]{:S(2)}, u32[]{:S(2)}) collective-permute-start(f32[8,8]{0,1:T(8,128)S(1)} %add.83), channel_id=1, source_target_pairs={{0,4},{2,6},{4,0},{6,2},{1,5},{3,7},{5,1},{7,3},{8,12},{10,14},{12... | collective-permute-start | bytes 776 | tf_op jit(solution)/shard_map/ppermute | solution.py:103
  272.0 5.5 %collective-permute-start.6 = (f32[8,8]{0,1:T(8,128)S(1)}, f32[8,8]{0,1:T(8,128)S(1)}, u32[]{:S(2)}, u32[]{:S(2)}) collective-permute-start(f32[8,8]{0,1:T(8,128)S(1)} %add.84), channel_id=1, source_target_pairs={{0,8},{8,0},{16,24},{24,16},{32,40},{40,32},{48,56},{56,48},{64,72... | collective-permute-start | bytes 776 | tf_op jit(solution)/shard_map/ppermute | solution.py:103
  277.5 6.4 %collective-permute-start.7 = (f32[8,8]{0,1:T(8,128)S(1)}, f32[8,8]{0,1:T(8,128)S(1)}, u32[]{:S(2)}, u32[]{:S(2)}) collective-permute-start(f32[8,8]{0,1:T(8,128)S(1)} %add.85), channel_id=1, source_target_pairs={{0,16},{8,24},{16,0},{24,8},{32,48},{40,56},{48,32},{56,40},{64,80... | collective-permute-start | bytes 776 | tf_op jit(solution)/shard_map/ppermute | solution.py:103
  283.9 9.4 %collective-permute-start.8 = (f32[8,8]{0,1:T(8,128)S(1)}, f32[8,8]{0,1:T(8,128)S(1)}, u32[]{:S(2)}, u32[]{:S(2)}) collective-permute-start(f32[8,8]{0,1:T(8,128)S(1)} %add.86), channel_id=1, source_target_pairs={{0,32},{8,40},{16,48},{24,56},{32,0},{40,8},{48,16},{56,24},{64,96... | collective-permute-start | bytes 776 | tf_op jit(solution)/shard_map/ppermute | solution.py:103
  293.3 14.2 %collective-permute-start.9 = (f32[8,8]{0,1:T(8,128)S(1)}, f32[8,8]{0,1:T(8,128)S(1)}, u32[]{:S(2)}, u32[]{:S(2)}) collective-permute-start(f32[8,8]{0,1:T(8,128)S(1)} %add.87), channel_id=1, source_target_pairs={{0,64},{8,72},{16,80},{24,88},{32,96},{40,104},{48,112},{56,120},{... | collective-permute-start | bytes 776 | tf_op jit(solution)/shard_map/ppermute | solution.py:103
  307.5 5.5 %collective-permute-start.10 = (f32[8,8]{0,1:T(8,128)S(1)}, f32[8,8]{0,1:T(8,128)S(1)}, u32[]{:S(2)}, u32[]{:S(2)}) collective-permute-start(f32[8,8]{0,1:T(8,128)S(1)} %add.88), channel_id=1, source_target_pairs={{0,128},{128,0},{256,384},{384,256},{512,640},{640,512},{768,896},... | collective-permute-start | bytes 776 | tf_op jit(solution)/shard_map/ppermute | solution.py:103
  313.0 6.4 %collective-permute-start.11 = (f32[8,8]{0,1:T(8,128)S(1)}, f32[8,8]{0,1:T(8,128)S(1)}, u32[]{:S(2)}, u32[]{:S(2)}) collective-permute-start(f32[8,8]{0,1:T(8,128)S(1)} %add.89), channel_id=1, source_target_pairs={{0,256},{128,384},{256,0},{384,128},{512,768},{640,896},{768,512},... | collective-permute-start | bytes 776 | tf_op jit(solution)/shard_map/ppermute | solution.py:103
  319.4 9.4 %collective-permute-start.12 = (f32[8,8]{0,1:T(8,128)S(1)}, f32[8,8]{0,1:T(8,128)S(1)}, u32[]{:S(2)}, u32[]{:S(2)}) collective-permute-start(f32[8,8]{0,1:T(8,128)S(1)} %add.90), channel_id=1, source_target_pairs={{0,512},{128,640},{256,768},{384,896},{512,0},{640,128},{768,256},... | collective-permute-start | bytes 776 | tf_op jit(solution)/shard_map/ppermute | solution.py:103
Sparse Core Ops, SparseCore 0:
  53.7 27.3 all-gather.2
  83.8 25.0 all-gather.4
  145.2 79.4 reduce-scatter.1

commit v3 on v2

--- a/solution.py
+++ b/solution.py
@@ -95,6 +95,16 @@
     return mine + lax.ppermute(other, axis, pairs)
 
 
+def double(value, axis, bit):
+    me = (lax.axis_index(axis) >> bit) & 1
+    size = lax.axis_size(axis)
+    pairs = [(i, i ^ (1 << bit)) for i in range(size)]
+    other = lax.ppermute(value, axis, pairs)
+    first = jnp.where(me == 0, value, other)
+    second = jnp.where(me == 0, other, value)
+    return jnp.concatenate([first, second], axis=0)
+
+
 def butterfly_sum(value, axis):
     size = lax.axis_size(axis)
     step = 1
@@ -109,9 +119,10 @@
     own_context = contexts[0]
     own_cotangent = cotangents[0]
     rank_width = adapter.shape[1] // 2
-    piece = adapter
-    for axis in ("z", "x", "core"):
-        piece = lax.all_gather(piece, axis, axis=0, tiled=True)
+    piece = lax.all_gather(adapter, "z", axis=0, tiled=True)
+    piece = double(piece, "x", 0)
+    piece = double(piece, "x", 1)
+    piece = double(piece, "core", 0)
     zs, xs, cs = (lax.axis_size(a) for a in FSDP)
     blocks_in = piece.reshape(cs, xs, zs, -1, piece.shape[1])
     piece = blocks_in.transpose(2, 1, 0, 3, 4).reshape(piece.shape)
@@ -125,8 +136,11 @@
     )
     grad_rows = jnp.concatenate([down_part, up_part], axis=1)
     full = grad_rows.shape
-    grad_rows = grad_rows.reshape(zs, xs, cs, -1, full[1]).transpose(2, 0, 1, 3, 4).reshape(full)
-    grad_rows = halve(grad_rows, "core", 0)
+    by_core = grad_rows.reshape(zs * xs, cs, -1, full[1])
+    me = lax.axis_index("core")
+    mine = lax.dynamic_index_in_dim(by_core, me, 1, keepdims=False).reshape(-1, full[1])
+    other = lax.dynamic_index_in_dim(by_core, 1 - me, 1, keepdims=False).reshape(-1, full[1])
+    grad_rows = mine + lax.ppermute(other, "core", [(0, 1), (1, 0)])
     grad_rows = lax.psum_scatter(grad_rows, "z", scatter_dimension=0, tiled=True)
     grad_rows = halve(grad_rows, "x", 1)
     grad_rows = halve(grad_rows, "x", 0)

time: 341 us -> 302 us (0.89)
  waiting for transfers between devices: 182 us -> 141 us
  starting transfers between devices: 44.5 us -> 49.8 us
  local copies, waits for them, and re-layouts: 17.1 us -> 13.2 us
    all_gather x2 -> x0, waiting for transfers between devices: 55.2 us -> none  [body(): piece = lax.all_gather(piece, axis, axis=0, tiled=True)]
    ppermute x0 -> x4, waiting for transfers between devices: none -> 25.3 us  [the longest x3 21.3 us: double(): other = lax.ppermute(value, axis, pairs)]
    ppermute x0 -> x4, starting transfers between devices: none -> 9.35 us  [the longest x3 7.29 us: double(): other = lax.ppermute(value, axis, pairs)]
    reduce_scatter x1, waiting for transfers between devices: 79.6 us -> 70.9 us  [body(): lax.psum_scatter(grad_rows, 'z', scatter_dimension=0, tiled=True)]
    ppermute x3 -> x2, waiting for transfers between devices: 11.1 us -> 6.88 us  [halve(): return mine + lax.ppermute(other, axis, pairs)]
    add x3 -> x2, other arithmetic: 4.7 us -> 0.85 us  [halve(): return mine + lax.ppermute(other, axis, pairs)]
    ppermute x3 -> x2, starting transfers between devices: 8.7 us -> 6.56 us  [halve(): return mine + lax.ppermute(other, axis, pairs)]
  transfers between devices with their start and end apart: 16 -> 17, of which waited for: 16 -> 17; matrix products, arithmetic and copies ran while one was open for 0% -> 0% of each run, Pallas kernels for 0% -> 0%
where the time goes in v3:
time: 302 us; the launch traced here: 300 us
  waiting for transfers between devices  141 us (47%)
  blocking collectives  58.9 us (20%)
  starting transfers between devices  49.8 us (16%)
  between operations  14.3 us (5%)
  other arithmetic  13.4 us (4%)
  local copies, waits for them, and re-layouts  13.2 us (4%)
  matrix products  7.57 us (3%)
    reduce_scatter x1, waiting for transfers between devices, body(): lax.psum_scatter(grad_rows, 'z', scatter_dimension=0, tiled=True)  70.9 us
    all_gather x1, blocking collectives, body(): piece = lax.all_gather(adapter, 'z', axis=0, tiled=True)  44 us
    ppermute x10, waiting for transfers between devices, butterfly_sum(): value = value + lax.ppermute(value, axis, pairs)  37.8 us
    ppermute x10, starting transfers between devices, butterfly_sum(): value = value + lax.ppermute(value, axis, pairs)  33.9 us
    ppermute x3, waiting for transfers between devices, double(): other = lax.ppermute(value, axis, pairs)  21.3 us
    all_to_all x1, blocking collectives, body(): pieces = lax.all_to_all(blocks, 'task', 0, 0, tiled=True)  14.9 us
    ppermute x3, starting transfers between devices, double(): other = lax.ppermute(value, axis, pairs)  7.29 us
    ppermute x2, waiting for transfers between devices, halve(): return mine + lax.ppermute(other, axis, pairs)  6.88 us
  transfers between devices with their start and end apart: 17, of which 17 were waited for; matrix products, arithmetic and copies ran while one was open for 0% of the time, Pallas kernels for 0%

profile of v3, /device:TPU:6, one launch (start us, length us, event | category | flops | bytes accessed | tf_op | source)
XLA Modules:
  0.0 300.5 jit_solution(5149571524674072128)
XLA Ops:
  7.2 44.0 %all_gather.3 = bf16[512,256]{1,0:T(8,128)(2,1)S(1)} all-gather(bf16[32,256]{1,0:T(8,128)(2,1)} %param.11), channel_id=1, replica_groups=mesh['task'=8,'z'=16,'x'=4,'core'=2] {'z'}, dimensions={0}, use_global_device_ids=true | all-gather | bytes 278528 | tf_op jit(solution)/shard_map/all_gather | solution.py:122
  51.2 2.7 collective-permute-start
  54.0 8.3 %collective-permute-done = bf16[512,256]{1,0:T(8,128)(2,1)S(1)} collective-permute-done((bf16[512,256]{1,0:T(8,128)(2,1)S(1)}, bf16[512,256]{1,0:T(8,128)(2,1)S(1)}, u32[]{:S(2)}, u32[]{:S(2)}) %collective-permute-start) | collective-permute-done | bytes 262176 | tf_op jit(solution)/shard_map/ppermute | solution.py:102
  62.4 2.7 collective-permute-start.1
  65.0 10.0 %collective-permute-done.1 = bf16[1024,256]{1,0:T(8,128)(2,1)} collective-permute-done((bf16[1024,256]{1,0:T(8,128)(2,1)S(1)}, bf16[1024,256]{1,0:T(8,128)(2,1)}, u32[]{:S(2)}, u32[]{:S(2)}) %collective-permute-start.1) | collective-permute-done | bytes 524320 | tf_op jit(solution)/shard_map/ppermute | solution.py:102
  79.3 3.0 collective-permute-done.2
  86.0 3.6 %convolution_bitcast_fusion = f32[4096,128]{0,1:T(8,128)} fusion(bf16[1,192,4096]{2,1,0:T(8,128)(2,1)S(1)} %copy-done, bf16[1,192,4096]{2,1,0:T(8,128)(2,1)S(1)} %copy-done.1, bf16[4096,256]{1,0:T(8,128)(2,1)} %bitcast.50), kind=kOutput, calls=%fused_computation | convolution fusion | flops 402677760 | bytes 6291456 | tf_op jit(solution)/shard_map/dot_general | solution.py:134
  89.6 3.6 %convolution_bitcast_fusion.1 = f32[4096,128]{0,1:T(8,128)} fusion(bf16[1,192,4096]{2,1,0:T(8,128)(2,1)S(1)} %copy-done.1, bf16[1,192,4096]{2,1,0:T(8,128)(2,1)S(1)} %copy-done, bf16[4096,256]{1,0:T(8,128)(2,1)} %bitcast.51), kind=kOutput, calls=%fused_computation.1 | convolution fusion | flops 402677760 | bytes 6291456 | tf_op jit(solution)/shard_map/dot_general | solution.py:131
  93.2 4.6 %pad_maximum_fusion = f32[4096,256]{0,1:T(8,128)} fusion(f32[4096,128]{0,1:T(8,128)} %convolution_bitcast_fusion, f32[4096,128]{0,1:T(8,128)} %convolution_bitcast_fusion.1), kind=kLoop, calls=%fused_computation.2 | loop fusion | flops 1048576 | bytes 8388608 | tf_op jit(solution)/shard_map/concatenate | solution.py:137
  97.8 5.7 %copy.21 = f32[4096,256]{1,0:T(8,128)} copy(f32[4096,256]{0,1:T(8,128)} %pad_maximum_fusion) | data formatting | bytes 8388608 | tf_op jit(solution)/shard_map/concatenate | solution.py:137
  103.5 2.5 constant_dynamic-slice_fusion.1
  108.1 4.0 %collective-permute-done.3 = f32[2048,256]{1,0:T(8,128)S(1)} collective-permute-done((f32[2048,256]{1,0:T(8,128)S(1)}, f32[2048,256]{1,0:T(8,128)S(1)}, u32[]{:S(2)}, u32[]{:S(2)}) %collective-permute-start.3) | collective-permute-done | bytes 2097184 | tf_op jit(solution)/shard_map/ppermute | solution.py:143
  113.9 70.9 %reduce-scatter.2.cloned.1.call-done = f32[128,256]{1,0:T(8,128)} async-done(((f32[2048,256]{1,0:T(8,128)}), f32[128,256]{1,0:T(8,128)}) %reduce-scatter.2.cloned.1.call-update) | async-done | bytes 131088 | tf_op jit(solution)/shard_map/reduce_scatter | solution.py:144
  185.6 3.6 %collective-permute-start.4 = (f32[64,256]{1,0:T(8,128)S(1)}, f32[64,256]{1,0:T(8,128)S(1)}, u32[]{:S(2)}, u32[]{:S(2)}) collective-permute-start(f32[64,256]{1,0:T(8,128)S(1)} %dynamic-slice_bitcast_fusion), channel_id=1, source_target_pairs={{0,4},{2,6},{4,0},{6,2},{1,5},{3,7},{5,1},{7,3},{8,12},{10,14},{12... | collective-permute-start | bytes 196616 | tf_op jit(solution)/shard_map/ppermute | solution.py:95
  189.2 4.1 %collective-permute-done.4 = f32[64,256]{1,0:T(8,128)S(1)} collective-permute-done((f32[64,256]{1,0:T(8,128)S(1)}, f32[64,256]{1,0:T(8,128)S(1)}, u32[]{:S(2)}, u32[]{:S(2)}) %collective-permute-start.4) | collective-permute-done | bytes 65568 | tf_op jit(solution)/shard_map/ppermute | solution.py:95
  194.2 3.0 collective-permute-start.5
  197.2 2.8 collective-permute-done.5
  200.2 14.9 %all_to_all.5 = f32[8,1,1024]{2,1,0:T(1,128)S(1)} all-to-all(f32[8,1,1024]{2,1,0:T(1,128)S(1)} %reshape.90), channel_id=1, replica_groups=mesh['task'=8,'z'=16,'x'=4,'core'=2] {'task'}, dimensions={0} | all-to-all | bytes 65536 | tf_op jit(solution)/shard_map/all_to_all | solution.py:150
  219.9 2.7 collective-permute-start.7
  222.7 2.7 collective-permute-done.7
  225.4 3.3 %collective-permute-start.8 = (f32[8,8]{0,1:T(8,128)S(1)}, f32[8,8]{0,1:T(8,128)S(1)}, u32[]{:S(2)}, u32[]{:S(2)}) collective-permute-start(f32[8,8]{0,1:T(8,128)S(1)} %add.83), channel_id=1, source_target_pairs={{0,4},{2,6},{4,0},{6,2},{1,5},{3,7},{5,1},{7,3},{8,12},{10,14},{12... | collective-permute-start | bytes 776 | tf_op jit(solution)/shard_map/ppermute | solution.py:113
  228.7 3.7 %collective-permute-done.8 = f32[8,8]{0,1:T(8,128)S(1)} collective-permute-done((f32[8,8]{0,1:T(8,128)S(1)}, f32[8,8]{0,1:T(8,128)S(1)}, u32[]{:S(2)}, u32[]{:S(2)}) %collective-permute-start.8) | collective-permute-done | bytes 288 | tf_op jit(solution)/shard_map/ppermute | solution.py:113
  234.7 3.2 %collective-permute-done.9 = f32[8,8]{0,1:T(8,128)S(1)} collective-permute-done((f32[8,8]{0,1:T(8,128)S(1)}, f32[8,8]{0,1:T(8,128)S(1)}, u32[]{:S(2)}, u32[]{:S(2)}) %collective-permute-start.9) | collective-permute-done | bytes 288 | tf_op jit(solution)/shard_map/ppermute | solution.py:113
  237.9 3.0 collective-permute-start.10
  240.9 3.4 %collective-permute-done.10 = f32[8,8]{0,1:T(8,128)S(1)} collective-permute-done((f32[8,8]{0,1:T(8,128)S(1)}, f32[8,8]{0,1:T(8,128)S(1)}, u32[]{:S(2)}, u32[]{:S(2)}) %collective-permute-start.10) | collective-permute-done | bytes 288 | tf_op jit(solution)/shard_map/ppermute | solution.py:113
  244.3 4.9 %collective-permute-start.11 = (f32[8,8]{0,1:T(8,128)S(1)}, f32[8,8]{0,1:T(8,128)S(1)}, u32[]{:S(2)}, u32[]{:S(2)}) collective-permute-start(f32[8,8]{0,1:T(8,128)S(1)} %add.86), channel_id=1, source_target_pairs={{0,32},{8,40},{16,48},{24,56},{32,0},{40,8},{48,16},{56,24},{64,96... | collective-permute-start | bytes 776 | tf_op jit(solution)/shard_map/ppermute | solution.py:113
  249.2 4.5 %collective-permute-done.11 = f32[8,8]{0,1:T(8,128)S(1)} collective-permute-done((f32[8,8]{0,1:T(8,128)S(1)}, f32[8,8]{0,1:T(8,128)S(1)}, u32[]{:S(2)}, u32[]{:S(2)}) %collective-permute-start.11) | collective-permute-done | bytes 288 | tf_op jit(solution)/shard_map/ppermute | solution.py:113
  253.7 8.5 %collective-permute-start.12 = (f32[8,8]{0,1:T(8,128)S(1)}, f32[8,8]{0,1:T(8,128)S(1)}, u32[]{:S(2)}, u32[]{:S(2)}) collective-permute-start(f32[8,8]{0,1:T(8,128)S(1)} %add.87), channel_id=1, source_target_pairs={{0,64},{8,72},{16,80},{24,88},{32,96},{40,104},{48,112},{56,120},{... | collective-permute-start | bytes 776 | tf_op jit(solution)/shard_map/ppermute | solution.py:113
  262.2 5.7 %collective-permute-done.12 = f32[8,8]{0,1:T(8,128)S(1)} collective-permute-done((f32[8,8]{0,1:T(8,128)S(1)}, f32[8,8]{0,1:T(8,128)S(1)}, u32[]{:S(2)}, u32[]{:S(2)}) %collective-permute-start.12) | collective-permute-done | bytes 288 | tf_op jit(solution)/shard_map/ppermute | solution.py:113
  270.4 3.0 %collective-permute-done.13 = f32[8,8]{0,1:T(8,128)S(1)} collective-permute-done((f32[8,8]{0,1:T(8,128)S(1)}, f32[8,8]{0,1:T(8,128)S(1)}, u32[]{:S(2)}, u32[]{:S(2)}) %collective-permute-start.13) | collective-permute-done | bytes 288 | tf_op jit(solution)/shard_map/ppermute | solution.py:113
  275.7 4.1 %collective-permute-done.14 = f32[8,8]{0,1:T(8,128)S(1)} collective-permute-done((f32[8,8]{0,1:T(8,128)S(1)}, f32[8,8]{0,1:T(8,128)S(1)}, u32[]{:S(2)}, u32[]{:S(2)}) %collective-permute-start.14) | collective-permute-done | bytes 288 | tf_op jit(solution)/shard_map/ppermute | solution.py:113
  282.9 6.4 %collective-permute-done.15 = f32[8,8]{0,1:T(8,128)S(1)} collective-permute-done((f32[8,8]{0,1:T(8,128)S(1)}, f32[8,8]{0,1:T(8,128)S(1)}, u32[]{:S(2)}, u32[]{:S(2)}) %collective-permute-start.15) | collective-permute-done | bytes 288 | tf_op jit(solution)/shard_map/ppermute | solution.py:113
  (50 shorter events, 33.2 us)
Async XLA Ops:
  7.2 78.4 %copy-start = (bf16[1,192,4096]{2,1,0:T(8,128)(2,1)S(1)}, bf16[1,192,4096]{2,1,0:T(8,128)(2,1)}, u32[]{:S(2)}) copy-start(bf16[1,192,4096]{2,1,0:T(8,128)(2,1)} %param.10) | copy-start | bytes 4718596
  7.2 177.6 %reduce-scatter.2.cloned.1.call-start = ((), (), s32[]{:S(2)}) async-start(), calls=%async_computation.2 | async-start | bytes 2228224 | tf_op jit(solution)/shard_map/reduce_scatter | solution.py:144
  51.2 11.1 %collective-permute-start = (bf16[512,256]{1,0:T(8,128)(2,1)S(1)}, bf16[512,256]{1,0:T(8,128)(2,1)S(1)}, u32[]{:S(2)}, u32[]{:S(2)}) collective-permute-start(bf16[512,256]{1,0:T(8,128)(2,1)S(1)} %all_gather.3), channel_id=1, source_target_pairs={{0,2},{2,0},{4,6},{6,4},{1,3},{3,1},{5,7},{7,5},{8,10},{10,8},{12,... | collective-permute-start | bytes 786440 | tf_op jit(solution)/shard_map/ppermute | solution.py:102
  62.4 12.7 %collective-permute-start.1 = (bf16[1024,256]{1,0:T(8,128)(2,1)S(1)}, bf16[1024,256]{1,0:T(8,128)(2,1)}, u32[]{:S(2)}, u32[]{:S(2)}) collective-permute-start(bf16[1024,256]{1,0:T(8,128)(2,1)S(1)} %pad_maximum_fusion.3), channel_id=1, source_target_pairs={{0,4},{2,6},{4,0},{6,2},{1,5},{3,7},{5,1},{7,3},{8,12},{10,14},{12... | collective-permute-start | bytes 1572872 | tf_op jit(solution)/shard_map/ppermute | solution.py:102
  77.3 4.9 %collective-permute-start.2 = (bf16[2048,256]{1,0:T(8,128)(2,1)}, bf16[2048,256]{1,0:T(8,128)(2,1)}, u32[]{:S(2)}, u32[]{:S(2)}) collective-permute-start(bf16[2048,256]{1,0:T(8,128)(2,1)} %pad_maximum_fusion.2), channel_id=1, source_target_pairs={{0,1},{1,0},{2,3},{3,2},{4,5},{5,4},{6,7},{7,6},{8,9},{9,8},{10,11... | collective-permute-start | bytes 3145736 | tf_op jit(solution)/shard_map/ppermute | solution.py:102
  84.0 2.0 copy-start.1
  106.1 6.1 %collective-permute-start.3 = (f32[2048,256]{1,0:T(8,128)S(1)}, f32[2048,256]{1,0:T(8,128)S(1)}, u32[]{:S(2)}, u32[]{:S(2)}) collective-permute-start(f32[2048,256]{1,0:T(8,128)S(1)} %bitcast.52), channel_id=1, source_target_pairs={{0,1},{1,0},{2,3},{3,2},{4,5},{5,4},{6,7},{7,6},{8,9},{9,8},{10,11... | collective-permute-start | bytes 6291464 | tf_op jit(solution)/shard_map/ppermute | solution.py:143
  185.6 7.7 %collective-permute-start.4 = (f32[64,256]{1,0:T(8,128)S(1)}, f32[64,256]{1,0:T(8,128)S(1)}, u32[]{:S(2)}, u32[]{:S(2)}) collective-permute-start(f32[64,256]{1,0:T(8,128)S(1)} %dynamic-slice_bitcast_fusion), channel_id=1, source_target_pairs={{0,4},{2,6},{4,0},{6,2},{1,5},{3,7},{5,1},{7,3},{8,12},{10,14},{12... | collective-permute-start | bytes 196616 | tf_op jit(solution)/shard_map/ppermute | solution.py:95
  194.2 5.8 %collective-permute-start.5 = (f32[32,256]{1,0:T(8,128)S(1)}, f32[32,256]{1,0:T(8,128)S(1)}, u32[]{:S(2)}, u32[]{:S(2)}) collective-permute-start(f32[32,256]{1,0:T(8,128)S(1)} %dynamic-slice_bitcast_fusion.1), channel_id=1, source_target_pairs={{0,2},{2,0},{4,6},{6,4},{1,3},{3,1},{5,7},{7,5},{8,10},{10,8},{12,... | collective-permute-start | bytes 98312 | tf_op jit(solution)/shard_map/ppermute | solution.py:95
  216.5 74.7 %copy-start.2 = (f32[8,32,32]{2,1,0:T(8,128)}, f32[8,32,32]{2,1,0:T(8,128)S(1)}, u32[]{:S(2)}) copy-start(f32[8,32,32]{2,1,0:T(8,128)S(1)} %reshape.91.pieces_ref) | copy-start | bytes 98308
  216.8 3.1 %collective-permute-start.6 = (f32[8,8]{0,1:T(8,128)S(1)}, f32[8,8]{0,1:T(8,128)S(1)}, u32[]{:S(2)}, u32[]{:S(2)}) collective-permute-start(f32[8,8]{0,1:T(8,128)S(1)} %convolution_bitcast_fusion.2), channel_id=1, source_target_pairs={{0,1},{1,0},{2,3},{3,2},{4,5},{5,4},{6,7},{7,6},{8,9},{9,8},{10,11... | collective-permute-start | bytes 776 | tf_op jit(solution)/shard_map/ppermute | solution.py:113
  219.9 5.5 %collective-permute-start.7 = (f32[8,8]{0,1:T(8,128)S(1)}, f32[8,8]{0,1:T(8,128)S(1)}, u32[]{:S(2)}, u32[]{:S(2)}) collective-permute-start(f32[8,8]{0,1:T(8,128)S(1)} %add.82), channel_id=1, source_target_pairs={{0,2},{2,0},{4,6},{6,4},{1,3},{3,1},{5,7},{7,5},{8,10},{10,8},{12,... | collective-permute-start | bytes 776 | tf_op jit(solution)/shard_map/ppermute | solution.py:113
  225.4 7.0 %collective-permute-start.8 = (f32[8,8]{0,1:T(8,128)S(1)}, f32[8,8]{0,1:T(8,128)S(1)}, u32[]{:S(2)}, u32[]{:S(2)}) collective-permute-start(f32[8,8]{0,1:T(8,128)S(1)} %add.83), channel_id=1, source_target_pairs={{0,4},{2,6},{4,0},{6,2},{1,5},{3,7},{5,1},{7,3},{8,12},{10,14},{12... | collective-permute-start | bytes 776 | tf_op jit(solution)/shard_map/ppermute | solution.py:113
  232.4 5.5 %collective-permute-start.9 = (f32[8,8]{0,1:T(8,128)S(1)}, f32[8,8]{0,1:T(8,128)S(1)}, u32[]{:S(2)}, u32[]{:S(2)}) collective-permute-start(f32[8,8]{0,1:T(8,128)S(1)} %add.84), channel_id=1, source_target_pairs={{0,8},{8,0},{16,24},{24,16},{32,40},{40,32},{48,56},{56,48},{64,72... | collective-permute-start | bytes 776 | tf_op jit(solution)/shard_map/ppermute | solution.py:113
  237.9 6.4 %collective-permute-start.10 = (f32[8,8]{0,1:T(8,128)S(1)}, f32[8,8]{0,1:T(8,128)S(1)}, u32[]{:S(2)}, u32[]{:S(2)}) collective-permute-start(f32[8,8]{0,1:T(8,128)S(1)} %add.85), channel_id=1, source_target_pairs={{0,16},{8,24},{16,0},{24,8},{32,48},{40,56},{48,32},{56,40},{64,80... | collective-permute-start | bytes 776 | tf_op jit(solution)/shard_map/ppermute | solution.py:113
  244.3 9.4 %collective-permute-start.11 = (f32[8,8]{0,1:T(8,128)S(1)}, f32[8,8]{0,1:T(8,128)S(1)}, u32[]{:S(2)}, u32[]{:S(2)}) collective-permute-start(f32[8,8]{0,1:T(8,128)S(1)} %add.86), channel_id=1, source_target_pairs={{0,32},{8,40},{16,48},{24,56},{32,0},{40,8},{48,16},{56,24},{64,96... | collective-permute-start | bytes 776 | tf_op jit(solution)/shard_map/ppermute | solution.py:113
  253.7 14.2 %collective-permute-start.12 = (f32[8,8]{0,1:T(8,128)S(1)}, f32[8,8]{0,1:T(8,128)S(1)}, u32[]{:S(2)}, u32[]{:S(2)}) collective-permute-start(f32[8,8]{0,1:T(8,128)S(1)} %add.87), channel_id=1, source_target_pairs={{0,64},{8,72},{16,80},{24,88},{32,96},{40,104},{48,112},{56,120},{... | collective-permute-start | bytes 776 | tf_op jit(solution)/shard_map/ppermute | solution.py:113
  267.9 5.5 %collective-permute-start.13 = (f32[8,8]{0,1:T(8,128)S(1)}, f32[8,8]{0,1:T(8,128)S(1)}, u32[]{:S(2)}, u32[]{:S(2)}) collective-permute-start(f32[8,8]{0,1:T(8,128)S(1)} %add.88), channel_id=1, source_target_pairs={{0,128},{128,0},{256,384},{384,256},{512,640},{640,512},{768,896},... | collective-permute-start | bytes 776 | tf_op jit(solution)/shard_map/ppermute | solution.py:113
  273.4 6.4 %collective-permute-start.14 = (f32[8,8]{0,1:T(8,128)S(1)}, f32[8,8]{0,1:T(8,128)S(1)}, u32[]{:S(2)}, u32[]{:S(2)}) collective-permute-start(f32[8,8]{0,1:T(8,128)S(1)} %add.89), channel_id=1, source_target_pairs={{0,256},{128,384},{256,0},{384,128},{512,768},{640,896},{768,512},... | collective-permute-start | bytes 776 | tf_op jit(solution)/shard_map/ppermute | solution.py:113
  279.8 9.4 %collective-permute-start.15 = (f32[8,8]{0,1:T(8,128)S(1)}, f32[8,8]{0,1:T(8,128)S(1)}, u32[]{:S(2)}, u32[]{:S(2)}) collective-permute-start(f32[8,8]{0,1:T(8,128)S(1)} %add.90), channel_id=1, source_target_pairs={{0,512},{128,640},{256,768},{384,896},{512,0},{640,128},{768,256},... | collective-permute-start | bytes 776 | tf_op jit(solution)/shard_map/ppermute | solution.py:113
Sparse Core Ops, SparseCore 0:
  114.0 70.7 reduce-scatter.1

commit v4 on v3

--- a/solution.py
+++ b/solution.py
@@ -149,9 +149,12 @@
     blocks = grad_rows.reshape(rows, tasks, width // tasks).transpose(1, 0, 2)
     pieces = lax.all_to_all(blocks, "task", 0, 0, tiled=True)
     partial_gram = jnp.einsum("sij,tij->st", pieces, pieces, precision=lax.Precision.HIGHEST)
-    gram_matrix = partial_gram
-    for axis in ALL_AXES:
-        gram_matrix = butterfly_sum(gram_matrix, axis)
+    gram_matrix = butterfly_sum(partial_gram, "core")
+    for axis in ("x", "z", "task"):
+        gathered = lax.all_gather(gram_matrix, axis, axis=0, tiled=False)
+        gram_matrix = gathered[0]
+        for position in range(1, gathered.shape[0]):
+            gram_matrix = gram_matrix + gathered[position]
     return tail(gram_matrix, pieces, moment_one, moment_two)
 
 

time: 302 us -> 296 us (0.980)
  blocking collectives: 58.9 us -> 123 us
  waiting for transfers between devices: 141 us -> 104 us
  starting transfers between devices: 49.8 us -> 17.6 us
    all_gather x0 -> x3, blocking collectives: none -> 64 us  [body(): gathered = lax.all_gather(gram_matrix, axis, axis=0, tiled=False)]
    ppermute x10 -> x1, waiting for transfers between devices: 37.8 us -> 0.49 us  [butterfly_sum(): value = value + lax.ppermute(value, axis, pairs)]
    ppermute x10 -> x1, starting transfers between devices: 33.9 us -> 1.95 us  [butterfly_sum(): value = value + lax.ppermute(value, axis, pairs)]
  transfers between devices with their start and end apart: 17 -> 8, of which waited for: 17 -> 8; matrix products, arithmetic and copies ran while one was open for 0% -> 0% of each run, Pallas kernels for 0% -> 0%
where the time goes in v4:
time: 296 us; the launch traced here: 295 us
  blocking collectives  123 us (42%)
  waiting for transfers between devices  104 us (35%)
  starting transfers between devices  17.6 us (6%)
  between operations  14.2 us (5%)
  other arithmetic  13.4 us (5%)
  local copies, waits for them, and re-layouts  13.1 us (4%)
  matrix products  7.58 us (3%)
    reduce_scatter x1, waiting for transfers between devices, body(): lax.psum_scatter(grad_rows, 'z', scatter_dimension=0, tiled=True)  71 us
    all_gather x3, blocking collectives, body(): gathered = lax.all_gather(gram_matrix, axis, axis=0, tiled=False)  64 us
    all_gather x1, blocking collectives, body(): piece = lax.all_gather(adapter, 'z', axis=0, tiled=True)  44 us
    ppermute x3, waiting for transfers between devices, double(): other = lax.ppermute(value, axis, pairs)  21.3 us
    all_to_all x1, blocking collectives, body(): pieces = lax.all_to_all(blocks, 'task', 0, 0, tiled=True)  14.7 us
    ppermute x3, starting transfers between devices, double(): other = lax.ppermute(value, axis, pairs)  7.29 us
    ppermute x2, waiting for transfers between devices, halve(): return mine + lax.ppermute(other, axis, pairs)  7.16 us
    ppermute x2, starting transfers between devices, halve(): return mine + lax.ppermute(other, axis, pairs)  6.29 us
  transfers between devices with their start and end apart: 8, of which 8 were waited for; matrix products, arithmetic and copies ran while one was open for 0% of the time, Pallas kernels for 0%

profile of v4, /device:TPU:6, one launch (start us, length us, event | category | flops | bytes accessed | tf_op | source)
XLA Modules:
  0.0 295.1 jit_solution(4296334660687157163)
XLA Ops:
  7.2 44.0 %all_gather.17 = bf16[512,256]{1,0:T(8,128)(2,1)S(1)} all-gather(bf16[32,256]{1,0:T(8,128)(2,1)} %param.11), channel_id=1, replica_groups=mesh['task'=8,'z'=16,'x'=4,'core'=2] {'z'}, dimensions={0}, use_global_device_ids=true | all-gather | bytes 278528 | tf_op jit(solution)/shard_map/all_gather | solution.py:122
  51.2 2.7 collective-permute-start
  54.0 8.3 %collective-permute-done = bf16[512,256]{1,0:T(8,128)(2,1)S(1)} collective-permute-done((bf16[512,256]{1,0:T(8,128)(2,1)S(1)}, bf16[512,256]{1,0:T(8,128)(2,1)S(1)}, u32[]{:S(2)}, u32[]{:S(2)}) %collective-permute-start) | collective-permute-done | bytes 262176 | tf_op jit(solution)/shard_map/ppermute | solution.py:102
  62.4 2.7 collective-permute-start.1
  65.0 10.0 %collective-permute-done.1 = bf16[1024,256]{1,0:T(8,128)(2,1)} collective-permute-done((bf16[1024,256]{1,0:T(8,128)(2,1)S(1)}, bf16[1024,256]{1,0:T(8,128)(2,1)}, u32[]{:S(2)}, u32[]{:S(2)}) %collective-permute-start.1) | collective-permute-done | bytes 524320 | tf_op jit(solution)/shard_map/ppermute | solution.py:102
  75.0 1.2 broadcast_select_fusion.3
  76.3 1.0 pad_maximum_fusion.2
  77.3 1.9 collective-permute-start.2
  79.2 3.0 %collective-permute-done.2 = bf16[2048,256]{1,0:T(8,128)(2,1)} collective-permute-done((bf16[2048,256]{1,0:T(8,128)(2,1)}, bf16[2048,256]{1,0:T(8,128)(2,1)}, u32[]{:S(2)}, u32[]{:S(2)}) %collective-permute-start.2) | collective-permute-done | bytes 1048608 | tf_op jit(solution)/shard_map/ppermute | solution.py:102
  82.2 1.6 broadcast_select_fusion.1
  84.0 1.6 copy.22
  86.0 3.6 %convolution_bitcast_fusion = f32[4096,128]{0,1:T(8,128)} fusion(bf16[1,192,4096]{2,1,0:T(8,128)(2,1)S(1)} %copy-done, bf16[1,192,4096]{2,1,0:T(8,128)(2,1)S(1)} %copy-done.1, bf16[4096,256]{1,0:T(8,128)(2,1)} %bitcast.52), kind=kOutput, calls=%fused_computation | convolution fusion | flops 402677760 | bytes 6291456 | tf_op jit(solution)/shard_map/dot_general | solution.py:134
  89.6 3.6 %convolution_bitcast_fusion.1 = f32[4096,128]{0,1:T(8,128)} fusion(bf16[1,192,4096]{2,1,0:T(8,128)(2,1)S(1)} %copy-done.1, bf16[1,192,4096]{2,1,0:T(8,128)(2,1)S(1)} %copy-done, bf16[4096,256]{1,0:T(8,128)(2,1)} %bitcast.53), kind=kOutput, calls=%fused_computation.1 | convolution fusion | flops 402677760 | bytes 6291456 | tf_op jit(solution)/shard_map/dot_general | solution.py:131
  93.2 4.6 %pad_maximum_fusion = f32[4096,256]{0,1:T(8,128)} fusion(f32[4096,128]{0,1:T(8,128)} %convolution_bitcast_fusion, f32[4096,128]{0,1:T(8,128)} %convolution_bitcast_fusion.1), kind=kLoop, calls=%fused_computation.2 | loop fusion | flops 1048576 | bytes 8388608 | tf_op jit(solution)/shard_map/concatenate | solution.py:137
  97.8 5.6 %copy.23 = f32[4096,256]{1,0:T(8,128)} copy(f32[4096,256]{0,1:T(8,128)} %pad_maximum_fusion) | data formatting | bytes 8388608 | tf_op jit(solution)/shard_map/concatenate | solution.py:137
  103.4 2.5 constant_dynamic-slice_fusion.1
  106.0 2.0 collective-permute-start.3
  108.0 4.0 %collective-permute-done.3 = f32[2048,256]{1,0:T(8,128)S(1)} collective-permute-done((f32[2048,256]{1,0:T(8,128)S(1)}, f32[2048,256]{1,0:T(8,128)S(1)}, u32[]{:S(2)}, u32[]{:S(2)}) %collective-permute-start.3) | collective-permute-done | bytes 2097184 | tf_op jit(solution)/shard_map/ppermute | solution.py:143
  112.0 1.8 bitcast_add_fusion
  113.8 71.0 %reduce-scatter.2.cloned.1.call-done = f32[128,256]{1,0:T(8,128)} async-done(((f32[2048,256]{1,0:T(8,128)}), f32[128,256]{1,0:T(8,128)}) %reduce-scatter.2.cloned.1.call-update) | async-done | bytes 131088 | tf_op jit(solution)/shard_map/reduce_scatter | solution.py:144
  184.9 0.8 dynamic-slice_bitcast_fusion
  185.7 3.4 %collective-permute-start.4 = (f32[64,256]{1,0:T(8,128)S(1)}, f32[64,256]{1,0:T(8,128)S(1)}, u32[]{:S(2)}, u32[]{:S(2)}) collective-permute-start(f32[64,256]{1,0:T(8,128)S(1)} %dynamic-slice_bitcast_fusion), channel_id=1, source_target_pairs={{0,4},{2,6},{4,0},{6,2},{1,5},{3,7},{5,1},{7,3},{8,12},{10,14},{12... | collective-permute-start | bytes 196616 | tf_op jit(solution)/shard_map/ppermute | solution.py:95
  189.1 4.2 %collective-permute-done.4 = f32[64,256]{1,0:T(8,128)S(1)} collective-permute-done((f32[64,256]{1,0:T(8,128)S(1)}, f32[64,256]{1,0:T(8,128)S(1)}, u32[]{:S(2)}, u32[]{:S(2)}) %collective-permute-start.4) | collective-permute-done | bytes 65568 | tf_op jit(solution)/shard_map/ppermute | solution.py:95
  193.4 0.8 bitcast_add_fusion.1
  194.2 2.9 collective-permute-start.5
  197.1 2.9 collective-permute-done.5
  200.3 14.7 %all_to_all.5 = f32[8,1,1024]{2,1,0:T(1,128)S(1)} all-to-all(f32[8,1,1024]{2,1,0:T(1,128)S(1)} %reshape.108), channel_id=1, replica_groups=mesh['task'=8,'z'=16,'x'=4,'core'=2] {'task'}, dimensions={0} | all-to-all | bytes 65536 | tf_op jit(solution)/shard_map/all_to_all | solution.py:150
  216.7 1.9 collective-permute-start.6
  219.8 12.0 %all-gather = f32[32,8]{1,0:T(8,128)S(1)} all-gather(f32[8,8]{1,0:T(8,128)S(1)} %add.154), channel_id=2, replica_groups=mesh['task'=8,'z'=16,'x'=4,'core'=2] {'x'}, dimensions={0}, use_global_device_ids=true | all-gather | bytes 1280 | tf_op jit(solution)/shard_map/all_gather | solution.py:154
  231.8 27.3 %all_gather.20 = f32[16,8,8]{2,1,0:T(8,128)S(1)} all-gather(f32[1,8,8]{2,1,0:T(8,128)S(1)} %fusion.23), channel_id=1, replica_groups=mesh['task'=8,'z'=16,'x'=4,'core'=2] {'z'}, dimensions={0}, use_global_device_ids=true | all-gather | bytes 4352 | tf_op jit(solution)/shard_map/all_gather | solution.py:154
  259.2 24.7 %all_gather.21 = f32[8,8,8]{2,1,0:T(8,128)S(1)} all-gather(f32[1,8,8]{2,1,0:T(8,128)S(1)} %slice_add_fusion.7), channel_id=1, replica_groups=mesh['task'=8,'z'=16,'x'=4,'core'=2] {'task'}, dimensions={0}, use_global_device_ids=true | all-gather | bytes 2304 | tf_op jit(solution)/shard_map/all_gather | solution.py:154
  285.8 2.4 shard_map.76
  (29 shorter events, 5.7 us)
Async XLA Ops:
  7.2 78.4 %copy-start = (bf16[1,192,4096]{2,1,0:T(8,128)(2,1)S(1)}, bf16[1,192,4096]{2,1,0:T(8,128)(2,1)}, u32[]{:S(2)}) copy-start(bf16[1,192,4096]{2,1,0:T(8,128)(2,1)} %param.10) | copy-start | bytes 4718596
  7.2 177.7 %reduce-scatter.2.cloned.1.call-start = ((), (), s32[]{:S(2)}) async-start(), calls=%async_computation.2 | async-start | bytes 2228224 | tf_op jit(solution)/shard_map/reduce_scatter | solution.py:144
  51.2 11.1 %collective-permute-start = (bf16[512,256]{1,0:T(8,128)(2,1)S(1)}, bf16[512,256]{1,0:T(8,128)(2,1)S(1)}, u32[]{:S(2)}, u32[]{:S(2)}) collective-permute-start(bf16[512,256]{1,0:T(8,128)(2,1)S(1)} %all_gather.17), channel_id=1, source_target_pairs={{0,2},{2,0},{4,6},{6,4},{1,3},{3,1},{5,7},{7,5},{8,10},{10,8},{12,... | collective-permute-start | bytes 786440 | tf_op jit(solution)/shard_map/ppermute | solution.py:102
  62.4 12.7 %collective-permute-start.1 = (bf16[1024,256]{1,0:T(8,128)(2,1)S(1)}, bf16[1024,256]{1,0:T(8,128)(2,1)}, u32[]{:S(2)}, u32[]{:S(2)}) collective-permute-start(bf16[1024,256]{1,0:T(8,128)(2,1)S(1)} %pad_maximum_fusion.3), channel_id=1, source_target_pairs={{0,4},{2,6},{4,0},{6,2},{1,5},{3,7},{5,1},{7,3},{8,12},{10,14},{12... | collective-permute-start | bytes 1572872 | tf_op jit(solution)/shard_map/ppermute | solution.py:102
  77.3 4.9 %collective-permute-start.2 = (bf16[2048,256]{1,0:T(8,128)(2,1)}, bf16[2048,256]{1,0:T(8,128)(2,1)}, u32[]{:S(2)}, u32[]{:S(2)}) collective-permute-start(bf16[2048,256]{1,0:T(8,128)(2,1)} %pad_maximum_fusion.2), channel_id=1, source_target_pairs={{0,1},{1,0},{2,3},{3,2},{4,5},{5,4},{6,7},{7,6},{8,9},{9,8},{10,11... | collective-permute-start | bytes 3145736 | tf_op jit(solution)/shard_map/ppermute | solution.py:102
  84.0 2.0 copy-start.1
  106.0 6.1 %collective-permute-start.3 = (f32[2048,256]{1,0:T(8,128)S(1)}, f32[2048,256]{1,0:T(8,128)S(1)}, u32[]{:S(2)}, u32[]{:S(2)}) collective-permute-start(f32[2048,256]{1,0:T(8,128)S(1)} %bitcast.54), channel_id=1, source_target_pairs={{0,1},{1,0},{2,3},{3,2},{4,5},{5,4},{6,7},{7,6},{8,9},{9,8},{10,11... | collective-permute-start | bytes 6291464 | tf_op jit(solution)/shard_map/ppermute | solution.py:143
  185.7 7.7 %collective-permute-start.4 = (f32[64,256]{1,0:T(8,128)S(1)}, f32[64,256]{1,0:T(8,128)S(1)}, u32[]{:S(2)}, u32[]{:S(2)}) collective-permute-start(f32[64,256]{1,0:T(8,128)S(1)} %dynamic-slice_bitcast_fusion), channel_id=1, source_target_pairs={{0,4},{2,6},{4,0},{6,2},{1,5},{3,7},{5,1},{7,3},{8,12},{10,14},{12... | collective-permute-start | bytes 196616 | tf_op jit(solution)/shard_map/ppermute | solution.py:95
  194.2 5.8 %collective-permute-start.5 = (f32[32,256]{1,0:T(8,128)S(1)}, f32[32,256]{1,0:T(8,128)S(1)}, u32[]{:S(2)}, u32[]{:S(2)}) collective-permute-start(f32[32,256]{1,0:T(8,128)S(1)} %dynamic-slice_bitcast_fusion.1), channel_id=1, source_target_pairs={{0,2},{2,0},{4,6},{6,4},{1,3},{3,1},{5,7},{7,5},{8,10},{10,8},{12,... | collective-permute-start | bytes 98312 | tf_op jit(solution)/shard_map/ppermute | solution.py:95
  216.3 69.4 %copy-start.2 = (f32[8,32,32]{2,1,0:T(8,128)}, f32[8,32,32]{2,1,0:T(8,128)S(1)}, u32[]{:S(2)}) copy-start(f32[8,32,32]{2,1,0:T(8,128)S(1)} %reshape.109.pieces_ref) | copy-start | bytes 98308
  216.7 3.1 %collective-permute-start.6 = (f32[8,8]{1,0:T(8,128)S(1)}, f32[8,8]{1,0:T(8,128)S(1)}, u32[]{:S(2)}, u32[]{:S(2)}) collective-permute-start(f32[8,8]{1,0:T(8,128)S(1)} %convolution_bitcast_fusion.2), channel_id=1, source_target_pairs={{0,1},{1,0},{2,3},{3,2},{4,5},{5,4},{6,7},{7,6},{8,9},{9,8},{10,11... | collective-permute-start | bytes 776 | tf_op jit(solution)/shard_map/ppermute | solution.py:113
Sparse Core Ops, SparseCore 0:
  114.0 70.8 reduce-scatter.1

commit v5 on v4

--- a/solution.py
+++ b/solution.py
@@ -142,19 +142,23 @@
     other = lax.dynamic_index_in_dim(by_core, 1 - me, 1, keepdims=False).reshape(-1, full[1])
     grad_rows = mine + lax.ppermute(other, "core", [(0, 1), (1, 0)])
     grad_rows = lax.psum_scatter(grad_rows, "z", scatter_dimension=0, tiled=True)
-    grad_rows = halve(grad_rows, "x", 1)
-    grad_rows = halve(grad_rows, "x", 0)
     tasks = lax.axis_size("task")
     rows, width = grad_rows.shape
-    blocks = grad_rows.reshape(rows, tasks, width // tasks).transpose(1, 0, 2)
-    pieces = lax.all_to_all(blocks, "task", 0, 0, tiled=True)
+    tiles = grad_rows.reshape(xs, rows // xs, tasks, width // tasks).transpose(0, 2, 1, 3)
+    tiles = tiles.reshape(xs * tasks, rows // xs, width // tasks)
+    tiles = lax.all_to_all(tiles, ("x", "task"), 0, 0, tiled=True)
+    tiles = tiles.reshape(xs, tasks, rows // xs, width // tasks)
+    pieces = tiles[0]
+    for position in range(1, xs):
+        pieces = pieces + tiles[position]
     partial_gram = jnp.einsum("sij,tij->st", pieces, pieces, precision=lax.Precision.HIGHEST)
     gram_matrix = butterfly_sum(partial_gram, "core")
-    for axis in ("x", "z", "task"):
+    for axis in ("x", "z"):
         gathered = lax.all_gather(gram_matrix, axis, axis=0, tiled=False)
         gram_matrix = gathered[0]
         for position in range(1, gathered.shape[0]):
             gram_matrix = gram_matrix + gathered[position]
+    gram_matrix = butterfly_sum(gram_matrix, "task")
     return tail(gram_matrix, pieces, moment_one, moment_two)
 
 

time: 296 us -> 284 us (0.959)
  blocking collectives: 123 us -> 102 us
  waiting for transfers between devices: 104 us -> 109 us
  starting transfers between devices: 17.6 us -> 20.8 us
    all_gather x3 -> x2, blocking collectives: 64 us -> 39.5 us  [body(): gathered = lax.all_gather(gram_matrix, axis, axis=0, tiled=False)]
    ppermute x1 -> x4, waiting for transfers between devices: 0.49 us -> 12.3 us  [butterfly_sum(): value = value + lax.ppermute(value, axis, pairs)]
    ppermute x1 -> x4, starting transfers between devices: 1.95 us -> 11.4 us  [butterfly_sum(): value = value + lax.ppermute(value, axis, pairs)]
    ppermute x2 -> x0, waiting for transfers between devices: 7.16 us -> none  [halve(): return mine + lax.ppermute(other, axis, pairs)]
    ppermute x2 -> x0, starting transfers between devices: 6.29 us -> none  [halve(): return mine + lax.ppermute(other, axis, pairs)]
    all_to_all x1, blocking collectives: 14.7 us -> 18.1 us  [body(): tiles = lax.all_to_all(tiles, ('x', 'task'), 0, 0, tiled=True)]
  transfers between devices with their start and end apart: 8 -> 9, of which waited for: 8 -> 9; matrix products, arithmetic and copies ran while one was open for 0% -> 0% of each run, Pallas kernels for 0% -> 0%
where the time goes in v5:
time: 284 us; the launch traced here: 282 us
  waiting for transfers between devices  109 us (38%)
  blocking collectives  102 us (36%)
  starting transfers between devices  20.8 us (7%)
  between operations  14.2 us (5%)
  local copies, waits for them, and re-layouts  13.6 us (5%)
  other arithmetic  12.8 us (5%)
  matrix products  7.53 us (3%)
    reduce_scatter x1, waiting for transfers between devices, body(): lax.psum_scatter(grad_rows, 'z', scatter_dimension=0, tiled=True)  71.1 us
    all_gather x1, blocking collectives, body(): piece = lax.all_gather(adapter, 'z', axis=0, tiled=True)  44 us
    all_gather x2, blocking collectives, body(): gathered = lax.all_gather(gram_matrix, axis, axis=0, tiled=False)  39.5 us
    ppermute x3, waiting for transfers between devices, double(): other = lax.ppermute(value, axis, pairs)  21.3 us
    all_to_all x1, blocking collectives, body(): tiles = lax.all_to_all(tiles, ('x', 'task'), 0, 0, tiled=True)  18.1 us
    ppermute x4, waiting for transfers between devices, butterfly_sum(): value = value + lax.ppermute(value, axis, pairs)  12.3 us
    ppermute x4, starting transfers between devices, butterfly_sum(): value = value + lax.ppermute(value, axis, pairs)  11.4 us
    ppermute x3, starting transfers between devices, double(): other = lax.ppermute(value, axis, pairs)  7.29 us
  transfers between devices with their start and end apart: 9, of which 9 were waited for; matrix products, arithmetic and copies ran while one was open for 0% of the time, Pallas kernels for 0%

profile of v5, /device:TPU:6, one launch (start us, length us, event | category | flops | bytes accessed | tf_op | source)
XLA Modules:
  0.0 281.6 jit_solution(2881729942165409771)
XLA Ops:
  7.2 44.0 %all_gather.13 = bf16[512,256]{1,0:T(8,128)(2,1)S(1)} all-gather(bf16[32,256]{1,0:T(8,128)(2,1)} %param.11), channel_id=1, replica_groups=mesh['task'=8,'z'=16,'x'=4,'core'=2] {'z'}, dimensions={0}, use_global_device_ids=true | all-gather | bytes 278528 | tf_op jit(solution)/shard_map/all_gather | solution.py:122
  51.2 2.7 collective-permute-start
  54.0 8.3 %collective-permute-done = bf16[512,256]{1,0:T(8,128)(2,1)S(1)} collective-permute-done((bf16[512,256]{1,0:T(8,128)(2,1)S(1)}, bf16[512,256]{1,0:T(8,128)(2,1)S(1)}, u32[]{:S(2)}, u32[]{:S(2)}) %collective-permute-start) | collective-permute-done | bytes 262176 | tf_op jit(solution)/shard_map/ppermute | solution.py:102
  62.4 2.7 collective-permute-start.1
  65.0 10.0 %collective-permute-done.1 = bf16[1024,256]{1,0:T(8,128)(2,1)} collective-permute-done((bf16[1024,256]{1,0:T(8,128)(2,1)S(1)}, bf16[1024,256]{1,0:T(8,128)(2,1)}, u32[]{:S(2)}, u32[]{:S(2)}) %collective-permute-start.1) | collective-permute-done | bytes 524320 | tf_op jit(solution)/shard_map/ppermute | solution.py:102
  75.0 1.2 broadcast_select_fusion.3
  77.3 1.9 collective-permute-start.2
  79.2 3.0 %collective-permute-done.2 = bf16[2048,256]{1,0:T(8,128)(2,1)} collective-permute-done((bf16[2048,256]{1,0:T(8,128)(2,1)}, bf16[2048,256]{1,0:T(8,128)(2,1)}, u32[]{:S(2)}, u32[]{:S(2)}) %collective-permute-start.2) | collective-permute-done | bytes 1048608 | tf_op jit(solution)/shard_map/ppermute | solution.py:102
  82.2 1.6 broadcast_select_fusion.1
  84.0 1.5 copy.28
  86.0 3.6 %convolution_bitcast_fusion = f32[4096,128]{0,1:T(8,128)} fusion(bf16[1,192,4096]{2,1,0:T(8,128)(2,1)S(1)} %copy-done, bf16[1,192,4096]{2,1,0:T(8,128)(2,1)S(1)} %copy-done.1, bf16[4096,256]{1,0:T(8,128)(2,1)} %bitcast.41), kind=kOutput, calls=%fused_computation | convolution fusion | flops 402677760 | bytes 6291456 | tf_op jit(solution)/shard_map/dot_general | solution.py:134
  89.5 3.6 %convolution_bitcast_fusion.1 = f32[4096,128]{0,1:T(8,128)} fusion(bf16[1,192,4096]{2,1,0:T(8,128)(2,1)S(1)} %copy-done.1, bf16[1,192,4096]{2,1,0:T(8,128)(2,1)S(1)} %copy-done, bf16[4096,256]{1,0:T(8,128)(2,1)} %bitcast.42), kind=kOutput, calls=%fused_computation.1 | convolution fusion | flops 402677760 | bytes 6291456 | tf_op jit(solution)/shard_map/dot_general | solution.py:131
  93.1 4.6 %pad_maximum_fusion = f32[4096,256]{0,1:T(8,128)} fusion(f32[4096,128]{0,1:T(8,128)} %convolution_bitcast_fusion, f32[4096,128]{0,1:T(8,128)} %convolution_bitcast_fusion.1), kind=kLoop, calls=%fused_computation.2 | loop fusion | flops 1048576 | bytes 8388608 | tf_op jit(solution)/shard_map/concatenate | solution.py:137
  97.7 5.6 %copy.29 = f32[4096,256]{1,0:T(8,128)} copy(f32[4096,256]{0,1:T(8,128)} %pad_maximum_fusion) | data formatting | bytes 8388608 | tf_op jit(solution)/shard_map/concatenate | solution.py:137
  103.4 2.5 constant_dynamic-slice_fusion.1
  105.9 2.1 collective-permute-start.3
  108.0 3.9 %collective-permute-done.3 = f32[2048,256]{1,0:T(8,128)S(1)} collective-permute-done((f32[2048,256]{1,0:T(8,128)S(1)}, f32[2048,256]{1,0:T(8,128)S(1)}, u32[]{:S(2)}, u32[]{:S(2)}) %collective-permute-start.3) | collective-permute-done | bytes 2097184 | tf_op jit(solution)/shard_map/ppermute | solution.py:143
  112.0 1.8 bitcast_add_fusion
  113.8 71.1 %reduce-scatter.2.cloned.1.call-done = f32[128,256]{1,0:T(8,128)} async-done(((f32[2048,256]{1,0:T(8,128)}), f32[128,256]{1,0:T(8,128)}) %reduce-scatter.2.cloned.1.call-update) | async-done | bytes 131088 | tf_op jit(solution)/shard_map/reduce_scatter | solution.py:144
  184.9 1.1 reshape.98
  186.3 18.1 %all_to_all.5 = f32[32,1,1024]{2,1,0:T(1,128)S(1)} all-to-all(f32[32,1,1024]{2,1,0:T(1,128)S(1)} %reshape.120), channel_id=1, replica_groups=mesh['task'=8,'z'=16,'x'=4,'core'=2] {'x','task'}, dimensions={0} | all-to-all | bytes 262144 | tf_op jit(solution)/shard_map/all_to_all | solution.py:149
  206.5 1.9 collective-permute-start.4
  208.4 1.1 collective-permute-done.4
  209.6 12.0 %all-gather = f32[32,8]{1,0:T(8,128)S(1)} all-gather(f32[8,8]{1,0:T(8,128)S(1)} %add.115), channel_id=2, replica_groups=mesh['task'=8,'z'=16,'x'=4,'core'=2] {'x'}, dimensions={0}, use_global_device_ids=true | all-gather | bytes 1280 | tf_op jit(solution)/shard_map/all_gather | solution.py:157
  221.6 27.4 %all_gather.16 = f32[16,8,8]{2,1,0:T(8,128)S(1)} all-gather(f32[1,8,8]{2,1,0:T(8,128)S(1)} %fusion.22), channel_id=1, replica_groups=mesh['task'=8,'z'=16,'x'=4,'core'=2] {'z'}, dimensions={0}, use_global_device_ids=true | all-gather | bytes 4352 | tf_op jit(solution)/shard_map/all_gather | solution.py:157
  249.1 3.0 %collective-permute-start.5 = (f32[8,8]{0,1:T(8,128)S(1)}, f32[8,8]{0,1:T(8,128)S(1)}, u32[]{:S(2)}, u32[]{:S(2)}) collective-permute-start(f32[8,8]{0,1:T(8,128)S(1)} %copy.34), channel_id=1, source_target_pairs={{0,128},{128,0},{256,384},{384,256},{512,640},{640,512},{768,896},... | collective-permute-start | bytes 776 | tf_op jit(solution)/shard_map/ppermute | solution.py:113
  252.2 2.4 collective-permute-done.5
  254.6 3.2 %collective-permute-start.6 = (f32[8,8]{0,1:T(8,128)S(1)}, f32[8,8]{0,1:T(8,128)S(1)}, u32[]{:S(2)}, u32[]{:S(2)}) collective-permute-start(f32[8,8]{0,1:T(8,128)S(1)} %add.135), channel_id=1, source_target_pairs={{0,256},{128,384},{256,0},{384,128},{512,768},{640,896},{768,512},... | collective-permute-start | bytes 776 | tf_op jit(solution)/shard_map/ppermute | solution.py:113
  257.8 3.2 %collective-permute-done.6 = f32[8,8]{0,1:T(8,128)S(1)} collective-permute-done((f32[8,8]{0,1:T(8,128)S(1)}, f32[8,8]{0,1:T(8,128)S(1)}, u32[]{:S(2)}, u32[]{:S(2)}) %collective-permute-start.6) | collective-permute-done | bytes 288 | tf_op jit(solution)/shard_map/ppermute | solution.py:113
  261.0 3.2 %collective-permute-start.7 = (f32[8,8]{0,1:T(8,128)S(1)}, f32[8,8]{0,1:T(8,128)S(1)}, u32[]{:S(2)}, u32[]{:S(2)}) collective-permute-start(f32[8,8]{0,1:T(8,128)S(1)} %add.136), channel_id=1, source_target_pairs={{0,512},{128,640},{256,768},{384,896},{512,0},{640,128},{768,256},... | collective-permute-start | bytes 776 | tf_op jit(solution)/shard_map/ppermute | solution.py:113
  264.9 5.5 %collective-permute-done.7 = f32[8,8]{0,1:T(8,128)S(1)} collective-permute-done((f32[8,8]{0,1:T(8,128)S(1)}, f32[8,8]{0,1:T(8,128)S(1)}, u32[]{:S(2)}, u32[]{:S(2)}) %collective-permute-start.7) | collective-permute-done | bytes 288 | tf_op jit(solution)/shard_map/ppermute | solution.py:113
  272.3 2.4 shard_map.76
  (30 shorter events, 6.8 us)
Async XLA Ops:
  7.2 78.4 %copy-start = (bf16[1,192,4096]{2,1,0:T(8,128)(2,1)S(1)}, bf16[1,192,4096]{2,1,0:T(8,128)(2,1)}, u32[]{:S(2)}) copy-start(bf16[1,192,4096]{2,1,0:T(8,128)(2,1)} %param.10) | copy-start | bytes 4718596
  7.2 177.7 %reduce-scatter.2.cloned.1.call-start = ((), (), s32[]{:S(2)}) async-start(), calls=%async_computation.2 | async-start | bytes 2228224 | tf_op jit(solution)/shard_map/reduce_scatter | solution.py:144
  51.2 11.1 %collective-permute-start = (bf16[512,256]{1,0:T(8,128)(2,1)S(1)}, bf16[512,256]{1,0:T(8,128)(2,1)S(1)}, u32[]{:S(2)}, u32[]{:S(2)}) collective-permute-start(bf16[512,256]{1,0:T(8,128)(2,1)S(1)} %all_gather.13), channel_id=1, source_target_pairs={{0,2},{2,0},{4,6},{6,4},{1,3},{3,1},{5,7},{7,5},{8,10},{10,8},{12,... | collective-permute-start | bytes 786440 | tf_op jit(solution)/shard_map/ppermute | solution.py:102
  62.4 12.7 %collective-permute-start.1 = (bf16[1024,256]{1,0:T(8,128)(2,1)S(1)}, bf16[1024,256]{1,0:T(8,128)(2,1)}, u32[]{:S(2)}, u32[]{:S(2)}) collective-permute-start(bf16[1024,256]{1,0:T(8,128)(2,1)S(1)} %pad_maximum_fusion.3), channel_id=1, source_target_pairs={{0,4},{2,6},{4,0},{6,2},{1,5},{3,7},{5,1},{7,3},{8,12},{10,14},{12... | collective-permute-start | bytes 1572872 | tf_op jit(solution)/shard_map/ppermute | solution.py:102
  77.3 4.9 %collective-permute-start.2 = (bf16[2048,256]{1,0:T(8,128)(2,1)}, bf16[2048,256]{1,0:T(8,128)(2,1)}, u32[]{:S(2)}, u32[]{:S(2)}) collective-permute-start(bf16[2048,256]{1,0:T(8,128)(2,1)} %pad_maximum_fusion.2), channel_id=1, source_target_pairs={{0,1},{1,0},{2,3},{3,2},{4,5},{5,4},{6,7},{7,6},{8,9},{9,8},{10,11... | collective-permute-start | bytes 3145736 | tf_op jit(solution)/shard_map/ppermute | solution.py:102
  84.0 2.0 copy-start.1
  105.9 6.1 %collective-permute-start.3 = (f32[2048,256]{1,0:T(8,128)S(1)}, f32[2048,256]{1,0:T(8,128)S(1)}, u32[]{:S(2)}, u32[]{:S(2)}) collective-permute-start(f32[2048,256]{1,0:T(8,128)S(1)} %bitcast.43), channel_id=1, source_target_pairs={{0,1},{1,0},{2,3},{3,2},{4,5},{5,4},{6,7},{7,6},{8,9},{9,8},{10,11... | collective-permute-start | bytes 6291464 | tf_op jit(solution)/shard_map/ppermute | solution.py:143
  206.1 66.3 %copy-start.2 = (f32[8,32,32]{2,1,0:T(8,128)}, f32[8,32,32]{2,1,0:T(8,128)S(1)}, u32[]{:S(2)}) copy-start(f32[8,32,32]{2,1,0:T(8,128)S(1)} %slice_add_fusion.pieces_ref) | copy-start | bytes 98308
  206.5 3.1 %collective-permute-start.4 = (f32[8,8]{1,0:T(8,128)S(1)}, f32[8,8]{1,0:T(8,128)S(1)}, u32[]{:S(2)}, u32[]{:S(2)}) collective-permute-start(f32[8,8]{1,0:T(8,128)S(1)} %convolution_bitcast_fusion.2), channel_id=1, source_target_pairs={{0,1},{1,0},{2,3},{3,2},{4,5},{5,4},{6,7},{7,6},{8,9},{9,8},{10,11... | collective-permute-start | bytes 776 | tf_op jit(solution)/shard_map/ppermute | solution.py:113
  249.1 5.5 %collective-permute-start.5 = (f32[8,8]{0,1:T(8,128)S(1)}, f32[8,8]{0,1:T(8,128)S(1)}, u32[]{:S(2)}, u32[]{:S(2)}) collective-permute-start(f32[8,8]{0,1:T(8,128)S(1)} %copy.34), channel_id=1, source_target_pairs={{0,128},{128,0},{256,384},{384,256},{512,640},{640,512},{768,896},... | collective-permute-start | bytes 776 | tf_op jit(solution)/shard_map/ppermute | solution.py:113
  254.6 6.4 %collective-permute-start.6 = (f32[8,8]{0,1:T(8,128)S(1)}, f32[8,8]{0,1:T(8,128)S(1)}, u32[]{:S(2)}, u32[]{:S(2)}) collective-permute-start(f32[8,8]{0,1:T(8,128)S(1)} %add.135), channel_id=1, source_target_pairs={{0,256},{128,384},{256,0},{384,128},{512,768},{640,896},{768,512},... | collective-permute-start | bytes 776 | tf_op jit(solution)/shard_map/ppermute | solution.py:113
  261.0 9.4 %collective-permute-start.7 = (f32[8,8]{0,1:T(8,128)S(1)}, f32[8,8]{0,1:T(8,128)S(1)}, u32[]{:S(2)}, u32[]{:S(2)}) collective-permute-start(f32[8,8]{0,1:T(8,128)S(1)} %add.136), channel_id=1, source_target_pairs={{0,512},{128,640},{256,768},{384,896},{512,0},{640,128},{768,256},... | collective-permute-start | bytes 776 | tf_op jit(solution)/shard_map/ppermute | solution.py:113
Sparse Core Ops, SparseCore 0:
  113.9 70.9 reduce-scatter.1

commit v6 on v5

--- a/solution.py
+++ b/solution.py
@@ -119,13 +119,10 @@
     own_context = contexts[0]
     own_cotangent = cotangents[0]
     rank_width = adapter.shape[1] // 2
-    piece = lax.all_gather(adapter, "z", axis=0, tiled=True)
-    piece = double(piece, "x", 0)
-    piece = double(piece, "x", 1)
-    piece = double(piece, "core", 0)
     zs, xs, cs = (lax.axis_size(a) for a in FSDP)
-    blocks_in = piece.reshape(cs, xs, zs, -1, piece.shape[1])
-    piece = blocks_in.transpose(2, 1, 0, 3, 4).reshape(piece.shape)
+    fsdp = zs * xs * cs
+    piece = jnp.broadcast_to(adapter[None], (fsdp,) + adapter.shape)
+    piece = lax.all_to_all(piece, FSDP, 0, 0, tiled=True).reshape(-1, adapter.shape[1])
     low = jnp.dot(own_context, piece[:, :rank_width], preferred_element_type=jnp.float32).astype(jnp.bfloat16)
     back = jnp.dot(own_cotangent, piece[:, rank_width:], preferred_element_type=jnp.float32).astype(jnp.bfloat16)
     down_part = lax.dot_general(
@@ -152,13 +149,10 @@
     for position in range(1, xs):
         pieces = pieces + tiles[position]
     partial_gram = jnp.einsum("sij,tij->st", pieces, pieces, precision=lax.Precision.HIGHEST)
-    gram_matrix = butterfly_sum(partial_gram, "core")
-    for axis in ("x", "z"):
-        gathered = lax.all_gather(gram_matrix, axis, axis=0, tiled=False)
-        gram_matrix = gathered[0]
-        for position in range(1, gathered.shape[0]):
-            gram_matrix = gram_matrix + gathered[position]
-    gram_matrix = butterfly_sum(gram_matrix, "task")
+    devices = fsdp * tasks
+    gathered = jnp.broadcast_to(partial_gram[None], (devices,) + partial_gram.shape)
+    gathered = lax.all_to_all(gathered, ("task",) + FSDP, 0, 0, tiled=True)
+    gram_matrix = jnp.sum(gathered, axis=0)
     return tail(gram_matrix, pieces, moment_one, moment_two)
 
 

time: 284 us -> 480 us (1.69)
  waiting for transfers between devices: 109 us -> 359 us
  blocking collectives: 102 us -> 18.2 us
  starting transfers between devices: 20.8 us -> 49 us
    all_to_all x0 -> x2, waiting for transfers between devices: none -> 282 us  [the longest x1 186 us: body(): gathered = lax.all_to_all(gathered, ('task',) + FSDP, 0, 0, tiled=True)]
    all_gather x3 -> x0, blocking collectives: 83.4 us -> none  [the longest x1 44 us: body(): piece = lax.all_gather(adapter, 'z', axis=0, tiled=True)]
    all_to_all x0 -> x2, starting transfers between devices: none -> 46.4 us  [the longest x1 23.6 us: body(): lax.all_to_all(piece, FSDP, 0, 0, tiled=True).reshape(-1, adapter.shape[1])]
    ppermute x7 -> x0, waiting for transfers between devices: 33.6 us -> none  [the longest x3 21.3 us: double(): other = lax.ppermute(value, axis, pairs)]
    ppermute x7 -> x0, starting transfers between devices: 18.7 us -> none  [the longest x4 11.4 us: butterfly_sum(): value = value + lax.ppermute(value, axis, pairs)]
  transfers between devices with their start and end apart: 9 -> 4, of which waited for: 9 -> 4; matrix products, arithmetic and copies ran while one was open for 0% -> 0% of each run, Pallas kernels for 0% -> 0%
where the time goes in v6:
time: 480 us; the launch traced here: 479 us
  waiting for transfers between devices  359 us (75%)
  starting transfers between devices  49 us (10%)
  blocking collectives  18.2 us (4%)
  local copies, waits for them, and re-layouts  16.3 us (3%)
  between operations  14.1 us (3%)
  other arithmetic  12.6 us (3%)
  matrix products  7.56 us (2%)
    all_to_all x1, waiting for transfers between devices, body(): gathered = lax.all_to_all(gathered, ('task',) + FSDP, 0, 0, tiled=True)  186 us
    all_to_all x1, waiting for transfers between devices, body(): lax.all_to_all(piece, FSDP, 0, 0, tiled=True).reshape(-1, adapter.shape[1])  96.5 us
    reduce_scatter x1, waiting for transfers between devices, body(): lax.psum_scatter(grad_rows, 'z', scatter_dimension=0, tiled=True)  72.5 us
    all_to_all x1, starting transfers between devices, body(): lax.all_to_all(piece, FSDP, 0, 0, tiled=True).reshape(-1, adapter.shape[1])  23.6 us
    all_to_all x1, starting transfers between devices, body(): gathered = lax.all_to_all(gathered, ('task',) + FSDP, 0, 0, tiled=True)  22.8 us
    all_to_all x1, blocking collectives, body(): tiles = lax.all_to_all(tiles, ('x', 'task'), 0, 0, tiled=True)  18.2 us
  transfers between devices with their start and end apart: 4, of which 4 were waited for; matrix products, arithmetic and copies ran while one was open for 0% of the time, Pallas kernels for 0%

profile of v6, /device:TPU:6, one launch (start us, length us, event | category | flops | bytes accessed | tf_op | source)
XLA Modules:
  0.0 478.9 jit_solution(519787017838459205)
XLA Ops:
  7.2 2.4 broadcast_in_dim.4
  9.6 23.6 %all-to-all-start = ((bf16[128,32,256]{2,1,0:T(8,128)(2,1)}), bf16[128,32,256]{2,1,0:T(8,128)(2,1)}, u32[]{:S(2)}, u32[]{:S(2)}) async-start(bf16[128,32,256]{2,1,0:T(8,128)(2,1)} %broadcast_in_dim.4), calls=%async_computation | async-start | bytes 4194304 | tf_op jit(solution)/shard_map/all_to_all | solution.py:125
  33.3 96.5 %all-to-all-done = bf16[128,32,256]{2,1,0:T(8,128)(2,1)} async-done(((bf16[128,32,256]{2,1,0:T(8,128)(2,1)}), bf16[128,32,256]{2,1,0:T(8,128)(2,1)}, u32[]{:S(2)}, u32[]{:S(2)}) %all-to-all-start) | async-done | bytes 2097184 | tf_op jit(solution)/shard_map/all_to_all | solution.py:125
  129.8 3.6 convolution_bitcast_fusion
  133.4 3.6 convolution_bitcast_fusion.1
  137.0 4.6 pad_maximum_fusion
  141.6 5.6 %copy.30 = f32[4096,256]{1,0:T(8,128)} copy(f32[4096,256]{0,1:T(8,128)} %pad_maximum_fusion) | data formatting | bytes 8388608 | tf_op jit(solution)/shard_map/concatenate | solution.py:134
  147.2 2.5 constant_dynamic-slice_fusion.1
  149.8 2.5 collective-permute-start
  152.3 3.8 collective-permute-done
  156.1 1.8 bitcast_add_fusion
  157.9 72.5 %reduce-scatter.2.cloned.1.call-done = f32[128,256]{1,0:T(8,128)} async-done(((f32[2048,256]{1,0:T(8,128)}), f32[128,256]{1,0:T(8,128)}) %reduce-scatter.2.cloned.1.call-update) | async-done | bytes 131088 | tf_op jit(solution)/shard_map/reduce_scatter | solution.py:141
  230.4 1.1 reshape.92
  231.5 0.1 copy.31
  231.6 0.3 reshape.95
  231.8 18.2 %all_to_all.15 = f32[32,1,1024]{2,1,0:T(1,128)S(1)} all-to-all(f32[32,1,1024]{2,1,0:T(1,128)S(1)} %reshape.95), channel_id=1, replica_groups=mesh['task'=8,'z'=16,'x'=4,'core'=2] {'x','task'}, dimensions={0} | all-to-all | bytes 262144 | tf_op jit(solution)/shard_map/all_to_all | solution.py:146
  250.1 0.5 broadcast.61
  250.6 0.9 reduce.10
  251.5 0.2 reshape.96
  251.8 0.4 convolution_bitcast_fusion.2
  252.1 2.3 broadcast_in_dim.5
  254.4 22.8 %all-to-all-start.2 = ((f32[1024,8,8]{2,1,0:T(8,128)}), f32[1024,8,8]{2,1,0:T(8,128)}, u32[]{:S(2)}, u32[]{:S(2)}) async-start(f32[1024,8,8]{2,1,0:T(8,128)} %broadcast_in_dim.5), calls=%async_computation.3 | async-start | bytes 8388608 | tf_op jit(solution)/shard_map/all_to_all | solution.py:154
  277.2 0.6 compare_reduce_fusion
  277.8 185.9 %all-to-all-done.2 = f32[1024,8,8]{2,1,0:T(8,128)} async-done(((f32[1024,8,8]{2,1,0:T(8,128)}), f32[1024,8,8]{2,1,0:T(8,128)}, u32[]{:S(2)}, u32[]{:S(2)}) %all-to-all-start.2) | async-done | bytes 262176 | tf_op jit(solution)/shard_map/all_to_all | solution.py:154
  463.7 3.3 reduce_sum.9
  467.0 0.1 copy.35
  467.1 0.6 broadcast_select_fusion
  467.7 0.7 fusion.21
  468.4 0.1 copy.38
  468.5 0.6 scatter.6.clone.gram_ref
  469.0 0.6 scatter.9.gramt_ref
  469.6 2.4 shard_map.76
  (9 shorter events, 0.1 us)
Async XLA Ops:
  7.2 122.6 %copy-start = (bf16[1,192,4096]{2,1,0:T(8,128)(2,1)S(1)}, bf16[1,192,4096]{2,1,0:T(8,128)(2,1)}, u32[]{:S(2)}) copy-start(bf16[1,192,4096]{2,1,0:T(8,128)(2,1)} %param.10) | copy-start | bytes 4718596
  9.6 120.2 %copy-start.1 = (bf16[1,192,4096]{2,1,0:T(8,128)(2,1)S(1)}, bf16[1,192,4096]{2,1,0:T(8,128)(2,1)}, u32[]{:S(2)}) copy-start(bf16[1,192,4096]{2,1,0:T(8,128)(2,1)} %param.9) | copy-start | bytes 4718596
  9.6 120.2 %all-to-all-start = ((bf16[128,32,256]{2,1,0:T(8,128)(2,1)}), bf16[128,32,256]{2,1,0:T(8,128)(2,1)}, u32[]{:S(2)}, u32[]{:S(2)}) async-start(bf16[128,32,256]{2,1,0:T(8,128)(2,1)} %broadcast_in_dim.4), calls=%async_computation | async-start | bytes 4194304 | tf_op jit(solution)/shard_map/all_to_all | solution.py:125
  33.2 197.2 %reduce-scatter.2.cloned.1.call-start = ((), (), s32[]{:S(2)}) async-start(), calls=%async_computation.4 | async-start | bytes 2228224 | tf_op jit(solution)/shard_map/reduce_scatter | solution.py:141
  149.8 6.3 %collective-permute-start = (f32[2048,256]{1,0:T(8,128)S(1)}, f32[2048,256]{1,0:T(8,128)S(1)}, u32[]{:S(2)}, u32[]{:S(2)}) collective-permute-start(f32[2048,256]{1,0:T(8,128)S(1)} %bitcast.34), channel_id=1, source_target_pairs={{0,1},{1,0},{2,3},{3,2},{4,5},{5,4},{6,7},{7,6},{8,9},{9,8},{10,11... | collective-permute-start | bytes 6291464 | tf_op jit(solution)/shard_map/ppermute | solution.py:140
  251.7 2.7 copy-start.2
  254.4 209.3 %all-to-all-start.2 = ((f32[1024,8,8]{2,1,0:T(8,128)}), f32[1024,8,8]{2,1,0:T(8,128)}, u32[]{:S(2)}, u32[]{:S(2)}) async-start(f32[1024,8,8]{2,1,0:T(8,128)} %broadcast_in_dim.5), calls=%async_computation.3 | async-start | bytes 8388608 | tf_op jit(solution)/shard_map/all_to_all | solution.py:154
Sparse Core Ops, SparseCore 0:
  158.0 72.3 reduce-scatter.1

commit v7 on v5

--- a/solution.py
+++ b/solution.py
@@ -105,6 +105,12 @@
     return jnp.concatenate([first, second], axis=0)
 
 
+def gather_rows(value, axis):
+    size = lax.axis_size(axis)
+    copies = jnp.broadcast_to(value[None], (size,) + value.shape)
+    return lax.all_to_all(copies, axis, 0, 0, tiled=True)
+
+
 def butterfly_sum(value, axis):
     size = lax.axis_size(axis)
     step = 1
@@ -119,9 +125,8 @@
     own_context = contexts[0]
     own_cotangent = cotangents[0]
     rank_width = adapter.shape[1] // 2
-    piece = lax.all_gather(adapter, "z", axis=0, tiled=True)
-    piece = double(piece, "x", 0)
-    piece = double(piece, "x", 1)
+    piece = gather_rows(adapter, "z")
+    piece = gather_rows(piece, "x").reshape(-1, adapter.shape[1])
     piece = double(piece, "core", 0)
     zs, xs, cs = (lax.axis_size(a) for a in FSDP)
     blocks_in = piece.reshape(cs, xs, zs, -1, piece.shape[1])
@@ -154,7 +159,7 @@
     partial_gram = jnp.einsum("sij,tij->st", pieces, pieces, precision=lax.Precision.HIGHEST)
     gram_matrix = butterfly_sum(partial_gram, "core")
     for axis in ("x", "z"):
-        gathered = lax.all_gather(gram_matrix, axis, axis=0, tiled=False)
+        gathered = gather_rows(gram_matrix, axis)
         gram_matrix = gathered[0]
         for position in range(1, gathered.shape[0]):
             gram_matrix = gram_matrix + gathered[position]

time: 284 us -> 259 us (0.912)
  waiting for transfers between devices: 109 us -> 96 us
  starting transfers between devices: 20.8 us -> 14.9 us
  blocking collectives: 102 us -> 97.6 us
    all_gather x3 -> x0, blocking collectives: 83.4 us -> none  [the longest x1 44 us: body(): piece = lax.all_gather(adapter, 'z', axis=0, tiled=True)]
    all_to_all x0 -> x4, blocking collectives: none -> 79.5 us  [gather_rows(): return lax.all_to_all(copies, axis, 0, 0, tiled=True)]
    ppermute x3 -> x1, waiting for transfers between devices: 21.3 us -> 2.75 us  [double(): other = lax.ppermute(value, axis, pairs)]
    ppermute x3 -> x1, starting transfers between devices: 7.29 us -> 1.91 us  [double(): other = lax.ppermute(value, axis, pairs)]
    reduce_scatter x1, waiting for transfers between devices: 71.1 us -> 76.4 us  [body(): lax.psum_scatter(grad_rows, 'z', scatter_dimension=0, tiled=True)]
  transfers between devices with their start and end apart: 9 -> 7, of which waited for: 9 -> 7; matrix products, arithmetic and copies ran while one was open for 0% -> 0% of each run, Pallas kernels for 0% -> 0%
where the time goes in v7:
time: 259 us; the launch traced here: 258 us
  blocking collectives  97.6 us (38%)
  waiting for transfers between devices  96 us (37%)
  starting transfers between devices  14.9 us (6%)
  local copies, waits for them, and re-layouts  14.6 us (6%)
  between operations  14.2 us (5%)
  other arithmetic  10.2 us (4%)
  matrix products  7.58 us (3%)
    all_to_all x4, blocking collectives, gather_rows(): return lax.all_to_all(copies, axis, 0, 0, tiled=True)  79.5 us
    reduce_scatter x1, waiting for transfers between devices, body(): lax.psum_scatter(grad_rows, 'z', scatter_dimension=0, tiled=True)  76.4 us
    all_to_all x1, blocking collectives, body(): tiles = lax.all_to_all(tiles, ('x', 'task'), 0, 0, tiled=True)  18.2 us
    ppermute x4, waiting for transfers between devices, butterfly_sum(): value = value + lax.ppermute(value, axis, pairs)  12.8 us
    ppermute x4, starting transfers between devices, butterfly_sum(): value = value + lax.ppermute(value, axis, pairs)  10.9 us
    concatenate x1, local copies, waits for them, and re-layouts, body(): grad_rows = jnp.concatenate([down_part, up_part], axis=1)  5.62 us
  transfers between devices with their start and end apart: 7, of which 7 were waited for; matrix products, arithmetic and copies ran while one was open for 0% of the time, Pallas kernels for 0%

profile of v7, /device:TPU:6, one launch (start us, length us, event | category | flops | bytes accessed | tf_op | source)
XLA Modules:
  0.0 257.5 jit_solution(2290511261536660160)
XLA Ops:
  7.2 0.8 broadcast_in_dim.10
  8.1 37.0 %all_to_all.25 = bf16[16,32,256]{2,1,0:T(8,128)(2,1)S(1)} all-to-all(bf16[16,32,256]{2,1,0:T(8,128)(2,1)S(1)} %broadcast_in_dim.10), channel_id=1, replica_groups=mesh['task'=8,'z'=16,'x'=4,'core'=2] {'z'}, dimensions={0} | all-to-all | bytes 524288 | tf_op jit(solution)/shard_map/all_to_all | solution.py:111
  45.2 13.4 %all_to_all.26 = bf16[4,16,32,256]{3,2,1,0:T(8,128)(2,1)S(1)} all-to-all(bf16[4,16,32,256]{3,2,1,0:T(8,128)(2,1)S(1)} %broadcast_in_dim.11), channel_id=1, replica_groups=mesh['task'=8,'z'=16,'x'=4,'core'=2] {'x'}, dimensions={0} | all-to-all | bytes 2097152 | tf_op jit(solution)/shard_map/all_to_all | solution.py:111
  58.6 1.9 collective-permute-start
  60.6 2.8 %collective-permute-done = bf16[2048,256]{1,0:T(8,128)(2,1)} collective-permute-done((bf16[2048,256]{1,0:T(8,128)(2,1)S(1)}, bf16[2048,256]{1,0:T(8,128)(2,1)}, u32[]{:S(2)}, u32[]{:S(2)}) %collective-permute-start) | collective-permute-done | bytes 1048608 | tf_op jit(solution)/shard_map/ppermute | solution.py:102
  63.3 1.4 broadcast_select_fusion.1
  64.8 1.5 copy.20
  66.8 3.6 %convolution_bitcast_fusion = f32[4096,128]{0,1:T(8,128)} fusion(bf16[1,192,4096]{2,1,0:T(8,128)(2,1)S(1)} %copy-done, bf16[1,192,4096]{2,1,0:T(8,128)(2,1)S(1)} %copy-done.1, bf16[4096,256]{1,0:T(8,128)(2,1)} %bitcast.44), kind=kOutput, calls=%fused_computation | convolution fusion | flops 402677760 | bytes 6291456 | tf_op jit(solution)/shard_map/dot_general | solution.py:139
  70.4 3.6 %convolution_bitcast_fusion.1 = f32[4096,128]{0,1:T(8,128)} fusion(bf16[1,192,4096]{2,1,0:T(8,128)(2,1)S(1)} %copy-done.1, bf16[1,192,4096]{2,1,0:T(8,128)(2,1)S(1)} %copy-done, bf16[4096,256]{1,0:T(8,128)(2,1)} %bitcast.45), kind=kOutput, calls=%fused_computation.1 | convolution fusion | flops 402677760 | bytes 6291456 | tf_op jit(solution)/shard_map/dot_general | solution.py:136
  74.0 4.6 %pad_maximum_fusion = f32[4096,256]{0,1:T(8,128)} fusion(f32[4096,128]{0,1:T(8,128)} %convolution_bitcast_fusion, f32[4096,128]{0,1:T(8,128)} %convolution_bitcast_fusion.1), kind=kLoop, calls=%fused_computation.2 | loop fusion | flops 1048576 | bytes 8388608 | tf_op jit(solution)/shard_map/concatenate | solution.py:142
  78.6 5.6 %copy.21 = f32[4096,256]{1,0:T(8,128)} copy(f32[4096,256]{0,1:T(8,128)} %pad_maximum_fusion) | data formatting | bytes 8388608 | tf_op jit(solution)/shard_map/concatenate | solution.py:142
  84.3 2.5 constant_dynamic-slice_fusion.1
  86.8 2.0 collective-permute-start.1
  88.8 4.0 %collective-permute-done.1 = f32[2048,256]{1,0:T(8,128)S(1)} collective-permute-done((f32[2048,256]{1,0:T(8,128)S(1)}, f32[2048,256]{1,0:T(8,128)S(1)}, u32[]{:S(2)}, u32[]{:S(2)}) %collective-permute-start.1) | collective-permute-done | bytes 2097184 | tf_op jit(solution)/shard_map/ppermute | solution.py:148
  92.9 1.8 bitcast_add_fusion
  94.7 76.4 %reduce-scatter.2.cloned.1.call-done = f32[128,256]{1,0:T(8,128)} async-done(((f32[2048,256]{1,0:T(8,128)}), f32[128,256]{1,0:T(8,128)}) %reduce-scatter.2.cloned.1.call-update) | async-done | bytes 131088 | tf_op jit(solution)/shard_map/reduce_scatter | solution.py:149
  171.1 1.1 reshape.105
  172.6 18.2 %all_to_all.27 = f32[32,1,1024]{2,1,0:T(1,128)S(1)} all-to-all(f32[32,1,1024]{2,1,0:T(1,128)S(1)} %reshape.119), channel_id=1, replica_groups=mesh['task'=8,'z'=16,'x'=4,'core'=2] {'x','task'}, dimensions={0} | all-to-all | bytes 262144 | tf_op jit(solution)/shard_map/all_to_all | solution.py:154
  191.2 0.9 reduce.10
  192.8 1.9 collective-permute-start.2
  194.8 1.1 collective-permute-done.2
  195.9 7.8 %all_to_all.28 = f32[4,8,8]{2,1,0:T(8,128)S(1)} all-to-all(f32[4,8,8]{2,1,0:T(8,128)S(1)} %broadcast_in_dim.12), channel_id=1, replica_groups=mesh['task'=8,'z'=16,'x'=4,'core'=2] {'x'}, dimensions={0} | all-to-all | bytes 2048 | tf_op jit(solution)/shard_map/all_to_all | solution.py:111
  203.8 21.2 %all_to_all.29 = f32[16,8,8]{2,1,0:T(8,128)S(1)} all-to-all(f32[16,8,8]{2,1,0:T(8,128)S(1)} %broadcast_in_dim.14), channel_id=1, replica_groups=mesh['task'=8,'z'=16,'x'=4,'core'=2] {'z'}, dimensions={0} | all-to-all | bytes 8192 | tf_op jit(solution)/shard_map/all_to_all | solution.py:111
  225.0 2.7 %collective-permute-start.3 = (f32[8,8]{0,1:T(8,128)S(1)}, f32[8,8]{0,1:T(8,128)S(1)}, u32[]{:S(2)}, u32[]{:S(2)}) collective-permute-start(f32[8,8]{0,1:T(8,128)S(1)} %copy.26), channel_id=1, source_target_pairs={{0,128},{128,0},{256,384},{384,256},{512,640},{640,512},{768,896},... | collective-permute-start | bytes 776 | tf_op jit(solution)/shard_map/ppermute | solution.py:119
  227.7 2.8 %collective-permute-done.3 = f32[8,8]{0,1:T(8,128)S(1)} collective-permute-done((f32[8,8]{0,1:T(8,128)S(1)}, f32[8,8]{0,1:T(8,128)S(1)}, u32[]{:S(2)}, u32[]{:S(2)}) %collective-permute-start.3) | collective-permute-done | bytes 288 | tf_op jit(solution)/shard_map/ppermute | solution.py:119
  230.5 3.2 %collective-permute-start.4 = (f32[8,8]{0,1:T(8,128)S(1)}, f32[8,8]{0,1:T(8,128)S(1)}, u32[]{:S(2)}, u32[]{:S(2)}) collective-permute-start(f32[8,8]{0,1:T(8,128)S(1)} %add.135), channel_id=1, source_target_pairs={{0,256},{128,384},{256,0},{384,128},{512,768},{640,896},{768,512},... | collective-permute-start | bytes 776 | tf_op jit(solution)/shard_map/ppermute | solution.py:119
  233.7 3.2 %collective-permute-done.4 = f32[8,8]{0,1:T(8,128)S(1)} collective-permute-done((f32[8,8]{0,1:T(8,128)S(1)}, f32[8,8]{0,1:T(8,128)S(1)}, u32[]{:S(2)}, u32[]{:S(2)}) %collective-permute-start.4) | collective-permute-done | bytes 288 | tf_op jit(solution)/shard_map/ppermute | solution.py:119
  236.9 3.1 %collective-permute-start.5 = (f32[8,8]{0,1:T(8,128)S(1)}, f32[8,8]{0,1:T(8,128)S(1)}, u32[]{:S(2)}, u32[]{:S(2)}) collective-permute-start(f32[8,8]{0,1:T(8,128)S(1)} %add.136), channel_id=1, source_target_pairs={{0,512},{128,640},{256,768},{384,896},{512,0},{640,128},{768,256},... | collective-permute-start | bytes 776 | tf_op jit(solution)/shard_map/ppermute | solution.py:119
  240.0 0.6 compare_reduce_fusion
  240.7 5.6 %collective-permute-done.5 = f32[8,8]{0,1:T(8,128)S(1)} collective-permute-done((f32[8,8]{0,1:T(8,128)S(1)}, f32[8,8]{0,1:T(8,128)S(1)}, u32[]{:S(2)}, u32[]{:S(2)}) %collective-permute-start.5) | collective-permute-done | bytes 288 | tf_op jit(solution)/shard_map/ppermute | solution.py:119
  246.3 0.6 add_select_fusion
  248.2 2.4 shard_map.76
  (27 shorter events, 3.6 us)
Async XLA Ops:
  7.2 59.2 %copy-start = (bf16[1,192,4096]{2,1,0:T(8,128)(2,1)S(1)}, bf16[1,192,4096]{2,1,0:T(8,128)(2,1)}, u32[]{:S(2)}) copy-start(bf16[1,192,4096]{2,1,0:T(8,128)(2,1)} %param.10) | copy-start | bytes 4718596
  7.2 163.9 %reduce-scatter.2.cloned.1.call-start = ((), (), s32[]{:S(2)}) async-start(), calls=%async_computation.6 | async-start | bytes 2228224 | tf_op jit(solution)/shard_map/reduce_scatter | solution.py:149
  58.6 4.7 %collective-permute-start = (bf16[2048,256]{1,0:T(8,128)(2,1)S(1)}, bf16[2048,256]{1,0:T(8,128)(2,1)}, u32[]{:S(2)}, u32[]{:S(2)}) collective-permute-start(bf16[2048,256]{1,0:T(8,128)(2,1)S(1)} %bitcast.46), channel_id=1, source_target_pairs={{0,1},{1,0},{2,3},{3,2},{4,5},{5,4},{6,7},{7,6},{8,9},{9,8},{10,11... | collective-permute-start | bytes 3145736 | tf_op jit(solution)/shard_map/ppermute | solution.py:102
  64.8 2.0 copy-start.1
  86.8 6.1 %collective-permute-start.1 = (f32[2048,256]{1,0:T(8,128)S(1)}, f32[2048,256]{1,0:T(8,128)S(1)}, u32[]{:S(2)}, u32[]{:S(2)}) collective-permute-start(f32[2048,256]{1,0:T(8,128)S(1)} %bitcast.47), channel_id=1, source_target_pairs={{0,1},{1,0},{2,3},{3,2},{4,5},{5,4},{6,7},{7,6},{8,9},{9,8},{10,11... | collective-permute-start | bytes 6291464 | tf_op jit(solution)/shard_map/ppermute | solution.py:148
  192.4 55.9 %copy-start.2 = (f32[8,32,32]{2,1,0:T(8,128)}, f32[8,32,32]{2,1,0:T(8,128)S(1)}, u32[]{:S(2)}) copy-start(f32[8,32,32]{2,1,0:T(8,128)S(1)} %slice_add_fusion.pieces_ref) | copy-start | bytes 98308
  192.8 3.1 %collective-permute-start.2 = (f32[8,8]{1,0:T(8,128)S(1)}, f32[8,8]{1,0:T(8,128)S(1)}, u32[]{:S(2)}, u32[]{:S(2)}) collective-permute-start(f32[8,8]{1,0:T(8,128)S(1)} %convolution_bitcast_fusion.2), channel_id=1, source_target_pairs={{0,1},{1,0},{2,3},{3,2},{4,5},{5,4},{6,7},{7,6},{8,9},{9,8},{10,11... | collective-permute-start | bytes 776 | tf_op jit(solution)/shard_map/ppermute | solution.py:119
  225.0 5.5 %collective-permute-start.3 = (f32[8,8]{0,1:T(8,128)S(1)}, f32[8,8]{0,1:T(8,128)S(1)}, u32[]{:S(2)}, u32[]{:S(2)}) collective-permute-start(f32[8,8]{0,1:T(8,128)S(1)} %copy.26), channel_id=1, source_target_pairs={{0,128},{128,0},{256,384},{384,256},{512,640},{640,512},{768,896},... | collective-permute-start | bytes 776 | tf_op jit(solution)/shard_map/ppermute | solution.py:119
  230.5 6.4 %collective-permute-start.4 = (f32[8,8]{0,1:T(8,128)S(1)}, f32[8,8]{0,1:T(8,128)S(1)}, u32[]{:S(2)}, u32[]{:S(2)}) collective-permute-start(f32[8,8]{0,1:T(8,128)S(1)} %add.135), channel_id=1, source_target_pairs={{0,256},{128,384},{256,0},{384,128},{512,768},{640,896},{768,512},... | collective-permute-start | bytes 776 | tf_op jit(solution)/shard_map/ppermute | solution.py:119
  236.9 9.4 %collective-permute-start.5 = (f32[8,8]{0,1:T(8,128)S(1)}, f32[8,8]{0,1:T(8,128)S(1)}, u32[]{:S(2)}, u32[]{:S(2)}) collective-permute-start(f32[8,8]{0,1:T(8,128)S(1)} %add.136), channel_id=1, source_target_pairs={{0,512},{128,640},{256,768},{384,896},{512,0},{640,128},{768,256},... | collective-permute-start | bytes 776 | tf_op jit(solution)/shard_map/ppermute | solution.py:119
Sparse Core Ops, SparseCore 0:
  94.8 76.2 reduce-scatter.1

commit v8 on v7

--- a/solution.py
+++ b/solution.py
@@ -146,7 +146,11 @@
     mine = lax.dynamic_index_in_dim(by_core, me, 1, keepdims=False).reshape(-1, full[1])
     other = lax.dynamic_index_in_dim(by_core, 1 - me, 1, keepdims=False).reshape(-1, full[1])
     grad_rows = mine + lax.ppermute(other, "core", [(0, 1), (1, 0)])
-    grad_rows = lax.psum_scatter(grad_rows, "z", scatter_dimension=0, tiled=True)
+    chunks = grad_rows.reshape((zs, -1) + grad_rows.shape[1:])
+    chunks = lax.all_to_all(chunks, "z", 0, 0, tiled=True)
+    grad_rows = chunks[0]
+    for position in range(1, zs):
+        grad_rows = grad_rows + chunks[position]
     tasks = lax.axis_size("task")
     rows, width = grad_rows.shape
     tiles = grad_rows.reshape(xs, rows // xs, tasks, width // tasks).transpose(0, 2, 1, 3)

time: 259 us -> 272 us (1.050)
  blocking collectives: 97.6 us -> 202 us
  waiting for transfers between devices: 96 us -> 19.1 us
  between operations: 14.2 us -> 0.8 us
    all_to_all x0 -> x1, blocking collectives: none -> 107 us  [body(): chunks = lax.all_to_all(chunks, 'z', 0, 0, tiled=True)]
    reduce_scatter x1 -> x0, waiting for transfers between devices: 76.4 us -> none  [body(): lax.psum_scatter(grad_rows, 'z', scatter_dimension=0, tiled=True)]
  transfers between devices with their start and end apart: 7 -> 6, of which waited for: 7 -> 6; matrix products, arithmetic and copies ran while one was open for 0% -> 0% of each run, Pallas kernels for 0% -> 0%
where the time goes in v8:
time: 272 us; the launch traced here: 270 us
  blocking collectives  202 us (74%)
  waiting for transfers between devices  19.1 us (7%)
  starting transfers between devices  15.3 us (6%)
  local copies, waits for them, and re-layouts  13.7 us (5%)
  other arithmetic  8.95 us (3%)
  matrix products  7.55 us (3%)
    all_to_all x1, blocking collectives, body(): chunks = lax.all_to_all(chunks, 'z', 0, 0, tiled=True)  107 us
    all_to_all x4, blocking collectives, gather_rows(): return lax.all_to_all(copies, axis, 0, 0, tiled=True)  77.3 us
    all_to_all x1, blocking collectives, body(): tiles = lax.all_to_all(tiles, ('x', 'task'), 0, 0, tiled=True)  18.2 us
    ppermute x4, waiting for transfers between devices, butterfly_sum(): value = value + lax.ppermute(value, axis, pairs)  12.4 us
    ppermute x4, starting transfers between devices, butterfly_sum(): value = value + lax.ppermute(value, axis, pairs)  11.4 us
    concatenate x1, local copies, waits for them, and re-layouts, body(): grad_rows = jnp.concatenate([down_part, up_part], axis=1)  5.62 us
  transfers between devices with their start and end apart: 6, of which 6 were waited for; matrix products, arithmetic and copies ran while one was open for 0% of the time, Pallas kernels for 0%

profile of v8, /device:TPU:6, one launch (start us, length us, event | category | flops | bytes accessed | tf_op | source)
XLA Modules:
  0.0 269.9 jit_solution(4533647393919691672)
XLA Ops:
  0.6 0.9 broadcast_in_dim.10
  1.5 37.0 %all_to_all.30 = bf16[16,32,256]{2,1,0:T(8,128)(2,1)S(1)} all-to-all(bf16[16,32,256]{2,1,0:T(8,128)(2,1)S(1)} %broadcast_in_dim.10), channel_id=1, replica_groups=mesh['task'=8,'z'=16,'x'=4,'core'=2] {'z'}, dimensions={0} | all-to-all | bytes 524288 | tf_op jit(solution)/shard_map/all_to_all | solution.py:111
  38.7 13.4 %all_to_all.31 = bf16[4,16,32,256]{3,2,1,0:T(8,128)(2,1)S(1)} all-to-all(bf16[4,16,32,256]{3,2,1,0:T(8,128)(2,1)S(1)} %broadcast_in_dim.11), channel_id=1, replica_groups=mesh['task'=8,'z'=16,'x'=4,'core'=2] {'x'}, dimensions={0} | all-to-all | bytes 2097152 | tf_op jit(solution)/shard_map/all_to_all | solution.py:111
  52.1 1.9 collective-permute-start
  54.0 2.8 %collective-permute-done = bf16[2048,256]{1,0:T(8,128)(2,1)} collective-permute-done((bf16[2048,256]{1,0:T(8,128)(2,1)S(1)}, bf16[2048,256]{1,0:T(8,128)(2,1)}, u32[]{:S(2)}, u32[]{:S(2)}) %collective-permute-start) | collective-permute-done | bytes 1048608 | tf_op jit(solution)/shard_map/ppermute | solution.py:102
  56.8 1.4 broadcast_select_fusion.1
  58.3 1.5 copy.20
  60.3 3.6 %convolution_bitcast_fusion = f32[4096,128]{0,1:T(8,128)} fusion(bf16[1,192,4096]{2,1,0:T(8,128)(2,1)S(1)} %copy-done, bf16[1,192,4096]{2,1,0:T(8,128)(2,1)S(1)} %copy-done.1, bf16[4096,256]{1,0:T(8,128)(2,1)} %bitcast.46), kind=kOutput, calls=%fused_computation | convolution fusion | flops 402677760 | bytes 6291456 | tf_op jit(solution)/shard_map/dot_general | solution.py:139
  63.8 3.6 %convolution_bitcast_fusion.1 = f32[4096,128]{0,1:T(8,128)} fusion(bf16[1,192,4096]{2,1,0:T(8,128)(2,1)S(1)} %copy-done.1, bf16[1,192,4096]{2,1,0:T(8,128)(2,1)S(1)} %copy-done, bf16[4096,256]{1,0:T(8,128)(2,1)} %bitcast.47), kind=kOutput, calls=%fused_computation.1 | convolution fusion | flops 402677760 | bytes 6291456 | tf_op jit(solution)/shard_map/dot_general | solution.py:136
  67.4 4.6 %pad_maximum_fusion = f32[4096,256]{0,1:T(8,128)} fusion(f32[4096,128]{0,1:T(8,128)} %convolution_bitcast_fusion, f32[4096,128]{0,1:T(8,128)} %convolution_bitcast_fusion.1), kind=kLoop, calls=%fused_computation.2 | loop fusion | flops 1048576 | bytes 8388608 | tf_op jit(solution)/shard_map/concatenate | solution.py:142
  72.0 5.6 %copy.21 = f32[4096,256]{1,0:T(8,128)} copy(f32[4096,256]{0,1:T(8,128)} %pad_maximum_fusion) | data formatting | bytes 8388608 | tf_op jit(solution)/shard_map/concatenate | solution.py:142
  77.7 2.5 constant_dynamic-slice_fusion.1
  80.2 2.0 collective-permute-start.1
  82.3 4.0 %collective-permute-done.1 = f32[2048,256]{1,0:T(8,128)S(1)} collective-permute-done((f32[2048,256]{1,0:T(8,128)S(1)}, f32[2048,256]{1,0:T(8,128)S(1)}, u32[]{:S(2)}, u32[]{:S(2)}) %collective-permute-start.1) | collective-permute-done | bytes 2097184 | tf_op jit(solution)/shard_map/ppermute | solution.py:148
  86.7 106.5 %all_to_all.32 = f32[16,128,256]{2,1,0:T(8,128)S(1)} all-to-all(f32[16,128,256]{2,1,0:T(8,128)S(1)} %bitcast.44), channel_id=1, replica_groups=mesh['task'=8,'z'=16,'x'=4,'core'=2] {'z'}, dimensions={0} | all-to-all | bytes 4194304 | tf_op jit(solution)/shard_map/all_to_all | solution.py:150
  193.9 18.2 %all_to_all.33 = f32[32,1,1024]{2,1,0:T(1,128)S(1)} all-to-all(f32[32,1,1024]{2,1,0:T(1,128)S(1)} %reshape.151), channel_id=1, replica_groups=mesh['task'=8,'z'=16,'x'=4,'core'=2] {'x','task'}, dimensions={0} | all-to-all | bytes 262144 | tf_op jit(solution)/shard_map/all_to_all | solution.py:158
  212.6 0.9 reduce.10
  214.1 1.9 collective-permute-start.2
  216.1 1.1 collective-permute-done.2
  217.2 7.8 %all_to_all.34 = f32[4,8,8]{2,1,0:T(8,128)S(1)} all-to-all(f32[4,8,8]{2,1,0:T(8,128)S(1)} %broadcast_in_dim.12), channel_id=1, replica_groups=mesh['task'=8,'z'=16,'x'=4,'core'=2] {'x'}, dimensions={0} | all-to-all | bytes 2048 | tf_op jit(solution)/shard_map/all_to_all | solution.py:111
  225.1 19.0 %all_to_all.35 = f32[16,8,8]{2,1,0:T(8,128)S(1)} all-to-all(f32[16,8,8]{2,1,0:T(8,128)S(1)} %broadcast_in_dim.14), channel_id=1, replica_groups=mesh['task'=8,'z'=16,'x'=4,'core'=2] {'z'}, dimensions={0} | all-to-all | bytes 8192 | tf_op jit(solution)/shard_map/all_to_all | solution.py:111
  244.2 3.1 %collective-permute-start.3 = (f32[8,8]{0,1:T(8,128)S(1)}, f32[8,8]{0,1:T(8,128)S(1)}, u32[]{:S(2)}, u32[]{:S(2)}) collective-permute-start(f32[8,8]{0,1:T(8,128)S(1)} %copy.26), channel_id=1, source_target_pairs={{0,128},{128,0},{256,384},{384,256},{512,640},{640,512},{768,896},... | collective-permute-start | bytes 776 | tf_op jit(solution)/shard_map/ppermute | solution.py:119
  247.3 2.4 collective-permute-done.3
  249.7 3.2 %collective-permute-start.4 = (f32[8,8]{0,1:T(8,128)S(1)}, f32[8,8]{0,1:T(8,128)S(1)}, u32[]{:S(2)}, u32[]{:S(2)}) collective-permute-start(f32[8,8]{0,1:T(8,128)S(1)} %add.215), channel_id=1, source_target_pairs={{0,256},{128,384},{256,0},{384,128},{512,768},{640,896},{768,512},... | collective-permute-start | bytes 776 | tf_op jit(solution)/shard_map/ppermute | solution.py:119
  252.9 3.2 %collective-permute-done.4 = f32[8,8]{0,1:T(8,128)S(1)} collective-permute-done((f32[8,8]{0,1:T(8,128)S(1)}, f32[8,8]{0,1:T(8,128)S(1)}, u32[]{:S(2)}, u32[]{:S(2)}) %collective-permute-start.4) | collective-permute-done | bytes 288 | tf_op jit(solution)/shard_map/ppermute | solution.py:119
  256.1 3.1 %collective-permute-start.5 = (f32[8,8]{0,1:T(8,128)S(1)}, f32[8,8]{0,1:T(8,128)S(1)}, u32[]{:S(2)}, u32[]{:S(2)}) collective-permute-start(f32[8,8]{0,1:T(8,128)S(1)} %add.216), channel_id=1, source_target_pairs={{0,512},{128,640},{256,768},{384,896},{512,0},{640,128},{768,256},... | collective-permute-start | bytes 776 | tf_op jit(solution)/shard_map/ppermute | solution.py:119
  259.3 0.6 compare_reduce_fusion
  259.9 5.6 %collective-permute-done.5 = f32[8,8]{0,1:T(8,128)S(1)} collective-permute-done((f32[8,8]{0,1:T(8,128)S(1)}, f32[8,8]{0,1:T(8,128)S(1)}, u32[]{:S(2)}, u32[]{:S(2)}) %collective-permute-start.5) | collective-permute-done | bytes 288 | tf_op jit(solution)/shard_map/ppermute | solution.py:119
  265.5 0.6 add_select_fusion
  266.2 0.6 scatter.6.clone.gram_ref
  266.8 0.6 scatter.9.gramt_ref
  267.4 2.4 shard_map.76
  (26 shorter events, 3.0 us)
Async XLA Ops:
  0.6 59.2 %copy-start = (bf16[1,192,4096]{2,1,0:T(8,128)(2,1)S(1)}, bf16[1,192,4096]{2,1,0:T(8,128)(2,1)}, u32[]{:S(2)}) copy-start(bf16[1,192,4096]{2,1,0:T(8,128)(2,1)} %param.10) | copy-start | bytes 4718596
  52.1 4.7 %collective-permute-start = (bf16[2048,256]{1,0:T(8,128)(2,1)S(1)}, bf16[2048,256]{1,0:T(8,128)(2,1)}, u32[]{:S(2)}, u32[]{:S(2)}) collective-permute-start(bf16[2048,256]{1,0:T(8,128)(2,1)S(1)} %bitcast.48), channel_id=1, source_target_pairs={{0,1},{1,0},{2,3},{3,2},{4,5},{5,4},{6,7},{7,6},{8,9},{9,8},{10,11... | collective-permute-start | bytes 3145736 | tf_op jit(solution)/shard_map/ppermute | solution.py:102
  58.3 2.0 copy-start.1
  80.2 6.1 %collective-permute-start.1 = (f32[2048,256]{1,0:T(8,128)S(1)}, f32[2048,256]{1,0:T(8,128)S(1)}, u32[]{:S(2)}, u32[]{:S(2)}) collective-permute-start(f32[2048,256]{1,0:T(8,128)S(1)} %bitcast.49), channel_id=1, source_target_pairs={{0,1},{1,0},{2,3},{3,2},{4,5},{5,4},{6,7},{7,6},{8,9},{9,8},{10,11... | collective-permute-start | bytes 6291464 | tf_op jit(solution)/shard_map/ppermute | solution.py:148
  213.7 53.7 %copy-start.2 = (f32[8,32,32]{2,1,0:T(8,128)}, f32[8,32,32]{2,1,0:T(8,128)S(1)}, u32[]{:S(2)}) copy-start(f32[8,32,32]{2,1,0:T(8,128)S(1)} %slice_add_fusion.pieces_ref) | copy-start | bytes 98308
  214.1 3.1 %collective-permute-start.2 = (f32[8,8]{1,0:T(8,128)S(1)}, f32[8,8]{1,0:T(8,128)S(1)}, u32[]{:S(2)}, u32[]{:S(2)}) collective-permute-start(f32[8,8]{1,0:T(8,128)S(1)} %convolution_bitcast_fusion.2), channel_id=1, source_target_pairs={{0,1},{1,0},{2,3},{3,2},{4,5},{5,4},{6,7},{7,6},{8,9},{9,8},{10,11... | collective-permute-start | bytes 776 | tf_op jit(solution)/shard_map/ppermute | solution.py:119
  244.2 5.5 %collective-permute-start.3 = (f32[8,8]{0,1:T(8,128)S(1)}, f32[8,8]{0,1:T(8,128)S(1)}, u32[]{:S(2)}, u32[]{:S(2)}) collective-permute-start(f32[8,8]{0,1:T(8,128)S(1)} %copy.26), channel_id=1, source_target_pairs={{0,128},{128,0},{256,384},{384,256},{512,640},{640,512},{768,896},... | collective-permute-start | bytes 776 | tf_op jit(solution)/shard_map/ppermute | solution.py:119
  249.7 6.4 %collective-permute-start.4 = (f32[8,8]{0,1:T(8,128)S(1)}, f32[8,8]{0,1:T(8,128)S(1)}, u32[]{:S(2)}, u32[]{:S(2)}) collective-permute-start(f32[8,8]{0,1:T(8,128)S(1)} %add.215), channel_id=1, source_target_pairs={{0,256},{128,384},{256,0},{384,128},{512,768},{640,896},{768,512},... | collective-permute-start | bytes 776 | tf_op jit(solution)/shard_map/ppermute | solution.py:119
  256.1 9.4 %collective-permute-start.5 = (f32[8,8]{0,1:T(8,128)S(1)}, f32[8,8]{0,1:T(8,128)S(1)}, u32[]{:S(2)}, u32[]{:S(2)}) collective-permute-start(f32[8,8]{0,1:T(8,128)S(1)} %add.216), channel_id=1, source_target_pairs={{0,512},{128,640},{256,768},{384,896},{512,0},{640,128},{768,256},... | collective-permute-start | bytes 776 | tf_op jit(solution)/shard_map/ppermute | solution.py:119

commit v9 on v7

--- a/solution.py
+++ b/solution.py
@@ -158,12 +158,11 @@
         pieces = pieces + tiles[position]
     partial_gram = jnp.einsum("sij,tij->st", pieces, pieces, precision=lax.Precision.HIGHEST)
     gram_matrix = butterfly_sum(partial_gram, "core")
-    for axis in ("x", "z"):
+    for axis in ("x", "z", "task"):
         gathered = gather_rows(gram_matrix, axis)
         gram_matrix = gathered[0]
         for position in range(1, gathered.shape[0]):
             gram_matrix = gram_matrix + gathered[position]
-    gram_matrix = butterfly_sum(gram_matrix, "task")
     return tail(gram_matrix, pieces, moment_one, moment_two)
 
 

time: 259 us -> 249 us (0.961)
  starting transfers between devices: 14.9 us -> 9.24 us
  waiting for transfers between devices: 96 us -> 91.7 us
    ppermute x4 -> x1, waiting for transfers between devices: 12.8 us -> 1.13 us  [butterfly_sum(): value = value + lax.ppermute(value, axis, pairs)]
    ppermute x4 -> x1, starting transfers between devices: 10.9 us -> 1.95 us  [butterfly_sum(): value = value + lax.ppermute(value, axis, pairs)]
    all_to_all x0 -> x1, waiting for transfers between devices: none -> 7.3 us  [gather_rows(): return lax.all_to_all(copies, axis, 0, 0, tiled=True)]
    all_to_all x0 -> x1, starting transfers between devices: none -> 3.32 us  [gather_rows(): return lax.all_to_all(copies, axis, 0, 0, tiled=True)]
  transfers between devices with their start and end apart: 7 -> 5, of which waited for: 7 -> 5; matrix products, arithmetic and copies ran while one was open for 0% -> 0% of each run, Pallas kernels for 0% -> 0%
where the time goes in v9:
time: 249 us; the launch traced here: 248 us
  blocking collectives  97.6 us (39%)
  waiting for transfers between devices  91.7 us (37%)
  local copies, waits for them, and re-layouts  15.1 us (6%)
  between operations  14.2 us (6%)
  other arithmetic  10.2 us (4%)
  starting transfers between devices  9.24 us (4%)
  matrix products  7.55 us (3%)
    all_to_all x4, blocking collectives, gather_rows(): return lax.all_to_all(copies, axis, 0, 0, tiled=True)  79.4 us
    reduce_scatter x1, waiting for transfers between devices, body(): lax.psum_scatter(grad_rows, 'z', scatter_dimension=0, tiled=True)  76.5 us
    all_to_all x1, blocking collectives, body(): tiles = lax.all_to_all(tiles, ('x', 'task'), 0, 0, tiled=True)  18.2 us
    all_to_all x1, waiting for transfers between devices, gather_rows(): return lax.all_to_all(copies, axis, 0, 0, tiled=True)  7.3 us
    concatenate x1, local copies, waits for them, and re-layouts, body(): grad_rows = jnp.concatenate([down_part, up_part], axis=1)  5.61 us
  transfers between devices with their start and end apart: 5, of which 5 were waited for; matrix products, arithmetic and copies ran while one was open for 0% of the time, Pallas kernels for 0%

profile of v9, /device:TPU:6, one launch (start us, length us, event | category | flops | bytes accessed | tf_op | source)
XLA Modules:
  0.0 248.0 jit_solution(13046766919618449883)
XLA Ops:
  7.2 0.8 broadcast_in_dim.14
  8.1 37.0 %all_to_all.30 = bf16[16,32,256]{2,1,0:T(8,128)(2,1)S(1)} all-to-all(bf16[16,32,256]{2,1,0:T(8,128)(2,1)S(1)} %broadcast_in_dim.14), channel_id=1, replica_groups=mesh['task'=8,'z'=16,'x'=4,'core'=2] {'z'}, dimensions={0} | all-to-all | bytes 524288 | tf_op jit(solution)/shard_map/all_to_all | solution.py:111
  45.2 13.4 %all_to_all.31 = bf16[4,16,32,256]{3,2,1,0:T(8,128)(2,1)S(1)} all-to-all(bf16[4,16,32,256]{3,2,1,0:T(8,128)(2,1)S(1)} %broadcast_in_dim.15), channel_id=1, replica_groups=mesh['task'=8,'z'=16,'x'=4,'core'=2] {'x'}, dimensions={0} | all-to-all | bytes 2097152 | tf_op jit(solution)/shard_map/all_to_all | solution.py:111
  58.6 1.9 collective-permute-start
  60.6 2.8 %collective-permute-done = bf16[2048,256]{1,0:T(8,128)(2,1)} collective-permute-done((bf16[2048,256]{1,0:T(8,128)(2,1)S(1)}, bf16[2048,256]{1,0:T(8,128)(2,1)}, u32[]{:S(2)}, u32[]{:S(2)}) %collective-permute-start) | collective-permute-done | bytes 1048608 | tf_op jit(solution)/shard_map/ppermute | solution.py:102
  63.3 1.4 broadcast_select_fusion.1
  64.8 1.5 copy.16
  66.8 3.6 %convolution_bitcast_fusion = f32[4096,128]{0,1:T(8,128)} fusion(bf16[1,192,4096]{2,1,0:T(8,128)(2,1)S(1)} %copy-done, bf16[1,192,4096]{2,1,0:T(8,128)(2,1)S(1)} %copy-done.1, bf16[4096,256]{1,0:T(8,128)(2,1)} %bitcast.46), kind=kOutput, calls=%fused_computation | convolution fusion | flops 402677760 | bytes 6291456 | tf_op jit(solution)/shard_map/dot_general | solution.py:139
  70.4 3.6 %convolution_bitcast_fusion.1 = f32[4096,128]{0,1:T(8,128)} fusion(bf16[1,192,4096]{2,1,0:T(8,128)(2,1)S(1)} %copy-done.1, bf16[1,192,4096]{2,1,0:T(8,128)(2,1)S(1)} %copy-done, bf16[4096,256]{1,0:T(8,128)(2,1)} %bitcast.47), kind=kOutput, calls=%fused_computation.1 | convolution fusion | flops 402677760 | bytes 6291456 | tf_op jit(solution)/shard_map/dot_general | solution.py:136
  74.0 4.6 %pad_maximum_fusion = f32[4096,256]{0,1:T(8,128)} fusion(f32[4096,128]{0,1:T(8,128)} %convolution_bitcast_fusion, f32[4096,128]{0,1:T(8,128)} %convolution_bitcast_fusion.1), kind=kLoop, calls=%fused_computation.2 | loop fusion | flops 1048576 | bytes 8388608 | tf_op jit(solution)/shard_map/concatenate | solution.py:142
  78.6 5.6 %copy.17 = f32[4096,256]{1,0:T(8,128)} copy(f32[4096,256]{0,1:T(8,128)} %pad_maximum_fusion) | data formatting | bytes 8388608 | tf_op jit(solution)/shard_map/concatenate | solution.py:142
  84.2 2.5 %constant_dynamic-slice_fusion.1 = (f32[64,1,32,256]{3,2,1,0:T(8,128)S(1)}, f32[64,1,32,256]{3,2,1,0:T(8,128)S(1)}) fusion(f32[64,2,32,256]{3,2,1,0:T(8,128)} %bitcast.44, s32[]{:T(128)S(6)} %select_n.22, s32[]{:T(128)S(6)} %select_n.23), kind=kLoop, calls=%fused_computation.53 | loop fusion | bytes 8388616 | tf_op jit(solution)/shard_map/jit(dynamic_index_in_dim)/dynamic_slice | solution.py:146
  86.8 2.0 collective-permute-start.1
  88.8 4.0 %collective-permute-done.1 = f32[2048,256]{1,0:T(8,128)S(1)} collective-permute-done((f32[2048,256]{1,0:T(8,128)S(1)}, f32[2048,256]{1,0:T(8,128)S(1)}, u32[]{:S(2)}, u32[]{:S(2)}) %collective-permute-start.1) | collective-permute-done | bytes 2097184 | tf_op jit(solution)/shard_map/ppermute | solution.py:148
  92.8 1.8 bitcast_add_fusion
  94.6 76.5 %reduce-scatter.2.cloned.1.call-done = f32[128,256]{1,0:T(8,128)} async-done(((f32[2048,256]{1,0:T(8,128)}), f32[128,256]{1,0:T(8,128)}) %reduce-scatter.2.cloned.1.call-update) | async-done | bytes 131088 | tf_op jit(solution)/shard_map/reduce_scatter | solution.py:149
  171.1 1.1 reshape.105
  172.5 18.2 %all_to_all.32 = f32[32,1,1024]{2,1,0:T(1,128)S(1)} all-to-all(f32[32,1,1024]{2,1,0:T(1,128)S(1)} %reshape.114), channel_id=1, replica_groups=mesh['task'=8,'z'=16,'x'=4,'core'=2] {'x','task'}, dimensions={0} | all-to-all | bytes 262144 | tf_op jit(solution)/shard_map/all_to_all | solution.py:154
  190.7 0.5 broadcast.62
  191.2 0.9 reduce.10
  192.8 1.9 collective-permute-start.2
  194.8 1.1 collective-permute-done.2
  195.9 7.8 %all_to_all.33 = f32[4,8,8]{2,1,0:T(8,128)S(1)} all-to-all(f32[4,8,8]{2,1,0:T(8,128)S(1)} %broadcast_in_dim.16), channel_id=1, replica_groups=mesh['task'=8,'z'=16,'x'=4,'core'=2] {'x'}, dimensions={0} | all-to-all | bytes 2048 | tf_op jit(solution)/shard_map/all_to_all | solution.py:111
  203.8 21.1 %all_to_all.34 = f32[16,8,8]{2,1,0:T(8,128)S(1)} all-to-all(f32[16,8,8]{2,1,0:T(8,128)S(1)} %broadcast_in_dim.18), channel_id=1, replica_groups=mesh['task'=8,'z'=16,'x'=4,'core'=2] {'z'}, dimensions={0} | all-to-all | bytes 8192 | tf_op jit(solution)/shard_map/all_to_all | solution.py:111
  224.9 0.6 broadcast_in_dim.40
  225.5 3.3 %all-to-all-start.5 = ((f32[8,8,8]{2,1,0:T(8,128)}), f32[8,8,8]{2,1,0:T(8,128)S(1)}, u32[]{:S(2)}, u32[]{:S(2)}) async-start(f32[8,8,8]{2,1,0:T(8,128)} %broadcast_in_dim.40), calls=%async_computation.6 | async-start | bytes 65536 | tf_op jit(solution)/shard_map/all_to_all | solution.py:111
  228.8 0.6 compare_reduce_fusion
  229.4 7.3 %all-to-all-done.5 = f32[8,8,8]{2,1,0:T(8,128)S(1)} async-done(((f32[8,8,8]{2,1,0:T(8,128)}), f32[8,8,8]{2,1,0:T(8,128)S(1)}, u32[]{:S(2)}, u32[]{:S(2)}) %all-to-all-start.5) | async-done | bytes 2080 | tf_op jit(solution)/shard_map/all_to_all | solution.py:111
  236.8 0.7 fusion.22
  237.5 0.6 scatter.6.gram_ref
  238.1 0.6 scatter.9.gramt_ref
  238.7 2.4 shard_map.76
  (21 shorter events, 1.8 us)
Async XLA Ops:
  7.2 59.2 %copy-start = (bf16[1,192,4096]{2,1,0:T(8,128)(2,1)S(1)}, bf16[1,192,4096]{2,1,0:T(8,128)(2,1)}, u32[]{:S(2)}) copy-start(bf16[1,192,4096]{2,1,0:T(8,128)(2,1)} %param.10) | copy-start | bytes 4718596
  7.2 163.9 %reduce-scatter.2.cloned.1.call-start = ((), (), s32[]{:S(2)}) async-start(), calls=%async_computation.7 | async-start | bytes 2228224 | tf_op jit(solution)/shard_map/reduce_scatter | solution.py:149
  58.6 4.7 %collective-permute-start = (bf16[2048,256]{1,0:T(8,128)(2,1)S(1)}, bf16[2048,256]{1,0:T(8,128)(2,1)}, u32[]{:S(2)}, u32[]{:S(2)}) collective-permute-start(bf16[2048,256]{1,0:T(8,128)(2,1)S(1)} %bitcast.48), channel_id=1, source_target_pairs={{0,1},{1,0},{2,3},{3,2},{4,5},{5,4},{6,7},{7,6},{8,9},{9,8},{10,11... | collective-permute-start | bytes 3145736 | tf_op jit(solution)/shard_map/ppermute | solution.py:102
  64.8 2.0 copy-start.1
  86.8 6.1 %collective-permute-start.1 = (f32[2048,256]{1,0:T(8,128)S(1)}, f32[2048,256]{1,0:T(8,128)S(1)}, u32[]{:S(2)}, u32[]{:S(2)}) collective-permute-start(f32[2048,256]{1,0:T(8,128)S(1)} %bitcast.49), channel_id=1, source_target_pairs={{0,1},{1,0},{2,3},{3,2},{4,5},{5,4},{6,7},{7,6},{8,9},{9,8},{10,11... | collective-permute-start | bytes 6291464 | tf_op jit(solution)/shard_map/ppermute | solution.py:148
  192.4 46.3 %copy-start.2 = (f32[8,32,32]{2,1,0:T(8,128)}, f32[8,32,32]{2,1,0:T(8,128)S(1)}, u32[]{:S(2)}) copy-start(f32[8,32,32]{2,1,0:T(8,128)S(1)} %slice_add_fusion.pieces_ref) | copy-start | bytes 98308
  192.8 3.1 %collective-permute-start.2 = (f32[8,8]{1,0:T(8,128)S(1)}, f32[8,8]{1,0:T(8,128)S(1)}, u32[]{:S(2)}, u32[]{:S(2)}) collective-permute-start(f32[8,8]{1,0:T(8,128)S(1)} %convolution_bitcast_fusion.2), channel_id=1, source_target_pairs={{0,1},{1,0},{2,3},{3,2},{4,5},{5,4},{6,7},{7,6},{8,9},{9,8},{10,11... | collective-permute-start | bytes 776 | tf_op jit(solution)/shard_map/ppermute | solution.py:119
  225.5 11.3 %all-to-all-start.5 = ((f32[8,8,8]{2,1,0:T(8,128)}), f32[8,8,8]{2,1,0:T(8,128)S(1)}, u32[]{:S(2)}, u32[]{:S(2)}) async-start(f32[8,8,8]{2,1,0:T(8,128)} %broadcast_in_dim.40), calls=%async_computation.6 | async-start | bytes 65536 | tf_op jit(solution)/shard_map/all_to_all | solution.py:111
Sparse Core Ops, SparseCore 0:
  94.7 76.3 reduce-scatter.1

commit v10 on v9

--- a/solution.py
+++ b/solution.py
@@ -9,8 +9,8 @@
 
 D = 4096
 RANK = 128
-FSDP = ("z", "x", "core")
-ALL_AXES = ("core", "x", "z", "task")
+FSDP = ("zh", "zl", "x", "core")
+Z = ("zh", "zl")
 
 
 def tail_kernel(gram_ref, gramt_ref, pieces_ref, m1_ref, m2_ref, first_ref, second_ref, step_ref):
@@ -125,10 +125,12 @@
     own_context = contexts[0]
     own_cotangent = cotangents[0]
     rank_width = adapter.shape[1] // 2
-    piece = gather_rows(adapter, "z")
+    piece = gather_rows(adapter, "zl")
+    piece = gather_rows(piece, "zh").reshape((-1,) + adapter.shape)
     piece = gather_rows(piece, "x").reshape(-1, adapter.shape[1])
     piece = double(piece, "core", 0)
-    zs, xs, cs = (lax.axis_size(a) for a in FSDP)
+    zs = lax.axis_size("zh") * lax.axis_size("zl")
+    xs, cs = lax.axis_size("x"), lax.axis_size("core")
     blocks_in = piece.reshape(cs, xs, zs, -1, piece.shape[1])
     piece = blocks_in.transpose(2, 1, 0, 3, 4).reshape(piece.shape)
     low = jnp.dot(own_context, piece[:, :rank_width], preferred_element_type=jnp.float32).astype(jnp.bfloat16)
@@ -146,7 +148,7 @@
     mine = lax.dynamic_index_in_dim(by_core, me, 1, keepdims=False).reshape(-1, full[1])
     other = lax.dynamic_index_in_dim(by_core, 1 - me, 1, keepdims=False).reshape(-1, full[1])
     grad_rows = mine + lax.ppermute(other, "core", [(0, 1), (1, 0)])
-    grad_rows = lax.psum_scatter(grad_rows, "z", scatter_dimension=0, tiled=True)
+    grad_rows = lax.psum_scatter(grad_rows, Z, scatter_dimension=0, tiled=True)
     tasks = lax.axis_size("task")
     rows, width = grad_rows.shape
     tiles = grad_rows.reshape(xs, rows // xs, tasks, width // tasks).transpose(0, 2, 1, 3)
@@ -158,7 +160,7 @@
         pieces = pieces + tiles[position]
     partial_gram = jnp.einsum("sij,tij->st", pieces, pieces, precision=lax.Precision.HIGHEST)
     gram_matrix = butterfly_sum(partial_gram, "core")
-    for axis in ("x", "z", "task"):
+    for axis in ("x", "zl", "zh", "task"):
         gathered = gather_rows(gram_matrix, axis)
         gram_matrix = gathered[0]
         for position in range(1, gathered.shape[0]):
@@ -168,7 +170,7 @@
 
 def solution(mesh):
     tasks, fsdp = mesh.devices.shape
-    split = Mesh(mesh.devices.reshape(tasks, fsdp // 8, 4, 2), ("task",) + FSDP)
+    split = Mesh(mesh.devices.reshape(tasks, fsdp // 32, 4, 4, 2), ("task",) + FSDP)
     in_specs = (
         P("task", FSDP, None),
         P("task", FSDP, None),

time: 249 us -> 266 us (1.068)
  blocking collectives: 97.6 us -> 116 us
    all_to_all x4 -> x6, blocking collectives: 79.4 us -> 97.5 us  [gather_rows(): return lax.all_to_all(copies, axis, 0, 0, tiled=True)]
where the time goes in v10:
time: 266 us; the launch traced here: 264 us
  blocking collectives  116 us (44%)
  waiting for transfers between devices  90 us (34%)
  local copies, waits for them, and re-layouts  15.1 us (6%)
  between operations  14.2 us (5%)
  other arithmetic  10.2 us (4%)
  starting transfers between devices  9.29 us (3%)
  matrix products  7.53 us (3%)
    all_to_all x6, blocking collectives, gather_rows(): return lax.all_to_all(copies, axis, 0, 0, tiled=True)  97.5 us
    reduce_scatter x1, waiting for transfers between devices, body(): grad_rows = lax.psum_scatter(grad_rows, Z, scatter_dimension=0, tiled=True)  74.8 us
    all_to_all x1, blocking collectives, body(): tiles = lax.all_to_all(tiles, ('x', 'task'), 0, 0, tiled=True)  18.2 us
    all_to_all x1, waiting for transfers between devices, gather_rows(): return lax.all_to_all(copies, axis, 0, 0, tiled=True)  7.3 us
    concatenate x1, local copies, waits for them, and re-layouts, body(): grad_rows = jnp.concatenate([down_part, up_part], axis=1)  5.61 us
  transfers between devices with their start and end apart: 5, of which 5 were waited for; matrix products, arithmetic and copies ran while one was open for 0% of the time, Pallas kernels for 0%

profile of v10, /device:TPU:6, one launch (start us, length us, event | category | flops | bytes accessed | tf_op | source)
XLA Modules:
  0.0 264.4 jit_solution(495580035388370336)
XLA Ops:
  7.2 0.8 broadcast_in_dim.22
  8.1 12.8 %all_to_all.40 = bf16[4,32,256]{2,1,0:T(8,128)(2,1)S(1)} all-to-all(bf16[4,32,256]{2,1,0:T(8,128)(2,1)S(1)} %broadcast_in_dim.22), channel_id=1, replica_groups=mesh['task'=8,'zh'=4,'zl'=4,'x'=4,'core'=2] {'zl'}, dimensions={0} | all-to-all | bytes 131072 | tf_op jit(solution)/shard_map/all_to_all | solution.py:111
  20.9 33.9 %all_to_all.41 = bf16[4,4,32,256]{3,2,1,0:T(8,128)(2,1)S(1)} all-to-all(bf16[4,4,32,256]{3,2,1,0:T(8,128)(2,1)S(1)} %broadcast_in_dim.23), channel_id=1, replica_groups=mesh['task'=8,'zh'=4,'zl'=4,'x'=4,'core'=2] {'zh'}, dimensions={0} | all-to-all | bytes 524288 | tf_op jit(solution)/shard_map/all_to_all | solution.py:111
  54.9 14.2 %all_to_all.42 = bf16[4,16,32,256]{3,2,1,0:T(8,128)(2,1)S(1)} all-to-all(bf16[4,16,32,256]{3,2,1,0:T(8,128)(2,1)S(1)} %broadcast_in_dim.25), channel_id=1, replica_groups=mesh['task'=8,'zh'=4,'zl'=4,'x'=4,'core'=2] {'x'}, dimensions={0} | all-to-all | bytes 2097152 | tf_op jit(solution)/shard_map/all_to_all | solution.py:111
  69.1 1.9 collective-permute-start
  71.0 2.8 %collective-permute-done = bf16[2048,256]{1,0:T(8,128)(2,1)} collective-permute-done((bf16[2048,256]{1,0:T(8,128)(2,1)S(1)}, bf16[2048,256]{1,0:T(8,128)(2,1)}, u32[]{:S(2)}, u32[]{:S(2)}) %collective-permute-start) | collective-permute-done | bytes 1048608 | tf_op jit(solution)/shard_map/ppermute | solution.py:102
  73.8 1.4 broadcast_select_fusion.1
  75.3 1.5 copy.16
  77.3 3.6 %convolution_bitcast_fusion = f32[4096,128]{0,1:T(8,128)} fusion(bf16[1,192,4096]{2,1,0:T(8,128)(2,1)S(1)} %copy-done, bf16[1,192,4096]{2,1,0:T(8,128)(2,1)S(1)} %copy-done.1, bf16[4096,256]{1,0:T(8,128)(2,1)} %bitcast.49), kind=kOutput, calls=%fused_computation | convolution fusion | flops 402677760 | bytes 6291456 | tf_op jit(solution)/shard_map/dot_general | solution.py:141
  80.8 3.6 %convolution_bitcast_fusion.1 = f32[4096,128]{0,1:T(8,128)} fusion(bf16[1,192,4096]{2,1,0:T(8,128)(2,1)S(1)} %copy-done.1, bf16[1,192,4096]{2,1,0:T(8,128)(2,1)S(1)} %copy-done, bf16[4096,256]{1,0:T(8,128)(2,1)} %bitcast.50), kind=kOutput, calls=%fused_computation.1 | convolution fusion | flops 402677760 | bytes 6291456 | tf_op jit(solution)/shard_map/dot_general | solution.py:138
  84.4 4.6 %pad_maximum_fusion = f32[4096,256]{0,1:T(8,128)} fusion(f32[4096,128]{0,1:T(8,128)} %convolution_bitcast_fusion, f32[4096,128]{0,1:T(8,128)} %convolution_bitcast_fusion.1), kind=kLoop, calls=%fused_computation.2 | loop fusion | flops 1048576 | bytes 8388608 | tf_op jit(solution)/shard_map/concatenate | solution.py:144
  89.0 5.6 %copy.17 = f32[4096,256]{1,0:T(8,128)} copy(f32[4096,256]{0,1:T(8,128)} %pad_maximum_fusion) | data formatting | bytes 8388608 | tf_op jit(solution)/shard_map/concatenate | solution.py:144
  94.6 2.5 constant_dynamic-slice_fusion.1
  97.2 2.1 collective-permute-start.1
  99.3 4.0 %collective-permute-done.1 = f32[2048,256]{1,0:T(8,128)S(1)} collective-permute-done((f32[2048,256]{1,0:T(8,128)S(1)}, f32[2048,256]{1,0:T(8,128)S(1)}, u32[]{:S(2)}, u32[]{:S(2)}) %collective-permute-start.1) | collective-permute-done | bytes 2097184 | tf_op jit(solution)/shard_map/ppermute | solution.py:150
  103.3 1.8 bitcast_add_fusion
  105.0 74.8 %reduce-scatter.2.cloned.1.call-done = f32[128,256]{1,0:T(8,128)} async-done(((f32[2048,256]{1,0:T(8,128)}), f32[128,256]{1,0:T(8,128)}) %reduce-scatter.2.cloned.1.call-update) | async-done | bytes 131088 | tf_op jit(solution)/shard_map/reduce_scatter | solution.py:151
  179.8 1.1 reshape.106
  181.3 18.2 %all_to_all.43 = f32[32,1,1024]{2,1,0:T(1,128)S(1)} all-to-all(f32[32,1,1024]{2,1,0:T(1,128)S(1)} %reshape.115), channel_id=1, replica_groups=mesh['task'=8,'zh'=4,'zl'=4,'x'=4,'core'=2] {'x','task'}, dimensions={0} | all-to-all | bytes 262144 | tf_op jit(solution)/shard_map/all_to_all | solution.py:156
  200.0 0.9 reduce.10
  201.6 1.9 collective-permute-start.2
  203.5 1.1 collective-permute-done.2
  204.7 7.8 %all_to_all.44 = f32[4,8,8]{2,1,0:T(8,128)S(1)} all-to-all(f32[4,8,8]{2,1,0:T(8,128)S(1)} %broadcast_in_dim.26), channel_id=1, replica_groups=mesh['task'=8,'zh'=4,'zl'=4,'x'=4,'core'=2] {'x'}, dimensions={0} | all-to-all | bytes 2048 | tf_op jit(solution)/shard_map/all_to_all | solution.py:111
  212.5 9.4 %all_to_all.45 = f32[4,8,8]{2,1,0:T(8,128)S(1)} all-to-all(f32[4,8,8]{2,1,0:T(8,128)S(1)} %broadcast_in_dim.55), channel_id=1, replica_groups=mesh['task'=8,'zh'=4,'zl'=4,'x'=4,'core'=2] {'zl'}, dimensions={0} | all-to-all | bytes 2048 | tf_op jit(solution)/shard_map/all_to_all | solution.py:111
  221.9 19.4 %all_to_all.46 = f32[4,8,8]{2,1,0:T(8,128)S(1)} all-to-all(f32[4,8,8]{2,1,0:T(8,128)S(1)} %broadcast_in_dim.57), channel_id=1, replica_groups=mesh['task'=8,'zh'=4,'zl'=4,'x'=4,'core'=2] {'zh'}, dimensions={0} | all-to-all | bytes 2048 | tf_op jit(solution)/shard_map/all_to_all | solution.py:111
  241.3 0.6 broadcast_in_dim.59
  242.0 3.3 %all-to-all-start.7 = ((f32[8,8,8]{2,1,0:T(8,128)}), f32[8,8,8]{2,1,0:T(8,128)S(1)}, u32[]{:S(2)}, u32[]{:S(2)}) async-start(f32[8,8,8]{2,1,0:T(8,128)} %broadcast_in_dim.59), calls=%async_computation.8 | async-start | bytes 65536 | tf_op jit(solution)/shard_map/all_to_all | solution.py:111
  245.3 0.6 compare_reduce_fusion
  245.9 7.3 %all-to-all-done.7 = f32[8,8,8]{2,1,0:T(8,128)S(1)} async-done(((f32[8,8,8]{2,1,0:T(8,128)}), f32[8,8,8]{2,1,0:T(8,128)S(1)}, u32[]{:S(2)}, u32[]{:S(2)}) %all-to-all-start.7) | async-done | bytes 2080 | tf_op jit(solution)/shard_map/all_to_all | solution.py:111
  253.2 0.7 fusion.22
  254.0 0.6 scatter.6.gram_ref
  255.2 2.4 shard_map.76
  (26 shorter events, 2.9 us)
Async XLA Ops:
  7.2 69.7 %copy-start = (bf16[1,192,4096]{2,1,0:T(8,128)(2,1)S(1)}, bf16[1,192,4096]{2,1,0:T(8,128)(2,1)}, u32[]{:S(2)}) copy-start(bf16[1,192,4096]{2,1,0:T(8,128)(2,1)} %param.10) | copy-start | bytes 4718596
  7.2 172.7 %reduce-scatter.2.cloned.1.call-start = ((), (), s32[]{:S(2)}) async-start(), calls=%async_computation.9 | async-start | bytes 2228224 | tf_op jit(solution)/shard_map/reduce_scatter | solution.py:151
  69.1 4.7 %collective-permute-start = (bf16[2048,256]{1,0:T(8,128)(2,1)S(1)}, bf16[2048,256]{1,0:T(8,128)(2,1)}, u32[]{:S(2)}, u32[]{:S(2)}) collective-permute-start(bf16[2048,256]{1,0:T(8,128)(2,1)S(1)} %bitcast.51), channel_id=1, source_target_pairs={{0,1},{1,0},{2,3},{3,2},{4,5},{5,4},{6,7},{7,6},{8,9},{9,8},{10,11... | collective-permute-start | bytes 3145736 | tf_op jit(solution)/shard_map/ppermute | solution.py:102
  75.3 2.0 copy-start.1
  97.2 6.1 %collective-permute-start.1 = (f32[2048,256]{1,0:T(8,128)S(1)}, f32[2048,256]{1,0:T(8,128)S(1)}, u32[]{:S(2)}, u32[]{:S(2)}) collective-permute-start(f32[2048,256]{1,0:T(8,128)S(1)} %bitcast.52), channel_id=1, source_target_pairs={{0,1},{1,0},{2,3},{3,2},{4,5},{5,4},{6,7},{7,6},{8,9},{9,8},{10,11... | collective-permute-start | bytes 6291464 | tf_op jit(solution)/shard_map/ppermute | solution.py:150
  201.2 54.0 %copy-start.2 = (f32[8,32,32]{2,1,0:T(8,128)}, f32[8,32,32]{2,1,0:T(8,128)S(1)}, u32[]{:S(2)}) copy-start(f32[8,32,32]{2,1,0:T(8,128)S(1)} %slice_add_fusion.pieces_ref) | copy-start | bytes 98308
  201.6 3.1 %collective-permute-start.2 = (f32[8,8]{1,0:T(8,128)S(1)}, f32[8,8]{1,0:T(8,128)S(1)}, u32[]{:S(2)}, u32[]{:S(2)}) collective-permute-start(f32[8,8]{1,0:T(8,128)S(1)} %convolution_bitcast_fusion.2), channel_id=1, source_target_pairs={{0,1},{1,0},{2,3},{3,2},{4,5},{5,4},{6,7},{7,6},{8,9},{9,8},{10,11... | collective-permute-start | bytes 776 | tf_op jit(solution)/shard_map/ppermute | solution.py:119
  242.0 11.3 %all-to-all-start.7 = ((f32[8,8,8]{2,1,0:T(8,128)}), f32[8,8,8]{2,1,0:T(8,128)S(1)}, u32[]{:S(2)}, u32[]{:S(2)}) async-start(f32[8,8,8]{2,1,0:T(8,128)} %broadcast_in_dim.59), calls=%async_computation.8 | async-start | bytes 65536 | tf_op jit(solution)/shard_map/all_to_all | solution.py:111
Sparse Core Ops, SparseCore 0:
  105.2 74.6 reduce-scatter.1

commit v11 on v9

--- a/solution.py
+++ b/solution.py
@@ -139,12 +139,18 @@
     up_part = lax.dot_general(
         own_cotangent, low, (((0,), (0,)), ((), ())), preferred_element_type=jnp.float32
     )
-    grad_rows = jnp.concatenate([down_part, up_part], axis=1)
-    full = grad_rows.shape
-    by_core = grad_rows.reshape(zs * xs, cs, -1, full[1])
     me = lax.axis_index("core")
-    mine = lax.dynamic_index_in_dim(by_core, me, 1, keepdims=False).reshape(-1, full[1])
-    other = lax.dynamic_index_in_dim(by_core, 1 - me, 1, keepdims=False).reshape(-1, full[1])
+
+    def core_half(index):
+        parts = [
+            lax.dynamic_index_in_dim(part.reshape(zs * xs, cs, -1, part.shape[1]), index, 1, keepdims=False)
+            for part in (down_part, up_part)
+        ]
+        joined = jnp.concatenate(parts, axis=-1)
+        return joined.reshape(-1, joined.shape[-1])
+
+    mine = core_half(me)
+    other = core_half(1 - me)
     grad_rows = mine + lax.ppermute(other, "core", [(0, 1), (1, 0)])
     grad_rows = lax.psum_scatter(grad_rows, "z", scatter_dimension=0, tiled=True)
     tasks = lax.axis_size("task")

time: 249 us -> 245 us (0.984)
  other arithmetic: 10.2 us -> 5.59 us
    dot_general x0 -> x2, local copies, waits for them, and re-layouts: none -> 5.8 us  [the longest x1 2.91 us: body(): lax.dot_general(own_cotangent, low, (((0,), (0,)), ((), ())), preferred_e...]
    concatenate x1 -> x0, local copies, waits for them, and re-layouts: 5.61 us -> none  [body(): grad_rows = jnp.concatenate([down_part, up_part], axis=1)]
    concatenate x1, other arithmetic: 4.61 us -> 0.14 us  [core_half(): joined = jnp.concatenate(parts, axis=-1)]
where the time goes in v11:
time: 245 us; the launch traced here: 244 us
  blocking collectives  97.6 us (40%)
  waiting for transfers between devices  91.7 us (37%)
  local copies, waits for them, and re-layouts  15.4 us (6%)
  between operations  14.2 us (6%)
  starting transfers between devices  9.24 us (4%)
  matrix products  7.52 us (3%)
  other arithmetic  5.59 us (2%)
  Pallas kernels  2.45 us (1%)
    all_to_all x4, blocking collectives, gather_rows(): return lax.all_to_all(copies, axis, 0, 0, tiled=True)  79.3 us
    reduce_scatter x1, waiting for transfers between devices, body(): lax.psum_scatter(grad_rows, 'z', scatter_dimension=0, tiled=True)  76.5 us
    all_to_all x1, blocking collectives, body(): tiles = lax.all_to_all(tiles, ('x', 'task'), 0, 0, tiled=True)  18.3 us
    all_to_all x1, waiting for transfers between devices, gather_rows(): return lax.all_to_all(copies, axis, 0, 0, tiled=True)  7.3 us
  transfers between devices with their start and end apart: 5, of which 5 were waited for; matrix products, arithmetic and copies ran while one was open for 0% of the time, Pallas kernels for 0%

profile of v11, /device:TPU:6, one launch (start us, length us, event | category | flops | bytes accessed | tf_op | source)
XLA Modules:
  0.0 243.6 jit_solution(10689216166119597662)
XLA Ops:
  7.2 0.8 broadcast_in_dim.14
  8.1 37.0 %all_to_all.30 = bf16[16,32,256]{2,1,0:T(8,128)(2,1)S(1)} all-to-all(bf16[16,32,256]{2,1,0:T(8,128)(2,1)S(1)} %broadcast_in_dim.14), channel_id=1, replica_groups=mesh['task'=8,'z'=16,'x'=4,'core'=2] {'z'}, dimensions={0} | all-to-all | bytes 524288 | tf_op jit(solution)/shard_map/all_to_all | solution.py:111
  45.2 13.4 %all_to_all.31 = bf16[4,16,32,256]{3,2,1,0:T(8,128)(2,1)S(1)} all-to-all(bf16[4,16,32,256]{3,2,1,0:T(8,128)(2,1)S(1)} %broadcast_in_dim.15), channel_id=1, replica_groups=mesh['task'=8,'z'=16,'x'=4,'core'=2] {'x'}, dimensions={0} | all-to-all | bytes 2097152 | tf_op jit(solution)/shard_map/all_to_all | solution.py:111
  58.6 1.9 collective-permute-start
  60.6 2.8 %collective-permute-done = bf16[2048,256]{1,0:T(8,128)(2,1)} collective-permute-done((bf16[2048,256]{1,0:T(8,128)(2,1)S(1)}, bf16[2048,256]{1,0:T(8,128)(2,1)}, u32[]{:S(2)}, u32[]{:S(2)}) %collective-permute-start) | collective-permute-done | bytes 1048608 | tf_op jit(solution)/shard_map/ppermute | solution.py:102
  63.3 1.4 broadcast_select_fusion.1
  64.8 1.5 copy.17
  66.8 3.6 %convolution_bitcast_fusion = f32[4096,128]{0,1:T(8,128)} fusion(bf16[1,192,4096]{2,1,0:T(8,128)(2,1)S(1)} %copy-done, bf16[1,192,4096]{2,1,0:T(8,128)(2,1)S(1)} %copy-done.1, bf16[4096,256]{1,0:T(8,128)(2,1)} %bitcast.49), kind=kOutput, calls=%fused_computation | convolution fusion | flops 402677760 | bytes 6291456 | tf_op jit(solution)/shard_map/dot_general | solution.py:139
  70.4 3.6 %convolution_bitcast_fusion.1 = f32[4096,128]{0,1:T(8,128)} fusion(bf16[1,192,4096]{2,1,0:T(8,128)(2,1)S(1)} %copy-done.1, bf16[1,192,4096]{2,1,0:T(8,128)(2,1)S(1)} %copy-done, bf16[4096,256]{1,0:T(8,128)(2,1)} %bitcast.50), kind=kOutput, calls=%fused_computation.1 | convolution fusion | flops 402677760 | bytes 6291456 | tf_op jit(solution)/shard_map/dot_general | solution.py:136
  74.0 2.9 %copy.19 = f32[4096,128]{1,0:T(8,128)} copy(f32[4096,128]{0,1:T(8,128)} %convolution_bitcast_fusion) | data formatting | bytes 4194304 | tf_op jit(solution)/shard_map/dot_general | solution.py:139
  76.9 2.9 %copy.18 = f32[4096,128]{1,0:T(8,128)} copy(f32[4096,128]{0,1:T(8,128)} %convolution_bitcast_fusion.1) | data formatting | bytes 4194304 | tf_op jit(solution)/shard_map/dot_general | solution.py:136
  79.8 2.6 %constant_dynamic-slice_fusion.2 = (f32[64,1,32,128]{3,2,1,0:T(8,128)S(1)}, f32[64,1,32,128]{3,2,1,0:T(8,128)S(1)}, f32[64,1,32,128]{3,2,1,0:T(8,128)S(1)}, f32[64,1,32,128]{3,2,1,0:T(8,128)S(1)}) fusion(f32[64,2,32,128]{3,2,1,0:T(8,128)} %bitcast.46, s32[]{:T(128)S(6)} %select_n.24, s32[]{:T(128)S(6)} %select_n.25, f32[64,2,32,128]{3,2,1,0:T(8,128)} %bitcast.47), kind=kLoop, calls=%fused_computation.54 | loop fusion | bytes 8388616 | tf_op jit(solution)/shard_map/jit(dynamic_index_in_dim)/dynamic_slice | solution.py:146
  82.6 2.0 collective-permute-start.1
  84.6 4.0 %collective-permute-done.1 = f32[2048,256]{1,0:T(8,128)S(1)} collective-permute-done((f32[2048,256]{1,0:T(8,128)S(1)}, f32[2048,256]{1,0:T(8,128)S(1)}, u32[]{:S(2)}, u32[]{:S(2)}) %collective-permute-start.1) | collective-permute-done | bytes 2097184 | tf_op jit(solution)/shard_map/ppermute | solution.py:154
  88.6 1.6 maximum_add_fusion
  90.3 76.5 %reduce-scatter.2.cloned.1.call-done = f32[128,256]{1,0:T(8,128)} async-done(((f32[2048,256]{1,0:T(8,128)}), f32[128,256]{1,0:T(8,128)}) %reduce-scatter.2.cloned.1.call-update) | async-done | bytes 131088 | tf_op jit(solution)/shard_map/reduce_scatter | solution.py:155
  166.8 1.1 reshape.111
  168.2 18.3 %all_to_all.32 = f32[32,1,1024]{2,1,0:T(1,128)S(1)} all-to-all(f32[32,1,1024]{2,1,0:T(1,128)S(1)} %reshape.120), channel_id=1, replica_groups=mesh['task'=8,'z'=16,'x'=4,'core'=2] {'x','task'}, dimensions={0} | all-to-all | bytes 262144 | tf_op jit(solution)/shard_map/all_to_all | solution.py:160
  186.5 0.5 broadcast.62
  187.0 0.9 reduce.10
  188.6 1.9 collective-permute-start.2
  190.5 1.1 collective-permute-done.2
  191.7 7.8 %all_to_all.33 = f32[4,8,8]{2,1,0:T(8,128)S(1)} all-to-all(f32[4,8,8]{2,1,0:T(8,128)S(1)} %broadcast_in_dim.16), channel_id=1, replica_groups=mesh['task'=8,'z'=16,'x'=4,'core'=2] {'x'}, dimensions={0} | all-to-all | bytes 2048 | tf_op jit(solution)/shard_map/all_to_all | solution.py:111
  199.5 21.0 %all_to_all.34 = f32[16,8,8]{2,1,0:T(8,128)S(1)} all-to-all(f32[16,8,8]{2,1,0:T(8,128)S(1)} %broadcast_in_dim.18), channel_id=1, replica_groups=mesh['task'=8,'z'=16,'x'=4,'core'=2] {'z'}, dimensions={0} | all-to-all | bytes 8192 | tf_op jit(solution)/shard_map/all_to_all | solution.py:111
  220.5 0.6 broadcast_in_dim.40
  221.2 3.3 %all-to-all-start.5 = ((f32[8,8,8]{2,1,0:T(8,128)}), f32[8,8,8]{2,1,0:T(8,128)S(1)}, u32[]{:S(2)}, u32[]{:S(2)}) async-start(f32[8,8,8]{2,1,0:T(8,128)} %broadcast_in_dim.40), calls=%async_computation.6 | async-start | bytes 65536 | tf_op jit(solution)/shard_map/all_to_all | solution.py:111
  224.5 0.6 compare_reduce_fusion
  225.1 7.3 %all-to-all-done.5 = f32[8,8,8]{2,1,0:T(8,128)S(1)} async-done(((f32[8,8,8]{2,1,0:T(8,128)}), f32[8,8,8]{2,1,0:T(8,128)S(1)}, u32[]{:S(2)}, u32[]{:S(2)}) %all-to-all-start.5) | async-done | bytes 2080 | tf_op jit(solution)/shard_map/all_to_all | solution.py:111
  232.4 0.7 fusion.22
  233.2 0.6 scatter.6.gram_ref
  233.8 0.6 scatter.9.gramt_ref
  234.3 2.4 %shard_map.76 = (f32[32,32]{1,0:T(8,128)}, f32[32,32]{1,0:T(8,128)}, f32[32,32]{1,0:T(8,128)}) custom-call(f32[8,128]{1,0:T(8,128)} %scatter.6.gram_ref, f32[8,128]{1,0:T(8,128)} %scatter.9.gramt_ref, f32[8,32,32]{2,1,0:T(8,128)} %copy-done.2, f32[32,32]{1,0:T(8,128)} %m1_ref.1, f32[32,32]{1,0:T(8,128)} %m2_ref.1), custom_call_target="tpu_custom_call" | custom-call | tf_op jit(solution)/shard_map/pallas_call | solution.py:83
  (22 shorter events, 2.0 us)
Async XLA Ops:
  7.2 59.2 %copy-start = (bf16[1,192,4096]{2,1,0:T(8,128)(2,1)S(1)}, bf16[1,192,4096]{2,1,0:T(8,128)(2,1)}, u32[]{:S(2)}) copy-start(bf16[1,192,4096]{2,1,0:T(8,128)(2,1)} %param.10) | copy-start | bytes 4718596
  7.2 159.6 %reduce-scatter.2.cloned.1.call-start = ((), (), s32[]{:S(2)}) async-start(), calls=%async_computation.7 | async-start | bytes 2228224 | tf_op jit(solution)/shard_map/reduce_scatter | solution.py:155
  58.6 4.7 %collective-permute-start = (bf16[2048,256]{1,0:T(8,128)(2,1)S(1)}, bf16[2048,256]{1,0:T(8,128)(2,1)}, u32[]{:S(2)}, u32[]{:S(2)}) collective-permute-start(bf16[2048,256]{1,0:T(8,128)(2,1)S(1)} %bitcast.51), channel_id=1, source_target_pairs={{0,1},{1,0},{2,3},{3,2},{4,5},{5,4},{6,7},{7,6},{8,9},{9,8},{10,11... | collective-permute-start | bytes 3145736 | tf_op jit(solution)/shard_map/ppermute | solution.py:102
  64.8 2.0 copy-start.1
  82.6 6.1 %collective-permute-start.1 = (f32[2048,256]{1,0:T(8,128)S(1)}, f32[2048,256]{1,0:T(8,128)S(1)}, u32[]{:S(2)}, u32[]{:S(2)}) collective-permute-start(f32[2048,256]{1,0:T(8,128)S(1)} %pad_maximum_fusion.1), channel_id=1, source_target_pairs={{0,1},{1,0},{2,3},{3,2},{4,5},{5,4},{6,7},{7,6},{8,9},{9,8},{10,11... | collective-permute-start | bytes 6291464 | tf_op jit(solution)/shard_map/ppermute | solution.py:154
  188.2 46.2 %copy-start.2 = (f32[8,32,32]{2,1,0:T(8,128)}, f32[8,32,32]{2,1,0:T(8,128)S(1)}, u32[]{:S(2)}) copy-start(f32[8,32,32]{2,1,0:T(8,128)S(1)} %slice_add_fusion.pieces_ref) | copy-start | bytes 98308
  188.6 3.1 %collective-permute-start.2 = (f32[8,8]{1,0:T(8,128)S(1)}, f32[8,8]{1,0:T(8,128)S(1)}, u32[]{:S(2)}, u32[]{:S(2)}) collective-permute-start(f32[8,8]{1,0:T(8,128)S(1)} %convolution_bitcast_fusion.2), channel_id=1, source_target_pairs={{0,1},{1,0},{2,3},{3,2},{4,5},{5,4},{6,7},{7,6},{8,9},{9,8},{10,11... | collective-permute-start | bytes 776 | tf_op jit(solution)/shard_map/ppermute | solution.py:119
  221.2 11.3 %all-to-all-start.5 = ((f32[8,8,8]{2,1,0:T(8,128)}), f32[8,8,8]{2,1,0:T(8,128)S(1)}, u32[]{:S(2)}, u32[]{:S(2)}) async-start(f32[8,8,8]{2,1,0:T(8,128)} %broadcast_in_dim.40), calls=%async_computation.6 | async-start | bytes 65536 | tf_op jit(solution)/shard_map/all_to_all | solution.py:111
Sparse Core Ops, SparseCore 0:
  90.4 76.3 reduce-scatter.1

commit v12 on v11

--- a/solution.py
+++ b/solution.py
@@ -106,7 +106,8 @@
 
 
 def gather_rows(value, axis):
-    size = lax.axis_size(axis)
+    names = axis if isinstance(axis, tuple) else (axis,)
+    size = math.prod(lax.axis_size(name) for name in names)
     copies = jnp.broadcast_to(value[None], (size,) + value.shape)
     return lax.all_to_all(copies, axis, 0, 0, tiled=True)
 
@@ -126,11 +127,10 @@
     own_cotangent = cotangents[0]
     rank_width = adapter.shape[1] // 2
     piece = gather_rows(adapter, "z")
-    piece = gather_rows(piece, "x").reshape(-1, adapter.shape[1])
-    piece = double(piece, "core", 0)
+    piece = gather_rows(piece, ("x", "core"))
     zs, xs, cs = (lax.axis_size(a) for a in FSDP)
-    blocks_in = piece.reshape(cs, xs, zs, -1, piece.shape[1])
-    piece = blocks_in.transpose(2, 1, 0, 3, 4).reshape(piece.shape)
+    blocks_in = piece.reshape((xs, cs, zs) + adapter.shape)
+    piece = blocks_in.transpose(2, 0, 1, 3, 4).reshape(-1, adapter.shape[1])
     low = jnp.dot(own_context, piece[:, :rank_width], preferred_element_type=jnp.float32).astype(jnp.bfloat16)
     back = jnp.dot(own_cotangent, piece[:, rank_width:], preferred_element_type=jnp.float32).astype(jnp.bfloat16)
     down_part = lax.dot_general(
@@ -163,8 +163,8 @@
     for position in range(1, xs):
         pieces = pieces + tiles[position]
     partial_gram = jnp.einsum("sij,tij->st", pieces, pieces, precision=lax.Precision.HIGHEST)
-    gram_matrix = butterfly_sum(partial_gram, "core")
-    for axis in ("x", "z", "task"):
+    gram_matrix = partial_gram
+    for axis in (("x", "core"), "z", "task"):
         gathered = gather_rows(gram_matrix, axis)
         gram_matrix = gathered[0]
         for position in range(1, gathered.shape[0]):

time: 245 us -> 251 us (1.024)
  waiting for transfers between devices: 91.7 us -> 109 us
  blocking collectives: 97.6 us -> 84.3 us
  local copies, waits for them, and re-layouts: 15.4 us -> 18 us
    all_to_all x1 -> x2, waiting for transfers between devices: 7.3 us -> 32.5 us  [gather_rows(): return lax.all_to_all(copies, axis, 0, 0, tiled=True)]
    all_to_all x4 -> x3, blocking collectives: 79.3 us -> 66 us  [gather_rows(): return lax.all_to_all(copies, axis, 0, 0, tiled=True)]
    all_to_all x1 -> x2, starting transfers between devices: 3.32 us -> 8.1 us  [gather_rows(): return lax.all_to_all(copies, axis, 0, 0, tiled=True)]
    reduce_scatter x1, waiting for transfers between devices: 76.5 us -> 72.6 us  [body(): lax.psum_scatter(grad_rows, 'z', scatter_dimension=0, tiled=True)]
    ppermute x2 -> x0, waiting for transfers between devices: 3.88 us -> none  [the longest x1 2.75 us: double(): other = lax.ppermute(value, axis, pairs)]
    ppermute x2 -> x0, starting transfers between devices: 3.86 us -> none  [the longest x1 1.95 us: butterfly_sum(): value = value + lax.ppermute(value, axis, pairs)]
    all_to_all x0 -> x1, local copies, waits for them, and re-layouts: none -> 3.14 us  [gather_rows(): return lax.all_to_all(copies, axis, 0, 0, tiled=True)]
  transfers between devices with their start and end apart: 5 -> 4, of which waited for: 5 -> 4; matrix products, arithmetic and copies ran while one was open for 0% -> 0% of each run, Pallas kernels for 0% -> 0%
where the time goes in v12:
time: 251 us; the launch traced here: 250 us
  waiting for transfers between devices  109 us (43%)
  blocking collectives  84.3 us (34%)
  local copies, waits for them, and re-layouts  18 us (7%)
  between operations  14.1 us (6%)
  starting transfers between devices  10 us (4%)
  matrix products  7.53 us (3%)
  other arithmetic  4.09 us (2%)
    reduce_scatter x1, waiting for transfers between devices, body(): lax.psum_scatter(grad_rows, 'z', scatter_dimension=0, tiled=True)  72.6 us
    all_to_all x3, blocking collectives, gather_rows(): return lax.all_to_all(copies, axis, 0, 0, tiled=True)  66 us
    all_to_all x2, waiting for transfers between devices, gather_rows(): return lax.all_to_all(copies, axis, 0, 0, tiled=True)  32.5 us
    all_to_all x1, blocking collectives, body(): tiles = lax.all_to_all(tiles, ('x', 'task'), 0, 0, tiled=True)  18.3 us
    all_to_all x2, starting transfers between devices, gather_rows(): return lax.all_to_all(copies, axis, 0, 0, tiled=True)  8.1 us
  transfers between devices with their start and end apart: 4, of which 4 were waited for; matrix products, arithmetic and copies ran while one was open for 0% of the time, Pallas kernels for 0%

profile of v12, /device:TPU:6, one launch (start us, length us, event | category | flops | bytes accessed | tf_op | source)
XLA Modules:
  0.0 249.7 jit_solution(5827563317565015632)
XLA Ops:
  7.2 0.9 broadcast_in_dim.14
  8.0 37.0 %all_to_all.30 = bf16[16,32,256]{2,1,0:T(8,128)(2,1)S(1)} all-to-all(bf16[16,32,256]{2,1,0:T(8,128)(2,1)S(1)} %broadcast_in_dim.14), channel_id=1, replica_groups=mesh['task'=8,'z'=16,'x'=4,'core'=2] {'z'}, dimensions={0} | all-to-all | bytes 524288 | tf_op jit(solution)/shard_map/all_to_all | solution.py:112
  45.1 1.6 broadcast_in_dim.15
  46.7 4.8 %all-to-all-start.1 = ((bf16[8,16,32,256]{3,2,1,0:T(8,128)(2,1)}), bf16[8,16,32,256]{3,2,1,0:T(8,128)(2,1)}, u32[]{:S(2)}, u32[]{:S(2)}) async-start(bf16[8,16,32,256]{3,2,1,0:T(8,128)(2,1)} %broadcast_in_dim.15), calls=%async_computation.1 | async-start | bytes 4194304 | tf_op jit(solution)/shard_map/all_to_all | solution.py:112
  51.4 25.2 %all-to-all-done.1 = bf16[8,16,32,256]{3,2,1,0:T(8,128)(2,1)} async-done(((bf16[8,16,32,256]{3,2,1,0:T(8,128)(2,1)}), bf16[8,16,32,256]{3,2,1,0:T(8,128)(2,1)}, u32[]{:S(2)}, u32[]{:S(2)}) %all-to-all-start.1) | async-done | bytes 2097184 | tf_op jit(solution)/shard_map/all_to_all | solution.py:112
  76.6 3.1 %copy.17 = bf16[8,16,32,256]{3,2,0,1:T(8,128)(2,1)} copy(bf16[8,16,32,256]{3,2,1,0:T(8,128)(2,1)} %all-to-all-done.1) | data formatting | bytes 4194304 | tf_op jit(solution)/shard_map/all_to_all | solution.py:112
  79.8 3.5 %convolution_bitcast_fusion = f32[4096,128]{0,1:T(8,128)} fusion(bf16[1,192,4096]{2,1,0:T(8,128)(2,1)S(1)} %copy-done, bf16[1,192,4096]{2,1,0:T(8,128)(2,1)S(1)} %copy-done.1, bf16[4096,256]{1,0:T(8,128)(2,1)} %bitcast.46), kind=kOutput, calls=%fused_computation | convolution fusion | flops 402677760 | bytes 6291456 | tf_op jit(solution)/shard_map/dot_general | solution.py:139
  83.3 3.6 %convolution_bitcast_fusion.1 = f32[4096,128]{0,1:T(8,128)} fusion(bf16[1,192,4096]{2,1,0:T(8,128)(2,1)S(1)} %copy-done.1, bf16[1,192,4096]{2,1,0:T(8,128)(2,1)S(1)} %copy-done, bf16[4096,256]{1,0:T(8,128)(2,1)} %bitcast.47), kind=kOutput, calls=%fused_computation.1 | convolution fusion | flops 402677760 | bytes 6291456 | tf_op jit(solution)/shard_map/dot_general | solution.py:136
  86.9 2.9 %copy.19 = f32[4096,128]{1,0:T(8,128)} copy(f32[4096,128]{0,1:T(8,128)} %convolution_bitcast_fusion) | data formatting | bytes 4194304 | tf_op jit(solution)/shard_map/dot_general | solution.py:139
  89.8 2.9 %copy.18 = f32[4096,128]{1,0:T(8,128)} copy(f32[4096,128]{0,1:T(8,128)} %convolution_bitcast_fusion.1) | data formatting | bytes 4194304 | tf_op jit(solution)/shard_map/dot_general | solution.py:136
  92.7 2.6 %constant_dynamic-slice_fusion.2 = (f32[64,1,32,128]{3,2,1,0:T(8,128)S(1)}, f32[64,1,32,128]{3,2,1,0:T(8,128)S(1)}, f32[64,1,32,128]{3,2,1,0:T(8,128)S(1)}, f32[64,1,32,128]{3,2,1,0:T(8,128)S(1)}) fusion(f32[64,2,32,128]{3,2,1,0:T(8,128)} %bitcast.44, s32[]{:T(128)S(6)} %select_n.9, s32[]{:T(128)S(6)} %select_n.10, f32[64,2,32,128]{3,2,1,0:T(8,128)} %bitcast.45), kind=kLoop, calls=%fused_computation.55 | loop fusion | bytes 8388616 | tf_op jit(solution)/shard_map/jit(dynamic_index_in_dim)/dynamic_slice | solution.py:146
  95.5 1.9 collective-permute-start
  97.4 4.1 %collective-permute-done = f32[2048,256]{1,0:T(8,128)S(1)} collective-permute-done((f32[2048,256]{1,0:T(8,128)S(1)}, f32[2048,256]{1,0:T(8,128)S(1)}, u32[]{:S(2)}, u32[]{:S(2)}) %collective-permute-start) | collective-permute-done | bytes 2097184 | tf_op jit(solution)/shard_map/ppermute | solution.py:154
  101.6 1.6 maximum_add_fusion
  103.2 72.6 %reduce-scatter.2.cloned.1.call-done = f32[128,256]{1,0:T(8,128)} async-done(((f32[2048,256]{1,0:T(8,128)}), f32[128,256]{1,0:T(8,128)}) %reduce-scatter.2.cloned.1.call-update) | async-done | bytes 131088 | tf_op jit(solution)/shard_map/reduce_scatter | solution.py:155
  175.8 1.1 reshape.107
  177.0 0.3 reshape.116
  177.2 18.3 %all_to_all.31 = f32[32,1,1024]{2,1,0:T(1,128)S(1)} all-to-all(f32[32,1,1024]{2,1,0:T(1,128)S(1)} %reshape.116), channel_id=1, replica_groups=mesh['task'=8,'z'=16,'x'=4,'core'=2] {'x','task'}, dimensions={0} | all-to-all | bytes 262144 | tf_op jit(solution)/shard_map/all_to_all | solution.py:160
  195.5 0.5 broadcast.62
  196.0 0.9 reduce.10
  197.0 0.2 reshape.117
  197.2 0.4 convolution_bitcast_fusion.2
  197.6 8.0 %all_to_all.32 = f32[8,8,8]{2,1,0:T(8,128)S(1)} all-to-all(f32[8,8,8]{2,1,0:T(8,128)S(1)} %broadcast_in_dim.16), channel_id=1, replica_groups=mesh['task'=8,'z'=16,'x'=4,'core'=2] {'x','core'}, dimensions={0} | all-to-all | bytes 4096 | tf_op jit(solution)/shard_map/all_to_all | solution.py:112
  205.6 21.0 %all_to_all.33 = f32[16,8,8]{2,1,0:T(8,128)S(1)} all-to-all(f32[16,8,8]{2,1,0:T(8,128)S(1)} %broadcast_in_dim.18), channel_id=1, replica_groups=mesh['task'=8,'z'=16,'x'=4,'core'=2] {'z'}, dimensions={0} | all-to-all | bytes 8192 | tf_op jit(solution)/shard_map/all_to_all | solution.py:112
  226.6 0.6 broadcast_in_dim.40
  227.2 3.3 %all-to-all-start.5 = ((f32[8,8,8]{2,1,0:T(8,128)}), f32[8,8,8]{2,1,0:T(8,128)S(1)}, u32[]{:S(2)}, u32[]{:S(2)}) async-start(f32[8,8,8]{2,1,0:T(8,128)} %broadcast_in_dim.40), calls=%async_computation.6 | async-start | bytes 65536 | tf_op jit(solution)/shard_map/all_to_all | solution.py:112
  230.5 0.6 compare_reduce_fusion
  231.1 7.3 %all-to-all-done.5 = f32[8,8,8]{2,1,0:T(8,128)S(1)} async-done(((f32[8,8,8]{2,1,0:T(8,128)}), f32[8,8,8]{2,1,0:T(8,128)S(1)}, u32[]{:S(2)}, u32[]{:S(2)}) %all-to-all-start.5) | async-done | bytes 2080 | tf_op jit(solution)/shard_map/all_to_all | solution.py:112
  238.5 0.7 fusion.22
  239.2 0.6 scatter.6.gram_ref
  239.8 0.6 scatter.9.gramt_ref
  240.4 2.4 shard_map.76
  (16 shorter events, 0.4 us)
Async XLA Ops:
  7.2 72.6 %copy-start = (bf16[1,192,4096]{2,1,0:T(8,128)(2,1)S(1)}, bf16[1,192,4096]{2,1,0:T(8,128)(2,1)}, u32[]{:S(2)}) copy-start(bf16[1,192,4096]{2,1,0:T(8,128)(2,1)} %param.10) | copy-start | bytes 4718596
  46.7 30.0 %all-to-all-start.1 = ((bf16[8,16,32,256]{3,2,1,0:T(8,128)(2,1)}), bf16[8,16,32,256]{3,2,1,0:T(8,128)(2,1)}, u32[]{:S(2)}, u32[]{:S(2)}) async-start(bf16[8,16,32,256]{3,2,1,0:T(8,128)(2,1)} %broadcast_in_dim.15), calls=%async_computation.1 | async-start | bytes 4194304 | tf_op jit(solution)/shard_map/all_to_all | solution.py:112
  51.4 124.3 %reduce-scatter.2.cloned.1.call-start = ((), (), s32[]{:S(2)}) async-start(), calls=%async_computation.7 | async-start | bytes 2228224 | tf_op jit(solution)/shard_map/reduce_scatter | solution.py:155
  51.4 28.4 %copy-start.1 = (bf16[1,192,4096]{2,1,0:T(8,128)(2,1)S(1)}, bf16[1,192,4096]{2,1,0:T(8,128)(2,1)}, u32[]{:S(2)}) copy-start(bf16[1,192,4096]{2,1,0:T(8,128)(2,1)} %param.9) | copy-start | bytes 4718596
  95.5 6.1 %collective-permute-start = (f32[2048,256]{1,0:T(8,128)S(1)}, f32[2048,256]{1,0:T(8,128)S(1)}, u32[]{:S(2)}, u32[]{:S(2)}) collective-permute-start(f32[2048,256]{1,0:T(8,128)S(1)} %pad_maximum_fusion), channel_id=1, source_target_pairs={{0,1},{1,0},{2,3},{3,2},{4,5},{5,4},{6,7},{7,6},{8,9},{9,8},{10,11... | collective-permute-start | bytes 6291464 | tf_op jit(solution)/shard_map/ppermute | solution.py:154
  197.2 43.2 %copy-start.2 = (f32[8,32,32]{2,1,0:T(8,128)}, f32[8,32,32]{2,1,0:T(8,128)S(1)}, u32[]{:S(2)}) copy-start(f32[8,32,32]{2,1,0:T(8,128)S(1)} %slice_add_fusion.pieces_ref) | copy-start | bytes 98308
  227.2 11.3 %all-to-all-start.5 = ((f32[8,8,8]{2,1,0:T(8,128)}), f32[8,8,8]{2,1,0:T(8,128)S(1)}, u32[]{:S(2)}, u32[]{:S(2)}) async-start(f32[8,8,8]{2,1,0:T(8,128)} %broadcast_in_dim.40), calls=%async_computation.6 | async-start | bytes 65536 | tf_op jit(solution)/shard_map/all_to_all | solution.py:112
Sparse Core Ops, SparseCore 0:
  103.4 72.3 reduce-scatter.1

commit v13 on v12

--- a/solution.py
+++ b/solution.py
@@ -127,10 +127,11 @@
     own_cotangent = cotangents[0]
     rank_width = adapter.shape[1] // 2
     piece = gather_rows(adapter, "z")
-    piece = gather_rows(piece, ("x", "core"))
+    piece = gather_rows(piece, "x").reshape(-1, adapter.shape[1])
+    piece = double(piece, "core", 0)
     zs, xs, cs = (lax.axis_size(a) for a in FSDP)
-    blocks_in = piece.reshape((xs, cs, zs) + adapter.shape)
-    piece = blocks_in.transpose(2, 0, 1, 3, 4).reshape(-1, adapter.shape[1])
+    blocks_in = piece.reshape(cs, xs, zs, -1, piece.shape[1])
+    piece = blocks_in.transpose(2, 1, 0, 3, 4).reshape(piece.shape)
     low = jnp.dot(own_context, piece[:, :rank_width], preferred_element_type=jnp.float32).astype(jnp.bfloat16)
     back = jnp.dot(own_cotangent, piece[:, rank_width:], preferred_element_type=jnp.float32).astype(jnp.bfloat16)
     down_part = lax.dot_general(

time: 251 us -> 242 us (0.964)
  waiting for transfers between devices: 109 us -> 90.6 us
  blocking collectives: 84.3 us -> 97.6 us
  starting transfers between devices: 10 us -> 7.29 us
  local copies, waits for them, and re-layouts: 18 us -> 15.4 us
    all_to_all x2 -> x1, waiting for transfers between devices: 32.5 us -> 7.3 us  [gather_rows(): return lax.all_to_all(copies, axis, 0, 0, tiled=True)]
    all_to_all x3 -> x4, blocking collectives: 66 us -> 79.5 us  [gather_rows(): return lax.all_to_all(copies, axis, 0, 0, tiled=True)]
    all_to_all x2 -> x1, starting transfers between devices: 8.1 us -> 3.33 us  [gather_rows(): return lax.all_to_all(copies, axis, 0, 0, tiled=True)]
    reduce_scatter x1, waiting for transfers between devices: 72.6 us -> 76.5 us  [body(): lax.psum_scatter(grad_rows, 'z', scatter_dimension=0, tiled=True)]
    all_to_all x1 -> x0, local copies, waits for them, and re-layouts: 3.14 us -> none  [gather_rows(): return lax.all_to_all(copies, axis, 0, 0, tiled=True)]
    ppermute x0 -> x1, waiting for transfers between devices: none -> 2.75 us  [double(): other = lax.ppermute(value, axis, pairs)]
where the time goes in v13:
time: 242 us; the launch traced here: 241 us
  blocking collectives  97.6 us (40%)
  waiting for transfers between devices  90.6 us (37%)
  local copies, waits for them, and re-layouts  15.4 us (6%)
  between operations  14.2 us (6%)
  matrix products  7.55 us (3%)
  starting transfers between devices  7.29 us (3%)
  other arithmetic  5.59 us (2%)
  Pallas kernels  2.45 us (1%)
    all_to_all x4, blocking collectives, gather_rows(): return lax.all_to_all(copies, axis, 0, 0, tiled=True)  79.5 us
    reduce_scatter x1, waiting for transfers between devices, body(): lax.psum_scatter(grad_rows, 'z', scatter_dimension=0, tiled=True)  76.5 us
    all_to_all x1, blocking collectives, body(): tiles = lax.all_to_all(tiles, ('x', 'task'), 0, 0, tiled=True)  18.1 us
    all_to_all x1, waiting for transfers between devices, gather_rows(): return lax.all_to_all(copies, axis, 0, 0, tiled=True)  7.3 us
  transfers between devices with their start and end apart: 4, of which 4 were waited for; matrix products, arithmetic and copies ran while one was open for 0% of the time, Pallas kernels for 0%

profile of v13, /device:TPU:6, one launch (start us, length us, event | category | flops | bytes accessed | tf_op | source)
XLA Modules:
  0.0 240.6 jit_solution(12292660281568931170)
XLA Ops:
  7.2 0.8 broadcast_in_dim.14
  8.1 37.0 %all_to_all.30 = bf16[16,32,256]{2,1,0:T(8,128)(2,1)S(1)} all-to-all(bf16[16,32,256]{2,1,0:T(8,128)(2,1)S(1)} %broadcast_in_dim.14), channel_id=1, replica_groups=mesh['task'=8,'z'=16,'x'=4,'core'=2] {'z'}, dimensions={0} | all-to-all | bytes 524288 | tf_op jit(solution)/shard_map/all_to_all | solution.py:112
  45.2 13.4 %all_to_all.31 = bf16[4,16,32,256]{3,2,1,0:T(8,128)(2,1)S(1)} all-to-all(bf16[4,16,32,256]{3,2,1,0:T(8,128)(2,1)S(1)} %broadcast_in_dim.15), channel_id=1, replica_groups=mesh['task'=8,'z'=16,'x'=4,'core'=2] {'x'}, dimensions={0} | all-to-all | bytes 2097152 | tf_op jit(solution)/shard_map/all_to_all | solution.py:112
  58.6 1.9 collective-permute-start
  60.6 2.8 %collective-permute-done = bf16[2048,256]{1,0:T(8,128)(2,1)} collective-permute-done((bf16[2048,256]{1,0:T(8,128)(2,1)S(1)}, bf16[2048,256]{1,0:T(8,128)(2,1)}, u32[]{:S(2)}, u32[]{:S(2)}) %collective-permute-start) | collective-permute-done | bytes 1048608 | tf_op jit(solution)/shard_map/ppermute | solution.py:102
  63.3 1.4 broadcast_select_fusion.1
  64.8 1.5 copy.17
  66.4 0.5 copy-done.1
  66.8 3.6 %convolution_bitcast_fusion = f32[4096,128]{0,1:T(8,128)} fusion(bf16[1,192,4096]{2,1,0:T(8,128)(2,1)S(1)} %copy-done, bf16[1,192,4096]{2,1,0:T(8,128)(2,1)S(1)} %copy-done.1, bf16[4096,256]{1,0:T(8,128)(2,1)} %bitcast.49), kind=kOutput, calls=%fused_computation | convolution fusion | flops 402677760 | bytes 6291456 | tf_op jit(solution)/shard_map/dot_general | solution.py:140
  70.4 3.6 %convolution_bitcast_fusion.1 = f32[4096,128]{0,1:T(8,128)} fusion(bf16[1,192,4096]{2,1,0:T(8,128)(2,1)S(1)} %copy-done.1, bf16[1,192,4096]{2,1,0:T(8,128)(2,1)S(1)} %copy-done, bf16[4096,256]{1,0:T(8,128)(2,1)} %bitcast.50), kind=kOutput, calls=%fused_computation.1 | convolution fusion | flops 402677760 | bytes 6291456 | tf_op jit(solution)/shard_map/dot_general | solution.py:137
  74.0 2.9 %copy.19 = f32[4096,128]{1,0:T(8,128)} copy(f32[4096,128]{0,1:T(8,128)} %convolution_bitcast_fusion) | data formatting | bytes 4194304 | tf_op jit(solution)/shard_map/dot_general | solution.py:140
  76.9 2.9 %copy.18 = f32[4096,128]{1,0:T(8,128)} copy(f32[4096,128]{0,1:T(8,128)} %convolution_bitcast_fusion.1) | data formatting | bytes 4194304 | tf_op jit(solution)/shard_map/dot_general | solution.py:137
  79.8 2.6 %constant_dynamic-slice_fusion.2 = (f32[64,1,32,128]{3,2,1,0:T(8,128)S(1)}, f32[64,1,32,128]{3,2,1,0:T(8,128)S(1)}, f32[64,1,32,128]{3,2,1,0:T(8,128)S(1)}, f32[64,1,32,128]{3,2,1,0:T(8,128)S(1)}) fusion(f32[64,2,32,128]{3,2,1,0:T(8,128)} %bitcast.46, s32[]{:T(128)S(6)} %select_n.24, s32[]{:T(128)S(6)} %select_n.25, f32[64,2,32,128]{3,2,1,0:T(8,128)} %bitcast.47), kind=kLoop, calls=%fused_computation.58 | loop fusion | bytes 8388616 | tf_op jit(solution)/shard_map/jit(dynamic_index_in_dim)/dynamic_slice | solution.py:147
  82.6 2.0 collective-permute-start.1
  84.6 4.0 %collective-permute-done.1 = f32[2048,256]{1,0:T(8,128)S(1)} collective-permute-done((f32[2048,256]{1,0:T(8,128)S(1)}, f32[2048,256]{1,0:T(8,128)S(1)}, u32[]{:S(2)}, u32[]{:S(2)}) %collective-permute-start.1) | collective-permute-done | bytes 2097184 | tf_op jit(solution)/shard_map/ppermute | solution.py:155
  88.6 1.6 maximum_add_fusion
  90.3 76.5 %reduce-scatter.2.cloned.1.call-done = f32[128,256]{1,0:T(8,128)} async-done(((f32[2048,256]{1,0:T(8,128)}), f32[128,256]{1,0:T(8,128)}) %reduce-scatter.2.cloned.1.call-update) | async-done | bytes 131088 | tf_op jit(solution)/shard_map/reduce_scatter | solution.py:156
  166.8 1.1 reshape.111
  168.2 18.1 %all_to_all.32 = f32[32,1,1024]{2,1,0:T(1,128)S(1)} all-to-all(f32[32,1,1024]{2,1,0:T(1,128)S(1)} %reshape.120), channel_id=1, replica_groups=mesh['task'=8,'z'=16,'x'=4,'core'=2] {'x','task'}, dimensions={0} | all-to-all | bytes 262144 | tf_op jit(solution)/shard_map/all_to_all | solution.py:161
  186.3 0.5 broadcast.62
  186.8 0.9 reduce.10
  188.0 0.4 convolution_bitcast_fusion.2
  188.4 8.0 %all_to_all.33 = f32[8,8,8]{2,1,0:T(8,128)S(1)} all-to-all(f32[8,8,8]{2,1,0:T(8,128)S(1)} %broadcast_in_dim.16), channel_id=1, replica_groups=mesh['task'=8,'z'=16,'x'=4,'core'=2] {'x','core'}, dimensions={0} | all-to-all | bytes 4096 | tf_op jit(solution)/shard_map/all_to_all | solution.py:112
  196.4 21.1 %all_to_all.34 = f32[16,8,8]{2,1,0:T(8,128)S(1)} all-to-all(f32[16,8,8]{2,1,0:T(8,128)S(1)} %broadcast_in_dim.18), channel_id=1, replica_groups=mesh['task'=8,'z'=16,'x'=4,'core'=2] {'z'}, dimensions={0} | all-to-all | bytes 8192 | tf_op jit(solution)/shard_map/all_to_all | solution.py:112
  217.5 0.6 broadcast_in_dim.40
  218.1 3.3 %all-to-all-start.5 = ((f32[8,8,8]{2,1,0:T(8,128)}), f32[8,8,8]{2,1,0:T(8,128)S(1)}, u32[]{:S(2)}, u32[]{:S(2)}) async-start(f32[8,8,8]{2,1,0:T(8,128)} %broadcast_in_dim.40), calls=%async_computation.6 | async-start | bytes 65536 | tf_op jit(solution)/shard_map/all_to_all | solution.py:112
  221.5 0.6 compare_reduce_fusion
  222.1 7.3 %all-to-all-done.5 = f32[8,8,8]{2,1,0:T(8,128)S(1)} async-done(((f32[8,8,8]{2,1,0:T(8,128)}), f32[8,8,8]{2,1,0:T(8,128)S(1)}, u32[]{:S(2)}, u32[]{:S(2)}) %all-to-all-start.5) | async-done | bytes 2080 | tf_op jit(solution)/shard_map/all_to_all | solution.py:112
  229.4 0.7 fusion.22
  230.1 0.6 scatter.6.gram_ref
  230.7 0.6 scatter.9.gramt_ref
  231.3 2.4 %shard_map.76 = (f32[32,32]{1,0:T(8,128)}, f32[32,32]{1,0:T(8,128)}, f32[32,32]{1,0:T(8,128)}) custom-call(f32[8,128]{1,0:T(8,128)} %scatter.6.gram_ref, f32[8,128]{1,0:T(8,128)} %scatter.9.gramt_ref, f32[8,32,32]{2,1,0:T(8,128)} %copy-done.2, f32[32,32]{1,0:T(8,128)} %m1_ref.1, f32[32,32]{1,0:T(8,128)} %m2_ref.1), custom_call_target="tpu_custom_call" | custom-call | tf_op jit(solution)/shard_map/pallas_call | solution.py:83
  (19 shorter events, 1.1 us)
Async XLA Ops:
  7.2 59.2 %copy-start = (bf16[1,192,4096]{2,1,0:T(8,128)(2,1)S(1)}, bf16[1,192,4096]{2,1,0:T(8,128)(2,1)}, u32[]{:S(2)}) copy-start(bf16[1,192,4096]{2,1,0:T(8,128)(2,1)} %param.10) | copy-start | bytes 4718596
  7.2 159.6 %reduce-scatter.2.cloned.1.call-start = ((), (), s32[]{:S(2)}) async-start(), calls=%async_computation.7 | async-start | bytes 2228224 | tf_op jit(solution)/shard_map/reduce_scatter | solution.py:156
  58.6 4.7 %collective-permute-start = (bf16[2048,256]{1,0:T(8,128)(2,1)S(1)}, bf16[2048,256]{1,0:T(8,128)(2,1)}, u32[]{:S(2)}, u32[]{:S(2)}) collective-permute-start(bf16[2048,256]{1,0:T(8,128)(2,1)S(1)} %bitcast.51), channel_id=1, source_target_pairs={{0,1},{1,0},{2,3},{3,2},{4,5},{5,4},{6,7},{7,6},{8,9},{9,8},{10,11... | collective-permute-start | bytes 3145736 | tf_op jit(solution)/shard_map/ppermute | solution.py:102
  64.8 2.0 copy-start.1
  82.6 6.1 %collective-permute-start.1 = (f32[2048,256]{1,0:T(8,128)S(1)}, f32[2048,256]{1,0:T(8,128)S(1)}, u32[]{:S(2)}, u32[]{:S(2)}) collective-permute-start(f32[2048,256]{1,0:T(8,128)S(1)} %pad_maximum_fusion.1), channel_id=1, source_target_pairs={{0,1},{1,0},{2,3},{3,2},{4,5},{5,4},{6,7},{7,6},{8,9},{9,8},{10,11... | collective-permute-start | bytes 6291464 | tf_op jit(solution)/shard_map/ppermute | solution.py:155
  188.0 43.3 %copy-start.2 = (f32[8,32,32]{2,1,0:T(8,128)}, f32[8,32,32]{2,1,0:T(8,128)S(1)}, u32[]{:S(2)}) copy-start(f32[8,32,32]{2,1,0:T(8,128)S(1)} %slice_add_fusion.pieces_ref) | copy-start | bytes 98308
  218.1 11.3 %all-to-all-start.5 = ((f32[8,8,8]{2,1,0:T(8,128)}), f32[8,8,8]{2,1,0:T(8,128)S(1)}, u32[]{:S(2)}, u32[]{:S(2)}) async-start(f32[8,8,8]{2,1,0:T(8,128)} %broadcast_in_dim.40), calls=%async_computation.6 | async-start | bytes 65536 | tf_op jit(solution)/shard_map/all_to_all | solution.py:112
Sparse Core Ops, SparseCore 0:
  90.4 76.3 reduce-scatter.1
